TPU v7x, 128 devices: a whole 4x4x4 slice. The times are simulated.
128 devices in a mesh: prow: 16 (over y, x), pcol: 8 (over z, core).
Axes of the slice: x: 4, y: 4, z: 4, core: 2. Of those that a mesh axis runs over, the one named last changes fastest.
Arguments:
- right_sides: float32 [24, 3, 4, 128, 1024], P(None, None, None, 'prow', 'pcol'), may hold values from -6 to 6
- modulus: float32 [4, 128, 1024], P(None, 'prow', 'pcol'), may hold values from 0.2 to 5
- margin_sides: int32 [16, 8, 4], P('prow', 'pcol'), may hold values 0 or 1
- coarse_vectors: float32 [64, 3, 4, 128, 1024], P(None, None, None, 'prow', 'pcol'), may hold values from -0.013671875 to 0.013671875
- coarse_inverse: float32 [8, 64, 64], P('pcol'), may hold values from -4.256688 to 39.729089
Outputs:
- preconditioned: float32 [24, 3, 4, 128, 1024], P(None, None, None, 'prow', 'pcol')
All inputs are finite; a program needn't handle non-finite values. No bound on the sum of `margin_sides` on one device may be relied on, other than what follows from the above.
Results may differ from a plain program's by a relative error of at most 0.00005.
Values sent between devices are 32-bit elements; how exact they have to be, the bound alone decides.
No kernel may reach another device: no remote copies, remote signals or barrier semaphores. Data moves between devices by JAX's collectives and lax.ppermute only.
A program may use at most 128 MiB of HBM per device.

v0:
```python
import jax
import jax.numpy as jnp
from jax import lax
from jax.sharding import PartitionSpec as P

RELAX_WEIGHT = 0.7
MASS_SHIFT = 0.5
DIAGONAL_SLOPE = 0.6 + 0.4 / 3.0
BOND_TOTAL = 44.0 / 3.0


def extended(x, sides, width):
    for axis, dim in sides:
        size, length = (lax.axis_size(axis), x.shape[dim])
        up = [(i, (i + 1) % size) for i in range(size - 1)]
        down = [(j, i) for i, j in up]
        last = lax.slice_in_dim(x, length - width, length, axis=dim)
        first = lax.slice_in_dim(x, 0, width, axis=dim)
        before = lax.ppermute(last, axis, up)
        after = lax.ppermute(first, axis, down)
        x = jnp.concatenate([before, x, after], axis=dim)
    return x


def bond_sum(field_padded, modulus_padded, factor_rows, factor_columns):
    plane_count = modulus_padded.shape[0] - 2
    row_count = modulus_padded.shape[1] - 2
    column_count = modulus_padded.shape[2] - 2
    own_field = field_padded[..., 1:-1, 1:-1, 1:-1]
    own_modulus = modulus_padded[1:-1, 1:-1, 1:-1]
    accumulated = MASS_SHIFT * own_field
    for step_p in (-1, 0, 1):
        for step_x in (-1, 0, 1):
            for step_y in (-1, 0, 1):
                if step_p == 0 and step_x == 0 and (step_y == 0):
                    continue
                length = step_p * step_p + step_x * step_x + step_y * step_y
                weight = 1.0 / (length * BOND_TOTAL)
                near_field = field_padded[
                    ...,
                    1 + step_p : 1 + step_p + plane_count,
                    1 + step_x : 1 + step_x + row_count,
                    1 + step_y : 1 + step_y + column_count,
                ]
                near_modulus = modulus_padded[
                    1 + step_p : 1 + step_p + plane_count,
                    1 + step_x : 1 + step_x + row_count,
                    1 + step_y : 1 + step_y + column_count,
                ]
                factor = factor_rows[step_x + 1] * factor_columns[step_y + 1]
                difference = own_field - factor * near_field
                bond_weight = 0.5 * weight * (own_modulus + near_modulus)
                direction = (step_p, step_x, step_y)
                projected = 0.0
                for component in range(3):
                    if direction[component] != 0:
                        projected = (
                            projected + direction[component] * difference[..., component, :, :, :]
                        )
                pieces = []
                for component in range(3):
                    piece = 0.6 * difference[..., component, :, :, :]
                    if direction[component] != 0:
                        piece = piece + 0.4 * direction[component] / length * projected
                    pieces.append(piece)
                accumulated = accumulated + bond_weight * jnp.stack(pieces, axis=-4)
    return accumulated


def per_device(right_sides, modulus, margin_sides, coarse_vectors, coarse_inverse):
    load_count = right_sides.shape[0]
    plane_count = right_sides.shape[2]
    row_count = right_sides.shape[3]
    column_count = right_sides.shape[4]
    stacked = jnp.concatenate(
        [right_sides.reshape(load_count * 3, plane_count, row_count, column_count), modulus[None]],
        axis=0,
    )
    padded_all = extended(stacked, (("prow", 2), ("pcol", 3)), 1)
    load_halo = padded_all[: load_count * 3].reshape(
        load_count, 3, plane_count, row_count + 2, column_count + 2
    )
    modulus_halo = padded_all[load_count * 3]
    first_halo = RELAX_WEIGHT * load_halo / (MASS_SHIFT + DIAGONAL_SLOPE * modulus_halo)
    first_padded = jnp.pad(first_halo, ((0, 0), (0, 0), (1, 1), (0, 0), (0, 0)))
    modulus_padded = jnp.pad(modulus_halo, ((1, 1), (0, 0), (0, 0)))
    side_values = margin_sides[0, 0].astype(jnp.float32)
    row_index = lax.broadcasted_iota(jnp.int32, (row_count, column_count), 0)
    column_index = lax.broadcasted_iota(jnp.int32, (row_count, column_count), 1)
    unity = jnp.ones((row_count, column_count), jnp.float32)
    factor_rows = jnp.stack(
        [
            jnp.where(row_index == 0, side_values[0], unity),
            unity,
            jnp.where(row_index == row_count - 1, side_values[1], unity),
        ]
    )
    factor_columns = jnp.stack(
        [
            jnp.where(column_index == 0, side_values[2], unity),
            unity,
            jnp.where(column_index == column_count - 1, side_values[3], unity),
        ]
    )
    diagonal = MASS_SHIFT + DIAGONAL_SLOPE * modulus
    first = first_halo[..., 1:-1, 1:-1]
    applied = bond_sum(first_padded, modulus_padded, factor_rows, factor_columns)
    smoothed = first + RELAX_WEIGHT * (right_sides - applied) / diagonal
    flat_vectors = coarse_vectors.reshape(coarse_vectors.shape[0], -1)
    flat_loads = right_sides.reshape(load_count, -1)
    partial_terms = lax.dot_general(
        flat_vectors, flat_loads, (((1,), (1,)), ((), ())), precision=lax.Precision.HIGHEST
    )
    restricted = lax.psum(partial_terms, "prow")
    solved = jnp.dot(coarse_inverse[0], restricted, precision=lax.Precision.HIGHEST)
    lifted = lax.dot_general(
        solved, flat_vectors, (((0,), (0,)), ((), ())), precision=lax.Precision.HIGHEST
    )
    return smoothed + lifted.reshape(right_sides.shape)


def solution(mesh):
    in_specs = (
        P(None, None, None, "prow", "pcol"),
        P(None, "prow", "pcol"),
        P("prow", "pcol", None),
        P(None, None, None, "prow", "pcol"),
        P("pcol", None, None),
    )
    out_specs = P(None, None, None, "prow", "pcol")
    return jax.shard_map(
        per_device, mesh=mesh, in_specs=in_specs, out_specs=out_specs, check_vma=False
    )
```

profile of v0, /device:TPU:1, one launch (start us, length us, event | category | flops | bytes accessed | tf_op | source)
XLA Modules:
  0.0 200.0 jit_solution(17554911430547905804)
XLA Ops:
  0.0 2.0 %pad_maximum_fusion.3 = (f32[73,4,1,128]{3,2,1,0:T(1,128)S(1)}, f32[73,4,1,128]{3,2,1,0:T(1,128)S(1)}) fusion(f32[1,4,8,128]{3,2,1,0:T(8,128)} %bitcast.43, f32[72,4,8,128]{3,2,1,0:T(8,128)} %bitcast.36), kind=kLoop, calls=%fused_computation.248 | loop fusion | flops 74752 | bytes 1495040 | tf_op jit(solution)/shard_map/slice | solution.py:17
  2.1 1.3 collective-permute-start.1
  3.4 4.6 %collective-permute-start = (f32[73,4,1,128]{3,2,1,0:T(1,128)S(1)}, f32[73,4,1,128]{3,2,1,0:T(1,128)S(1)}, u32[]{:S(2)}, u32[]{:S(2)}) collective-permute-start(f32[73,4,1,128]{3,2,1,0:T(1,128)S(1)} %get-tuple-element.79), channel_id=1, source_target_pairs={{0,8},{8,16},{16,24},{24,32},{32,40},{40,48},{48,56},{56,64},{64,7... | collective-permute-start | bytes 448520 | tf_op jit(solution)/shard_map/ppermute | solution.py:19
  8.6 6.5 %fusion.80 = f32[64,24]{0,1:T(8,128)S(1)} fusion(f32[24,3,4,8,128]{4,3,2,1,0:T(8,128)S(1)} %copy-done.2, f32[64,3,4,8,128]{4,3,2,1,0:T(8,128)} %param.8), kind=kOutput, calls=%fused_computation.135 | convolution fusion | flops 226492416 | bytes 4331520 | tf_op jit(solution)/shard_map/dot_general | solution.py:111
  15.1 59.3 %psum.7 = f32[64,24]{0,1:T(8,128)S(1)} all-reduce(f32[64,24]{0,1:T(8,128)S(1)} %fusion.80), channel_id=1, replica_groups=mesh['prow'=16,'pcol'=8] {'prow'}, use_global_device_ids=true, to_apply=%region_0.1 | all-reduce | flops 1536 | bytes 12288 | tf_op jit(solution)/shard_map/psum | solution.py:114
  75.0 1.3 compare_select_fusion
  76.3 1.3 compare_select_fusion.1
  77.6 0.7 broadcast_multiply_fusion.3
  78.8 3.1 %fusion.130 = (f32[73,4,10,1]{3,2,1,0:T(8,128)}, f32[73,4,10,1]{3,2,1,0:T(8,128)}) fusion(f32[73,4,10,128]{3,2,1,0:T(8,128)S(1)} %pad_maximum_fusion.1), kind=kLoop, calls=%fused_computation.314 | loop fusion | bytes 46720 | tf_op jit(solution)/shard_map/slice | solution.py:17
  81.9 2.5 %copy.78 = f32[73,4,10,1]{0,1,3,2:T(4,128)S(1)} copy(f32[73,4,10,1]{3,2,1,0:T(8,128)} %get-tuple-element.62) | data formatting | bytes 23360 | tf_op jit(solution)/shard_map/slice | solution.py:18
  84.4 16.9 %collective-permute-start.3 = (f32[73,4,10,1]{0,1,3,2:T(4,128)S(1)}, f32[73,4,10,1]{0,1,3,2:T(4,128)S(1)}, u32[]{:S(2)}, u32[]{:S(2)}) collective-permute-start(f32[73,4,10,1]{0,1,3,2:T(4,128)S(1)} %copy.78), channel_id=1, source_target_pairs={{1,0},{2,1},{3,2},{4,3},{5,4},{6,5},{7,6},{9,8},{10,9},{11,10},{12... | collective-permute-start | bytes 35048 | tf_op jit(solution)/shard_map/ppermute | solution.py:20
  101.3 2.5 %copy.77 = f32[73,4,10,1]{0,1,3,2:T(4,128)S(1)} copy(f32[73,4,10,1]{3,2,1,0:T(8,128)} %get-tuple-element.61) | data formatting | bytes 23360 | tf_op jit(solution)/shard_map/slice | solution.py:17
  103.9 3.6 %collective-permute-start.2 = (f32[73,4,10,1]{0,1,3,2:T(4,128)S(1)}, f32[73,4,10,1]{0,1,3,2:T(4,128)S(1)}, u32[]{:S(2)}, u32[]{:S(2)}) collective-permute-start(f32[73,4,10,1]{0,1,3,2:T(4,128)S(1)} %copy.77), channel_id=1, source_target_pairs={{0,1},{1,2},{2,3},{3,4},{4,5},{5,6},{6,7},{8,9},{9,10},{10,11},{11... | collective-permute-start | bytes 35048 | tf_op jit(solution)/shard_map/ppermute | solution.py:19
  107.5 0.8 convolution_bitcast_fusion
  108.3 3.7 %copy.139 = f32[8,8,96,128]{3,1,2,0:T(8,128)S(1)} copy(f32[8,8,96,128]{3,2,1,0:T(8,128)} %bitcast.41) | data formatting | bytes 6291456
  111.9 2.2 %copy.121 = f32[8,8,96,128]{3,2,1,0:T(8,128)} copy(f32[8,8,96,128]{3,1,2,0:T(8,128)S(1)} %copy.139) | data formatting | bytes 6291456
  114.1 3.3 %copy.80 = f32[73,4,10,1]{3,2,1,0:T(8,128)} copy(f32[73,4,10,1]{0,1,3,2:T(4,128)S(1)} %collective-permute-done.3) | data formatting | bytes 23360 | tf_op jit(solution)/shard_map/ppermute | solution.py:20
  117.4 3.3 %copy.79 = f32[73,4,10,1]{3,2,1,0:T(8,128)} copy(f32[73,4,10,1]{0,1,3,2:T(4,128)S(1)} %collective-permute-done.2) | data formatting | bytes 23360 | tf_op jit(solution)/shard_map/ppermute | solution.py:19
  120.7 1.0 pad_maximum_fusion.4
  121.8 0.8 fusion.89
  122.7 0.7 fusion.91
  123.4 4.8 %pad_maximum_fusion = f32[73,4,10,130]{3,2,1,0:T(8,128)S(1)} fusion(f32[73,4,10,1]{3,2,1,0:T(8,128)S(1)} %copy-done.3, f32[73,4,1,128]{3,2,1,0:T(1,128)S(1)} %collective-permute-done.1, f32[1,4,8,128]{3,2,1,0:T(8,128)S(1)} %bitcast.46, f32[72,4,8,128]{3,2,1,0:T(8,128)S(1)} %bitcast.39, f32[73,4,1,128]{3,2,1,0:T(1,128)S(1)} %collective-permute-done, ...), kind=kLoop, calls=%fused_computation.18 | loop fusion | flops 1898000 | bytes 3036800 | tf_op jit(solution)/shard_map/concatenate | solution.py:21
  128.2 1.1 slice_multiply_fusion
  129.3 2.5 %copy_divide_fusion = f32[24,3,4,10,130]{4,0,3,2,1:T(8,128)S(1)} fusion(f32[24,3,4,10,130]{4,3,2,1,0:T(8,128)S(1)} %bitcast.40, f32[4,10,130]{2,1,0:T(8,128)S(1)} %copy.83), kind=kLoop, calls=%fused_computation.25 | loop fusion | flops 374400 | bytes 3016000 | tf_op jit(solution)/shard_map/div | solution.py:84
  131.8 2.6 %fusion.21 = (f32[24,3,4,8,128]{4,0,3,2,1:T(8,128)S(1)}, f32[24,3,4,8,128]{4,0,3,2,1:T(8,128)S(1)}, f32[24,3,4,8,128]{4,0,3,2,1:T(8,128)S(1)}, f32[24,3,4,8,128]...) fusion(f32[24,3,4,10,130]{4,0,3,2,1:T(8,128)S(1)} %copy_divide_fusion, ...), kind=kLoop, calls=%fused_computation.42 | loop fusion | flops 3538944 | bytes 13570080 | tf_op jit(solution)/shard_map/sub | solution.py:51
  134.4 1.1 multiply_add_fusion.4
  135.5 0.8 multiply_add_fusion.2
  136.3 1.0 multiply_add_fusion.1
  137.3 2.5 %fusion.17 = (f32[24,3,4,8,128]{4,0,3,2,1:T(8,128)S(1)}, f32[24,3,4,8,128]{4,0,3,2,1:T(8,128)S(1)}, f32[24,3,4,8,128]{4,0,3,2,1:T(8,128)}, f32[24,3,4,8,128]{4,0...) fusion(f32[24,3,4,10,130]{4,0,3,2,1:T(8,128)S(1)} %copy_divide_fusion, ...), kind=kLoop, calls=%fused_computation.38 | loop fusion | flops 3538944 | bytes 13570560 | tf_op jit(solution)/shard_map/sub | solution.py:51
  139.9 0.9 multiply_add_fusion.8
  140.7 1.0 multiply_add_fusion.6
  141.8 1.1 multiply_add_fusion.10
  142.8 3.5 %fusion.8 = (f32[24,3,4,8,128]{4,0,3,2,1:T(8,128)S(1)}, f32[24,3,4,8,128]{4,0,3,2,1:T(8,128)S(1)}, f32[24,3,4,8,128]{4,0,3,2,1:T(8,128)}, f32[24,3,4,8,128]{4,0,...) fusion(f32[24,3,4,10,130]{4,0,3,2,1:T(8,128)S(1)} %copy_divide_, ...), kind=kLoop, calls=%fused_computation.29 | loop fusion | flops 4128768 | bytes 15929856 | tf_op jit(solution)/shard_map/sub | solution.py:51
  146.3 1.1 fusion.132
  147.4 2.9 %fusion.12 = (f32[24,3,4,8,128]{4,0,3,2,1:T(8,128)S(1)}, f32[24,3,4,8,128]{4,0,3,2,1:T(8,128)S(1)}, f32[24,3,4,8,128]{4,0,3,2,1:T(8,128)}, f32[24,3,4,8,128]{4,0...) fusion(f32[24,3,4,10,130]{4,0,3,2,1:T(8,128)S(1)} %copy_divide_fusion, ...), kind=kLoop, calls=%fused_computation.33 | loop fusion | flops 3538944 | bytes 13570560 | tf_op jit(solution)/shard_map/sub | solution.py:51
  150.3 2.3 %multiply_add_fusion.12 = (f32[24,1,4,8,128]{4,0,3,2,1:T(8,128)}, f32[24,1,4,8,128]{4,0,3,2,1:T(8,128)}, f32[24,1,4,8,128]{4,0,3,2,1:T(8,128)}) fusion(f32[24,3,4,8,128]{4,0,3,2,1:T(8,128)} %get-tuple-element.53), kind=kLoop, calls=%fused_computation.176 | loop fusion | flops 884736 | bytes 2359296 | tf_op jit(solution)/shard_map/add | solution.py:64
  152.6 0.8 multiply_add_fusion.16
  153.4 1.0 multiply_add_fusion.15
  155.0 1.1 multiply_add_fusion.18
  156.1 0.8 multiply_add_fusion.22
  156.9 1.0 multiply_add_fusion.21
  157.9 1.1 slice_multiply_fusion.15
  159.0 1.0 slice_multiply_fusion.17
  160.7 1.1 slice_multiply_fusion.18
  162.4 1.0 slice_multiply_fusion.20
  164.1 1.1 slice_multiply_fusion.22
  165.8 1.1 slice_multiply_fusion.23
  167.5 1.1 slice_multiply_fusion.25
  169.2 1.1 slice_multiply_fusion.26
  170.3 0.9 multiply_add_fusion.36
  171.2 1.1 multiply_add_fusion.35
  172.3 1.1 multiply_add_fusion.38
  173.4 0.9 multiply_add_fusion.43
  174.2 1.0 multiply_add_fusion.41
  175.2 1.1 multiply_add_fusion.45
  176.9 1.0 fusion.131
  178.0 1.1 multiply_add_fusion.48
  179.0 0.8 multiply_add_fusion.52
  179.9 1.0 multiply_add_fusion.50
  181.4 1.1 multiply_add_fusion.54
  182.5 0.8 multiply_add_fusion.57
  183.4 1.0 multiply_add_fusion.56
  185.5 13.2 %fusion.4 = f32[24,3,4,8,128]{4,0,3,2,1:T(8,128)S(1)} fusion(f32[24,64,1,1,1]{1,0,4,3,2:T(8,128)} %convolution_bitcast_fusion, f32[3,4,8,128,64]{3,2,1,0,4:T(8,128)S(1)} %bitcast.42, f32[24,1,4,8,128]{4,0,3,2,1:T(8,128)S(1)} %copy-done.17, f32[24,1,4,8,128]{4,0,3,2,1:T(8,128)S(1)} %copy-done.18, f32[24,1,4,8,128]{4,0,3,2,1:T(8,128)S(1)} %copy-done.16, ...), kind=kOutput, calls=%fused_computation.27 | convolution fusion | flops 258932736 | bytes 37804032 | tf_op jit(solution)/shard_map/dot_general | solution.py:116
  198.8 1.2 copy.115
  (133 shorter events, 8.1 us)
Async XLA Ops:
  0.0 107.5 %copy-start = (f32[1,64,64]{2,1,0:T(8,128)S(1)}, f32[1,64,64]{2,1,0:T(8,128)}, u32[]{:S(2)}) copy-start(f32[1,64,64]{2,1,0:T(8,128)} %param.9) | copy-start | bytes 49156
  0.0 7.9 %copy-start.15 = (f32[4,8,128]{2,1,0:T(8,128)S(1)}, f32[4,8,128]{2,1,0:T(8,128)}, u32[]{:S(2)}) copy-start(f32[4,8,128]{2,1,0:T(8,128)} %param.6) | copy-start | bytes 49156
  0.0 8.5 %copy-start.2 = (f32[24,3,4,8,128]{4,3,2,1,0:T(8,128)S(1)}, f32[24,3,4,8,128]{4,3,2,1,0:T(8,128)}, u32[]{:S(2)}) copy-start(f32[24,3,4,8,128]{4,3,2,1,0:T(8,128)} %param.5) | copy-start | bytes 3538948
  2.1 76.2 %collective-permute-start.1 = (f32[73,4,1,128]{3,2,1,0:T(1,128)S(1)}, f32[73,4,1,128]{3,2,1,0:T(1,128)S(1)}, u32[]{:S(2)}, u32[]{:S(2)}) collective-permute-start(f32[73,4,1,128]{3,2,1,0:T(1,128)S(1)} %get-tuple-element.80), channel_id=1, source_target_pairs={{8,0},{16,8},{24,16},{32,24},{40,32},{48,40},{56,48},{64,56},{72,6... | collective-permute-start | bytes 448520 | tf_op jit(solution)/shard_map/ppermute | solution.py:20
  3.4 74.9 %collective-permute-start = (f32[73,4,1,128]{3,2,1,0:T(1,128)S(1)}, f32[73,4,1,128]{3,2,1,0:T(1,128)S(1)}, u32[]{:S(2)}, u32[]{:S(2)}) collective-permute-start(f32[73,4,1,128]{3,2,1,0:T(1,128)S(1)} %get-tuple-element.79), channel_id=1, source_target_pairs={{0,8},{8,16},{16,24},{24,32},{32,40},{40,48},{48,56},{56,64},{64,7... | collective-permute-start | bytes 448520 | tf_op jit(solution)/shard_map/ppermute | solution.py:19
  8.5 65.8 %copy-start.47 = (s32[1,1,4]{2,1,0:T(1,128)S(1)}, s32[1,1,4]{2,1,0:T(1,128)}, u32[]{:S(2)}) copy-start(s32[1,1,4]{2,1,0:T(1,128)} %param.7) | copy-start | bytes 52
  76.3 2.5 %copy-start.42 = (f32[8]{0:T(128)}, f32[8]{0:T(128)S(1)}, u32[]{:S(2)}) copy-start(f32[8]{0:T(128)S(1)} %get-tuple-element.170) | copy-start | bytes 100
  76.3 2.5 %copy-start.46 = (f32[8]{0:T(128)}, f32[8]{0:T(128)S(1)}, u32[]{:S(2)}) copy-start(f32[8]{0:T(128)S(1)} %get-tuple-element.169) | copy-start | bytes 100
  77.6 1.2 copy-start.40
  77.6 1.2 copy-start.44
  84.4 29.7 %collective-permute-start.3 = (f32[73,4,10,1]{0,1,3,2:T(4,128)S(1)}, f32[73,4,10,1]{0,1,3,2:T(4,128)S(1)}, u32[]{:S(2)}, u32[]{:S(2)}) collective-permute-start(f32[73,4,10,1]{0,1,3,2:T(4,128)S(1)} %copy.78), channel_id=1, source_target_pairs={{1,0},{2,1},{3,2},{4,3},{5,4},{6,5},{7,6},{9,8},{10,9},{11,10},{12... | collective-permute-start | bytes 35048 | tf_op jit(solution)/shard_map/ppermute | solution.py:20
  103.9 13.6 %collective-permute-start.2 = (f32[73,4,10,1]{0,1,3,2:T(4,128)S(1)}, f32[73,4,10,1]{0,1,3,2:T(4,128)S(1)}, u32[]{:S(2)}, u32[]{:S(2)}) collective-permute-start(f32[73,4,10,1]{0,1,3,2:T(4,128)S(1)} %copy.77), channel_id=1, source_target_pairs={{0,1},{1,2},{2,3},{3,4},{4,5},{5,6},{6,7},{8,9},{9,10},{10,11},{11... | collective-permute-start | bytes 35048 | tf_op jit(solution)/shard_map/ppermute | solution.py:19
  120.7 2.7 %copy-start.3 = (f32[73,4,10,1]{3,2,1,0:T(8,128)S(1)}, f32[73,4,10,1]{3,2,1,0:T(8,128)}, u32[]{:S(2)}) copy-start(f32[73,4,10,1]{3,2,1,0:T(8,128)} %copy.80) | copy-start | bytes 35044
  120.7 2.7 %copy-start.4 = (f32[73,4,10,1]{3,2,1,0:T(8,128)S(1)}, f32[73,4,10,1]{3,2,1,0:T(8,128)}, u32[]{:S(2)}) copy-start(f32[73,4,10,1]{3,2,1,0:T(8,128)} %copy.79) | copy-start | bytes 35044
  136.3 1.0 copy-start.38
  136.3 1.0 copy-start.45
  141.8 1.1 copy-start.39
  141.8 1.1 copy-start.43
  146.3 1.1 copy-start.41
  153.4 1.6 copy-start.13
  159.0 1.7 copy-start.6
  160.7 1.7 copy-start.5
  162.4 1.7 copy-start.8
  164.1 1.7 copy-start.7
  165.8 1.7 copy-start.12
  167.5 1.7 copy-start.11
  175.2 1.7 copy-start.10
  179.0 6.0 %copy-start.28 = (f32[24,1,4,8,128]{4,0,3,2,1:T(8,128)S(1)}, f32[24,1,4,8,128]{4,0,3,2,1:T(8,128)}, u32[]{:S(2)}) copy-start(f32[24,1,4,8,128]{4,0,3,2,1:T(8,128)} %get-tuple-element.120) | copy-start | bytes 1179652
  179.9 1.6 copy-start.9
  179.9 5.2 %copy-start.26 = (f32[24,1,4,8,128]{4,0,3,2,1:T(8,128)S(1)}, f32[24,1,4,8,128]{4,0,3,2,1:T(8,128)}, u32[]{:S(2)}) copy-start(f32[24,1,4,8,128]{4,0,3,2,1:T(8,128)} %get-tuple-element.124) | copy-start | bytes 1179652
  179.9 5.2 %copy-start.27 = (f32[24,1,4,8,128]{4,0,3,2,1:T(8,128)S(1)}, f32[24,1,4,8,128]{4,0,3,2,1:T(8,128)}, u32[]{:S(2)}) copy-start(f32[24,1,4,8,128]{4,0,3,2,1:T(8,128)} %get-tuple-element.125) | copy-start | bytes 1179652
  181.4 3.7 %copy-start.20 = (f32[24,1,4,8,128]{4,0,3,2,1:T(8,128)S(1)}, f32[24,1,4,8,128]{4,0,3,2,1:T(8,128)}, u32[]{:S(2)}) copy-start(f32[24,1,4,8,128]{4,0,3,2,1:T(8,128)} %get-tuple-element.130) | copy-start | bytes 1179652
  181.4 3.7 %copy-start.21 = (f32[24,1,4,8,128]{4,0,3,2,1:T(8,128)S(1)}, f32[24,1,4,8,128]{4,0,3,2,1:T(8,128)}, u32[]{:S(2)}) copy-start(f32[24,1,4,8,128]{4,0,3,2,1:T(8,128)} %get-tuple-element.131) | copy-start | bytes 1179652
  181.4 3.7 %copy-start.22 = (f32[24,1,4,8,128]{4,0,3,2,1:T(8,128)S(1)}, f32[24,1,4,8,128]{4,0,3,2,1:T(8,128)}, u32[]{:S(2)}) copy-start(f32[24,1,4,8,128]{4,0,3,2,1:T(8,128)} %get-tuple-element.126) | copy-start | bytes 1179652
  181.4 3.7 %copy-start.23 = (f32[24,1,4,8,128]{4,0,3,2,1:T(8,128)S(1)}, f32[24,1,4,8,128]{4,0,3,2,1:T(8,128)}, u32[]{:S(2)}) copy-start(f32[24,1,4,8,128]{4,0,3,2,1:T(8,128)} %get-tuple-element.127) | copy-start | bytes 1179652
  181.4 3.7 %copy-start.24 = (f32[24,1,4,8,128]{4,0,3,2,1:T(8,128)S(1)}, f32[24,1,4,8,128]{4,0,3,2,1:T(8,128)}, u32[]{:S(2)}) copy-start(f32[24,1,4,8,128]{4,0,3,2,1:T(8,128)} %get-tuple-element.128) | copy-start | bytes 1179652
  181.4 3.7 %copy-start.25 = (f32[24,1,4,8,128]{4,0,3,2,1:T(8,128)S(1)}, f32[24,1,4,8,128]{4,0,3,2,1:T(8,128)}, u32[]{:S(2)}) copy-start(f32[24,1,4,8,128]{4,0,3,2,1:T(8,128)} %get-tuple-element.123) | copy-start | bytes 1179652
  182.5 2.3 %copy-start.33 = (f32[4,8,128]{2,0,1:T(4,128)S(1)}, f32[4,8,128]{2,0,1:T(4,128)}, u32[]{:S(2)}) copy-start(f32[4,8,128]{2,0,1:T(4,128)} %get-tuple-element.156) | copy-start | bytes 49156
  182.5 2.3 %copy-start.31 = (f32[4,8,128]{2,0,1:T(4,128)S(1)}, f32[4,8,128]{2,0,1:T(4,128)}, u32[]{:S(2)}) copy-start(f32[4,8,128]{2,0,1:T(4,128)} %get-tuple-element.157) | copy-start | bytes 49156
  182.5 2.4 %copy-start.29 = (f32[4,8,128]{2,0,1:T(4,128)S(1)}, f32[4,8,128]{2,0,1:T(4,128)}, u32[]{:S(2)}) copy-start(f32[4,8,128]{2,0,1:T(4,128)} %get-tuple-element.158) | copy-start | bytes 49156
  182.5 2.6 %copy-start.14 = (f32[8,8,96,128]{3,2,1,0:T(8,128)S(1)}, f32[8,8,96,128]{3,2,1,0:T(8,128)}, u32[]{:S(2)}) copy-start(f32[8,8,96,128]{3,2,1,0:T(8,128)} %copy.121) | copy-start | bytes 9437188
  183.4 1.3 copy-start.36
  183.4 1.3 copy-start.34
  183.4 1.3 copy-start.32
  183.4 1.3 copy-start.30
  183.4 1.4 copy-start.37
  183.4 1.4 copy-start.35
  183.4 1.8 copy-start.16
  183.4 1.9 copy-start.17
  183.4 2.0 copy-start.18
  183.4 2.1 %copy-start.19 = (f32[24,1,4,8,128]{4,0,3,2,1:T(8,128)S(1)}, f32[24,1,4,8,128]{4,0,3,2,1:T(8,128)}, u32[]{:S(2)}) copy-start(f32[24,1,4,8,128]{4,0,3,2,1:T(8,128)} %get-tuple-element.129) | copy-start | bytes 1179652
  185.5 14.5 %copy-start.1 = (f32[1,64,64]{2,1,0:T(8,128)S(1)}, f32[1,64,64]{2,1,0:T(8,128)}, u32[]{:S(2)}) copy-start(f32[1,64,64]{2,1,0:T(8,128)} %param.9) | copy-start | bytes 49156
where the time goes:
time: 201 us; the launch traced here: 200 us
  other arithmetic  64.5 us (32%)
  blocking collectives  59.3 us (30%)
  local copies, waits for them, and re-layouts  28.7 us (14%)
  starting transfers between devices  26.4 us (13%)
  matrix products  20.5 us (10%)
    psum x1, blocking collectives, per_device(): restricted = lax.psum(partial_terms, 'prow')  59.3 us
    add x24, other arithmetic, bond_sum(): piece = piece + 0.4 * direction[component] / length * projected  24.7 us
    ppermute x2, starting transfers between devices, extended(): after = lax.ppermute(first, axis, down)  18.2 us
    dot_general x1, matrix products, per_device(): lax.dot_general(solved, flat_vectors, (((0,), (0,)), ((), ())), precision...  13.2 us
    unnamed x98, local copies, waits for them, and re-layouts  12 us
    sub x4, other arithmetic, bond_sum(): difference = own_field - factor * near_field  11.5 us
    mul x8, other arithmetic, bond_sum(): piece = 0.6 * difference[..., component, :, :, :]  8.8 us
    ppermute x2, starting transfers between devices, extended(): before = lax.ppermute(last, axis, up)  8.19 us
  transfers between devices with their start and end apart: 4, of which 0 were waited for; matrix products, arithmetic and copies ran while one was open for 12% of the time, Pallas kernels for 0%

commit v1 on v0

--- a/solution.py
+++ b/solution.py
@@ -19,6 +19,16 @@
         before = lax.ppermute(last, axis, up)
         after = lax.ppermute(first, axis, down)
         x = jnp.concatenate([before, x, after], axis=dim)
+    return x
+
+
+def butterfly_sum(x, axis):
+    size = lax.axis_size(axis)
+    step = 1
+    while step < size:
+        pairs = [(i, i ^ step) for i in range(size)]
+        x = x + lax.ppermute(x, axis, pairs)
+        step *= 2
     return x
 
 
@@ -111,7 +121,7 @@
     partial_terms = lax.dot_general(
         flat_vectors, flat_loads, (((1,), (1,)), ((), ())), precision=lax.Precision.HIGHEST
     )
-    restricted = lax.psum(partial_terms, "prow")
+    restricted = butterfly_sum(partial_terms, "prow")
     solved = jnp.dot(coarse_inverse[0], restricted, precision=lax.Precision.HIGHEST)
     lifted = lax.dot_general(
         solved, flat_vectors, (((0,), (0,)), ((), ())), precision=lax.Precision.HIGHEST

time: 201 us -> 132 us (0.66)
  blocking collectives: 59.3 us -> 0 us
  other arithmetic: 64.5 us -> 57.8 us
  starting transfers between devices: 26.4 us -> 22.7 us
    psum x1 -> x0, blocking collectives: 59.3 us -> none  [per_device(): restricted = lax.psum(partial_terms, 'prow')]
    ppermute x2, starting transfers between devices: 18.2 us -> 5.71 us  [extended(): after = lax.ppermute(first, axis, down)]
    ppermute x0 -> x4, starting transfers between devices: none -> 9.38 us  [butterfly_sum(): x = x + lax.ppermute(x, axis, pairs)]
    unnamed x98 -> x58, local copies, waits for them, and re-layouts: 12 us -> 12.7 us
  transfers between devices with their start and end apart: 4 -> 8, of which waited for: 0 -> 1; matrix products, arithmetic and copies ran while one was open for 12% -> 15% of each run, Pallas kernels for 0% -> 0%
where the time goes in v1:
time: 132 us; the launch traced here: 131 us
  other arithmetic  57.8 us (44%)
  local copies, waits for them, and re-layouts  29.5 us (22%)
  starting transfers between devices  22.7 us (17%)
  matrix products  19.8 us (15%)
    add x24, other arithmetic, bond_sum(): piece = piece + 0.4 * direction[component] / length * projected  22.8 us
    unnamed x58, local copies, waits for them, and re-layouts  12.7 us
    dot_general x1, matrix products, per_device(): lax.dot_general(solved, flat_vectors, (((0,), (0,)), ((), ())), precision...  12.6 us
    sub x4, other arithmetic, bond_sum(): difference = own_field - factor * near_field  11.9 us
    ppermute x4, starting transfers between devices, butterfly_sum(): x = x + lax.ppermute(x, axis, pairs)  9.38 us
    mul x8, other arithmetic, bond_sum(): piece = 0.6 * difference[..., component, :, :, :]  8.75 us
    ppermute x2, starting transfers between devices, extended(): before = lax.ppermute(last, axis, up)  7.61 us
    dot_general x1, matrix products, per_device(): lax.dot_general(flat_vectors, flat_loads, (((1,), (1,)), ((), ())), preci...  7 us
  transfers between devices with their start and end apart: 8, of which 1 were waited for; matrix products, arithmetic and copies ran while one was open for 15% of the time, Pallas kernels for 0%

profile of v1, /device:TPU:1, one launch (start us, length us, event | category | flops | bytes accessed | tf_op | source)
XLA Modules:
  0.0 130.9 jit_solution(16682343423711854493)
XLA Ops:
  0.0 7.0 %fusion.80 = f32[64,24]{0,1:T(8,128)S(1)} fusion(f32[24,3,4,8,128]{4,3,2,1,0:T(8,128)} %param.5, f32[64,3,4,8,128]{4,3,2,1,0:T(8,128)} %param.8), kind=kOutput, calls=%fused_computation.135 | convolution fusion | flops 226492416 | bytes 4331520 | tf_op jit(solution)/shard_map/dot_general | solution.py:121
  7.0 2.1 %collective-permute-start.4 = (f32[64,24]{0,1:T(8,128)S(1)}, f32[64,24]{0,1:T(8,128)S(1)}, u32[]{:S(2)}, u32[]{:S(2)}) collective-permute-start(f32[64,24]{0,1:T(8,128)S(1)} %fusion.80), channel_id=1, source_target_pairs={{0,8},{8,0},{16,24},{24,16},{32,40},{40,32},{48,56},{56,48},{64,72... | collective-permute-start | bytes 18440 | tf_op jit(solution)/shard_map/ppermute | solution.py:30
  9.3 1.3 collective-permute-start.1
  10.6 4.0 %collective-permute-start = (f32[73,4,1,128]{3,2,1,0:T(1,128)S(1)}, f32[73,4,1,128]{3,2,1,0:T(1,128)S(1)}, u32[]{:S(2)}, u32[]{:S(2)}) collective-permute-start(f32[73,4,1,128]{3,2,1,0:T(1,128)S(1)} %get-tuple-element.79), channel_id=1, source_target_pairs={{0,8},{8,16},{16,24},{24,32},{32,40},{40,48},{48,56},{56,64},{64,7... | collective-permute-start | bytes 448520 | tf_op jit(solution)/shard_map/ppermute | solution.py:19
  14.7 0.7 fusion.134
  15.3 1.3 compare_select_fusion
  16.7 2.5 %collective-permute-start.5 = (f32[64,24]{0,1:T(8,128)S(1)}, f32[64,24]{0,1:T(8,128)S(1)}, u32[]{:S(2)}, u32[]{:S(2)}) collective-permute-start(f32[64,24]{0,1:T(8,128)S(1)} %add.699), channel_id=1, source_target_pairs={{0,16},{8,24},{16,0},{24,8},{32,48},{40,56},{48,32},{56,40},{64,80... | collective-permute-start | bytes 18440 | tf_op jit(solution)/shard_map/ppermute | solution.py:30
  19.2 1.2 compare_select_fusion.1
  20.9 1.8 %collective-permute-start.6 = (f32[64,24]{0,1:T(8,128)S(1)}, f32[64,24]{0,1:T(8,128)S(1)}, u32[]{:S(2)}, u32[]{:S(2)}) collective-permute-start(f32[64,24]{0,1:T(8,128)S(1)} %add.700), channel_id=1, source_target_pairs={{0,32},{8,40},{16,48},{24,56},{32,0},{40,8},{48,16},{56,24},{64,96... | collective-permute-start | bytes 18440 | tf_op jit(solution)/shard_map/ppermute | solution.py:30
  22.8 1.8 %copy.143 = f32[8,8,96,128]{3,1,2,0:T(8,128)S(1)} copy(f32[8,8,96,128]{3,2,1,0:T(8,128)S(1)} %bitcast.40) | data formatting | bytes 6291456
  24.6 2.2 %copy.125 = f32[8,8,96,128]{3,2,1,0:T(8,128)} copy(f32[8,8,96,128]{3,1,2,0:T(8,128)S(1)} %copy.143) | data formatting | bytes 6291456
  26.8 2.9 %collective-permute-start.7 = (f32[64,24]{0,1:T(8,128)S(1)}, f32[64,24]{0,1:T(8,128)S(1)}, u32[]{:S(2)}, u32[]{:S(2)}) collective-permute-start(f32[64,24]{0,1:T(8,128)S(1)} %add.701), channel_id=1, source_target_pairs={{0,64},{8,72},{16,80},{24,88},{32,96},{40,104},{48,112},{56,120},{... | collective-permute-start | bytes 18440 | tf_op jit(solution)/shard_map/ppermute | solution.py:30
  30.2 3.0 %fusion.131 = (f32[73,4,10,1]{3,2,1,0:T(8,128)}, f32[73,4,10,1]{3,2,1,0:T(8,128)}) fusion(f32[73,4,10,128]{3,2,1,0:T(8,128)S(1)} %pad_maximum_fusion.1), kind=kLoop, calls=%fused_computation.315 | loop fusion | bytes 46720 | tf_op jit(solution)/shard_map/slice | solution.py:17
  33.3 2.5 %copy.82 = f32[73,4,10,1]{0,1,3,2:T(4,128)S(1)} copy(f32[73,4,10,1]{3,2,1,0:T(8,128)} %get-tuple-element.62) | data formatting | bytes 23360 | tf_op jit(solution)/shard_map/slice | solution.py:18
  35.8 4.4 %collective-permute-start.3 = (f32[73,4,10,1]{0,1,3,2:T(4,128)S(1)}, f32[73,4,10,1]{0,1,3,2:T(4,128)S(1)}, u32[]{:S(2)}, u32[]{:S(2)}) collective-permute-start(f32[73,4,10,1]{0,1,3,2:T(4,128)S(1)} %copy.82), channel_id=1, source_target_pairs={{1,0},{2,1},{3,2},{4,3},{5,4},{6,5},{7,6},{9,8},{10,9},{11,10},{12... | collective-permute-start | bytes 35048 | tf_op jit(solution)/shard_map/ppermute | solution.py:20
  40.2 2.5 %copy.81 = f32[73,4,10,1]{0,1,3,2:T(4,128)S(1)} copy(f32[73,4,10,1]{3,2,1,0:T(8,128)} %get-tuple-element.61) | data formatting | bytes 23360 | tf_op jit(solution)/shard_map/slice | solution.py:17
  42.8 3.6 %collective-permute-start.2 = (f32[73,4,10,1]{0,1,3,2:T(4,128)S(1)}, f32[73,4,10,1]{0,1,3,2:T(4,128)S(1)}, u32[]{:S(2)}, u32[]{:S(2)}) collective-permute-start(f32[73,4,10,1]{0,1,3,2:T(4,128)S(1)} %copy.81), channel_id=1, source_target_pairs={{0,1},{1,2},{2,3},{3,4},{4,5},{5,6},{6,7},{8,9},{9,10},{10,11},{11... | collective-permute-start | bytes 35048 | tf_op jit(solution)/shard_map/ppermute | solution.py:19
  46.6 3.3 %copy.84 = f32[73,4,10,1]{3,2,1,0:T(8,128)} copy(f32[73,4,10,1]{0,1,3,2:T(4,128)S(1)} %collective-permute-done.3) | data formatting | bytes 23360 | tf_op jit(solution)/shard_map/ppermute | solution.py:20
  49.9 3.3 %copy.83 = f32[73,4,10,1]{3,2,1,0:T(8,128)} copy(f32[73,4,10,1]{0,1,3,2:T(4,128)S(1)} %collective-permute-done.2) | data formatting | bytes 23360 | tf_op jit(solution)/shard_map/ppermute | solution.py:19
  53.2 1.0 pad_maximum_fusion.4
  54.9 0.7 copy-done.4
  55.7 4.5 %pad_maximum_fusion = f32[73,4,10,130]{3,2,1,0:T(8,128)S(1)} fusion(f32[73,4,10,1]{3,2,1,0:T(8,128)S(1)} %copy-done.3, f32[73,4,1,128]{3,2,1,0:T(1,128)S(1)} %collective-permute-done.1, f32[1,4,8,128]{3,2,1,0:T(8,128)S(1)} %bitcast.45, f32[72,4,8,128]{3,2,1,0:T(8,128)S(1)} %bitcast.38, f32[73,4,1,128]{3,2,1,0:T(1,128)S(1)} %collective-permute-done, ...), kind=kLoop, calls=%fused_computation.18 | loop fusion | flops 1898000 | bytes 3036800 | tf_op jit(solution)/shard_map/concatenate | solution.py:21
  60.8 2.5 %copy_divide_fusion = f32[24,3,4,10,130]{4,0,3,2,1:T(8,128)S(1)} fusion(f32[24,3,4,10,130]{4,3,2,1,0:T(8,128)S(1)} %bitcast.39, f32[4,10,130]{2,1,0:T(8,128)S(1)} %copy.87), kind=kLoop, calls=%fused_computation.25 | loop fusion | flops 374400 | bytes 3016000 | tf_op jit(solution)/shard_map/div | solution.py:94
  63.3 3.3 %fusion.21 = (f32[24,3,4,8,128]{4,0,3,2,1:T(8,128)S(1)}, f32[24,3,4,8,128]{4,0,3,2,1:T(8,128)S(1)}, f32[24,3,4,8,128]{4,0,3,2,1:T(8,128)}, f32[24,3,4,8,128]{4,0...) fusion(f32[24,3,4,10,130]{4,0,3,2,1:T(8,128)S(1)} %copy_divide_fusion, ...), kind=kLoop, calls=%fused_computation.42 | loop fusion | flops 3538944 | bytes 13570560 | tf_op jit(solution)/shard_map/sub | solution.py:61
  66.6 0.9 multiply_add_fusion.4
  67.5 0.8 multiply_add_fusion.2
  68.3 1.0 multiply_add_fusion.1
  69.3 2.2 %fusion.17 = (f32[24,3,4,8,128]{4,0,3,2,1:T(8,128)S(1)}, f32[24,3,4,8,128]{4,0,3,2,1:T(8,128)S(1)}, f32[24,3,4,8,128]{4,0,3,2,1:T(8,128)S(1)}, f32[24,3,4,8,128]...) fusion(f32[24,3,4,10,130]{4,0,3,2,1:T(8,128)S(1)} %copy_divide_fusion, ...), kind=kLoop, calls=%fused_computation.38 | loop fusion | flops 3538944 | bytes 13570560 | tf_op jit(solution)/shard_map/sub | solution.py:61
  71.5 0.8 multiply_add_fusion.8
  72.3 1.0 multiply_add_fusion.6
  73.3 1.1 multiply_add_fusion.10
  74.4 3.5 %fusion.8 = (f32[24,3,4,8,128]{4,0,3,2,1:T(8,128)S(1)}, f32[24,3,4,8,128]{4,0,3,2,1:T(8,128)S(1)}, f32[24,3,4,8,128]{4,0,3,2,1:T(8,128)}, f32[24,3,4,8,128]{4,0,...) fusion(f32[24,3,4,10,130]{4,0,3,2,1:T(8,128)S(1)} %copy_divide_, ...), kind=kLoop, calls=%fused_computation.29 | loop fusion | flops 4128768 | bytes 15929856 | tf_op jit(solution)/shard_map/sub | solution.py:61
  77.8 1.1 fusion.133
  78.9 3.0 %fusion.12 = (f32[24,3,4,8,128]{4,0,3,2,1:T(8,128)S(1)}, f32[24,3,4,8,128]{4,0,3,2,1:T(8,128)S(1)}, f32[24,3,4,8,128]{4,0,3,2,1:T(8,128)}, f32[24,3,4,8,128]{4,0...) fusion(f32[24,3,4,10,130]{4,0,3,2,1:T(8,128)S(1)} %copy_divide_fusion, ...), kind=kLoop, calls=%fused_computation.33 | loop fusion | flops 3538944 | bytes 13570560 | tf_op jit(solution)/shard_map/sub | solution.py:61
  81.9 2.3 %multiply_add_fusion.12 = (f32[24,1,4,8,128]{4,0,3,2,1:T(8,128)}, f32[24,1,4,8,128]{4,0,3,2,1:T(8,128)}, f32[24,1,4,8,128]{4,0,3,2,1:T(8,128)}) fusion(f32[24,3,4,8,128]{4,0,3,2,1:T(8,128)} %get-tuple-element.53), kind=kLoop, calls=%fused_computation.176 | loop fusion | flops 884736 | bytes 2359296 | tf_op jit(solution)/shard_map/add | solution.py:74
  84.2 0.8 multiply_add_fusion.16
  85.1 1.0 multiply_add_fusion.15
  86.6 1.1 multiply_add_fusion.18
  87.7 0.8 multiply_add_fusion.22
  88.5 1.0 multiply_add_fusion.21
  90.1 1.1 slice_multiply_fusion.15
  91.8 1.0 slice_multiply_fusion.17
  92.8 0.7 copy-done.8
  93.5 1.1 slice_multiply_fusion.18
  94.6 1.1 slice_multiply_fusion.20
  95.6 0.6 copy-done.10
  96.3 1.1 slice_multiply_fusion.22
  98.0 1.1 slice_multiply_fusion.23
  99.7 1.1 slice_multiply_fusion.25
  101.4 1.1 slice_multiply_fusion.26
  102.4 0.9 multiply_add_fusion.36
  103.3 1.1 multiply_add_fusion.35
  104.4 1.0 multiply_add_fusion.38
  105.4 0.9 multiply_add_fusion.43
  106.3 1.0 multiply_add_fusion.41
  107.3 1.1 multiply_add_fusion.45
  109.0 1.1 fusion.132
  110.1 1.1 multiply_add_fusion.48
  111.2 0.8 multiply_add_fusion.52
  112.0 1.0 multiply_add_fusion.50
  113.6 1.1 multiply_add_fusion.54
  115.5 1.2 copy-done.16
  117.1 12.6 %fusion.4 = f32[24,3,4,8,128]{4,0,3,2,1:T(8,128)S(1)} fusion(f32[24,64,1,1,1]{1,0,4,3,2:T(8,128)S(1)} %convolution_bitcast_fusion, f32[3,4,8,128,64]{3,2,1,0,4:T(8,128)S(1)} %bitcast.41, f32[24,1,4,8,128]{4,0,3,2,1:T(8,128)S(1)} %get-tuple-element.133, f32[24,1,4,8,128]{4,0,3,2,1:T(8,128)S(1)} %copy-done.18, ...), kind=kOutput, calls=%fused_computation.27 | convolution fusion | flops 258932736 | bytes 37804032 | tf_op jit(solution)/shard_map/dot_general | solution.py:126
  129.7 1.2 copy.119
  (103 shorter events, 8.3 us)
Async XLA Ops:
  0.0 46.4 %copy-start = (f32[1,64,64]{2,1,0:T(8,128)S(1)}, f32[1,64,64]{2,1,0:T(8,128)}, u32[]{:S(2)}) copy-start(f32[1,64,64]{2,1,0:T(8,128)} %param.9) | copy-start | bytes 49156
  0.0 9.2 %copy-start.2 = (f32[24,3,4,8,128]{4,3,2,1,0:T(8,128)S(1)}, f32[24,3,4,8,128]{4,3,2,1,0:T(8,128)}, u32[]{:S(2)}) copy-start(f32[24,3,4,8,128]{4,3,2,1,0:T(8,128)} %param.5) | copy-start | bytes 3538948
  0.0 9.2 %copy-start.17 = (f32[4,8,128]{2,1,0:T(8,128)S(1)}, f32[4,8,128]{2,1,0:T(8,128)}, u32[]{:S(2)}) copy-start(f32[4,8,128]{2,1,0:T(8,128)} %param.6) | copy-start | bytes 49156
  0.0 22.8 %copy-start.5 = (f32[64,3,4,8,128]{4,3,2,1,0:T(8,128)S(1)}, f32[64,3,4,8,128]{4,3,2,1,0:T(8,128)}, u32[]{:S(2)}) copy-start(f32[64,3,4,8,128]{4,3,2,1,0:T(8,128)} %param.8) | copy-start | bytes 9437188
  7.0 7.6 %copy-start.27 = (s32[1,1,4]{2,1,0:T(1,128)S(1)}, s32[1,1,4]{2,1,0:T(1,128)}, u32[]{:S(2)}) copy-start(s32[1,1,4]{2,1,0:T(1,128)} %param.7) | copy-start | bytes 52
  7.0 9.6 %collective-permute-start.4 = (f32[64,24]{0,1:T(8,128)S(1)}, f32[64,24]{0,1:T(8,128)S(1)}, u32[]{:S(2)}, u32[]{:S(2)}) collective-permute-start(f32[64,24]{0,1:T(8,128)S(1)} %fusion.80), channel_id=1, source_target_pairs={{0,8},{8,0},{16,24},{24,16},{32,40},{40,32},{48,56},{56,48},{64,72... | collective-permute-start | bytes 18440 | tf_op jit(solution)/shard_map/ppermute | solution.py:30
  9.3 20.4 %collective-permute-start.1 = (f32[73,4,1,128]{3,2,1,0:T(1,128)S(1)}, f32[73,4,1,128]{3,2,1,0:T(1,128)S(1)}, u32[]{:S(2)}, u32[]{:S(2)}) collective-permute-start(f32[73,4,1,128]{3,2,1,0:T(1,128)S(1)} %get-tuple-element.80), channel_id=1, source_target_pairs={{8,0},{16,8},{24,16},{32,24},{40,32},{48,40},{56,48},{64,56},{72,6... | collective-permute-start | bytes 448520 | tf_op jit(solution)/shard_map/ppermute | solution.py:20
  10.6 19.1 %collective-permute-start = (f32[73,4,1,128]{3,2,1,0:T(1,128)S(1)}, f32[73,4,1,128]{3,2,1,0:T(1,128)S(1)}, u32[]{:S(2)}, u32[]{:S(2)}) collective-permute-start(f32[73,4,1,128]{3,2,1,0:T(1,128)S(1)} %get-tuple-element.79), channel_id=1, source_target_pairs={{0,8},{8,16},{16,24},{24,32},{32,40},{40,48},{48,56},{56,64},{64,7... | collective-permute-start | bytes 448520 | tf_op jit(solution)/shard_map/ppermute | solution.py:19
  16.7 4.3 %collective-permute-start.5 = (f32[64,24]{0,1:T(8,128)S(1)}, f32[64,24]{0,1:T(8,128)S(1)}, u32[]{:S(2)}, u32[]{:S(2)}) collective-permute-start(f32[64,24]{0,1:T(8,128)S(1)} %add.699), channel_id=1, source_target_pairs={{0,16},{8,24},{16,0},{24,8},{32,48},{40,56},{48,32},{56,40},{64,80... | collective-permute-start | bytes 18440 | tf_op jit(solution)/shard_map/ppermute | solution.py:30
  20.9 5.9 %collective-permute-start.6 = (f32[64,24]{0,1:T(8,128)S(1)}, f32[64,24]{0,1:T(8,128)S(1)}, u32[]{:S(2)}, u32[]{:S(2)}) collective-permute-start(f32[64,24]{0,1:T(8,128)S(1)} %add.700), channel_id=1, source_target_pairs={{0,32},{8,40},{16,48},{24,56},{32,0},{40,8},{48,16},{56,24},{64,96... | collective-permute-start | bytes 18440 | tf_op jit(solution)/shard_map/ppermute | solution.py:30
  26.8 19.6 %collective-permute-start.7 = (f32[64,24]{0,1:T(8,128)S(1)}, f32[64,24]{0,1:T(8,128)S(1)}, u32[]{:S(2)}, u32[]{:S(2)}) collective-permute-start(f32[64,24]{0,1:T(8,128)S(1)} %add.701), channel_id=1, source_target_pairs={{0,64},{8,72},{16,80},{24,88},{32,96},{40,104},{48,112},{56,120},{... | collective-permute-start | bytes 18440 | tf_op jit(solution)/shard_map/ppermute | solution.py:30
  35.8 10.8 %collective-permute-start.3 = (f32[73,4,10,1]{0,1,3,2:T(4,128)S(1)}, f32[73,4,10,1]{0,1,3,2:T(4,128)S(1)}, u32[]{:S(2)}, u32[]{:S(2)}) collective-permute-start(f32[73,4,10,1]{0,1,3,2:T(4,128)S(1)} %copy.82), channel_id=1, source_target_pairs={{1,0},{2,1},{3,2},{4,3},{5,4},{6,5},{7,6},{9,8},{10,9},{11,10},{12... | collective-permute-start | bytes 35048 | tf_op jit(solution)/shard_map/ppermute | solution.py:20
  42.8 7.1 %collective-permute-start.2 = (f32[73,4,10,1]{0,1,3,2:T(4,128)S(1)}, f32[73,4,10,1]{0,1,3,2:T(4,128)S(1)}, u32[]{:S(2)}, u32[]{:S(2)}) collective-permute-start(f32[73,4,10,1]{0,1,3,2:T(4,128)S(1)} %copy.81), channel_id=1, source_target_pairs={{0,1},{1,2},{2,3},{3,4},{4,5},{5,6},{6,7},{8,9},{9,10},{10,11},{11... | collective-permute-start | bytes 35048 | tf_op jit(solution)/shard_map/ppermute | solution.py:19
  53.2 1.7 %copy-start.3 = (f32[73,4,10,1]{3,2,1,0:T(8,128)S(1)}, f32[73,4,10,1]{3,2,1,0:T(8,128)}, u32[]{:S(2)}) copy-start(f32[73,4,10,1]{3,2,1,0:T(8,128)} %copy.84) | copy-start | bytes 35044
  53.2 2.4 %copy-start.4 = (f32[73,4,10,1]{3,2,1,0:T(8,128)S(1)}, f32[73,4,10,1]{3,2,1,0:T(8,128)}, u32[]{:S(2)}) copy-start(f32[73,4,10,1]{3,2,1,0:T(8,128)} %copy.83) | copy-start | bytes 35044
  85.1 1.6 %copy-start.15 = (f32[24,3,4,8,128]{4,0,3,2,1:T(8,128)S(1)}, f32[24,3,4,8,128]{4,0,3,2,1:T(8,128)}, u32[]{:S(2)}) copy-start(f32[24,3,4,8,128]{4,0,3,2,1:T(8,128)} %get-tuple-element.48) | copy-start | bytes 3538948
  88.5 1.6 %copy-start.7 = (f32[24,3,4,8,128]{4,0,3,2,1:T(8,128)S(1)}, f32[24,3,4,8,128]{4,0,3,2,1:T(8,128)}, u32[]{:S(2)}) copy-start(f32[24,3,4,8,128]{4,0,3,2,1:T(8,128)} %get-tuple-element.58) | copy-start | bytes 3538948
  90.1 1.7 %copy-start.6 = (f32[24,3,4,8,128]{4,0,3,2,1:T(8,128)S(1)}, f32[24,3,4,8,128]{4,0,3,2,1:T(8,128)}, u32[]{:S(2)}) copy-start(f32[24,3,4,8,128]{4,0,3,2,1:T(8,128)} %get-tuple-element.46) | copy-start | bytes 3538948
  91.8 1.7 %copy-start.8 = (f32[24,3,4,8,128]{4,0,3,2,1:T(8,128)S(1)}, f32[24,3,4,8,128]{4,0,3,2,1:T(8,128)}, u32[]{:S(2)}) copy-start(f32[24,3,4,8,128]{4,0,3,2,1:T(8,128)} %get-tuple-element.55) | copy-start | bytes 3538948
  94.6 1.7 %copy-start.10 = (f32[24,3,4,8,128]{4,0,3,2,1:T(8,128)S(1)}, f32[24,3,4,8,128]{4,0,3,2,1:T(8,128)}, u32[]{:S(2)}) copy-start(f32[24,3,4,8,128]{4,0,3,2,1:T(8,128)} %get-tuple-element.52) | copy-start | bytes 3538948
  96.3 1.7 %copy-start.9 = (f32[24,3,4,8,128]{4,0,3,2,1:T(8,128)S(1)}, f32[24,3,4,8,128]{4,0,3,2,1:T(8,128)}, u32[]{:S(2)}) copy-start(f32[24,3,4,8,128]{4,0,3,2,1:T(8,128)} %get-tuple-element.28) | copy-start | bytes 3538948
  98.0 1.7 %copy-start.14 = (f32[24,3,4,8,128]{4,0,3,2,1:T(8,128)S(1)}, f32[24,3,4,8,128]{4,0,3,2,1:T(8,128)}, u32[]{:S(2)}) copy-start(f32[24,3,4,8,128]{4,0,3,2,1:T(8,128)} %get-tuple-element.47) | copy-start | bytes 3538948
  99.7 1.7 %copy-start.13 = (f32[24,3,4,8,128]{4,0,3,2,1:T(8,128)S(1)}, f32[24,3,4,8,128]{4,0,3,2,1:T(8,128)}, u32[]{:S(2)}) copy-start(f32[24,3,4,8,128]{4,0,3,2,1:T(8,128)} %get-tuple-element.25) | copy-start | bytes 3538948
  107.3 1.7 %copy-start.12 = (f32[24,3,4,8,128]{4,0,3,2,1:T(8,128)S(1)}, f32[24,3,4,8,128]{4,0,3,2,1:T(8,128)}, u32[]{:S(2)}) copy-start(f32[24,3,4,8,128]{4,0,3,2,1:T(8,128)} %get-tuple-element.50) | copy-start | bytes 3538948
  112.0 1.6 %copy-start.11 = (f32[24,3,4,8,128]{4,0,3,2,1:T(8,128)S(1)}, f32[24,3,4,8,128]{4,0,3,2,1:T(8,128)}, u32[]{:S(2)}) copy-start(f32[24,3,4,8,128]{4,0,3,2,1:T(8,128)} %get-tuple-element.49) | copy-start | bytes 3538948
  113.6 1.6 %copy-start.22 = (f32[24,1,4,8,128]{4,0,3,2,1:T(8,128)S(1)}, f32[24,1,4,8,128]{4,0,3,2,1:T(8,128)}, u32[]{:S(2)}) copy-start(f32[24,1,4,8,128]{4,0,3,2,1:T(8,128)} %get-tuple-element.126) | copy-start | bytes 1179652
  113.6 1.6 %copy-start.23 = (f32[24,1,4,8,128]{4,0,3,2,1:T(8,128)S(1)}, f32[24,1,4,8,128]{4,0,3,2,1:T(8,128)}, u32[]{:S(2)}) copy-start(f32[24,1,4,8,128]{4,0,3,2,1:T(8,128)} %get-tuple-element.127) | copy-start | bytes 1179652
  113.6 1.7 %copy-start.24 = (f32[24,1,4,8,128]{4,0,3,2,1:T(8,128)S(1)}, f32[24,1,4,8,128]{4,0,3,2,1:T(8,128)}, u32[]{:S(2)}) copy-start(f32[24,1,4,8,128]{4,0,3,2,1:T(8,128)} %get-tuple-element.128) | copy-start | bytes 1179652
  113.6 1.8 %copy-start.25 = (f32[24,1,4,8,128]{4,0,3,2,1:T(8,128)S(1)}, f32[24,1,4,8,128]{4,0,3,2,1:T(8,128)}, u32[]{:S(2)}) copy-start(f32[24,1,4,8,128]{4,0,3,2,1:T(8,128)} %get-tuple-element.123) | copy-start | bytes 1179652
  113.6 1.9 %copy-start.26 = (f32[24,1,4,8,128]{4,0,3,2,1:T(8,128)S(1)}, f32[24,1,4,8,128]{4,0,3,2,1:T(8,128)}, u32[]{:S(2)}) copy-start(f32[24,1,4,8,128]{4,0,3,2,1:T(8,128)} %get-tuple-element.124) | copy-start | bytes 1179652
  114.7 2.0 %copy-start.16 = (f32[8,8,96,128]{3,2,1,0:T(8,128)S(1)}, f32[8,8,96,128]{3,2,1,0:T(8,128)}, u32[]{:S(2)}) copy-start(f32[8,8,96,128]{3,2,1,0:T(8,128)} %copy.125) | copy-start | bytes 9437188
  114.7 2.0 %copy-start.18 = (f32[24,1,4,8,128]{4,0,3,2,1:T(8,128)S(1)}, f32[24,1,4,8,128]{4,0,3,2,1:T(8,128)}, u32[]{:S(2)}) copy-start(f32[24,1,4,8,128]{4,0,3,2,1:T(8,128)} %get-tuple-element.134) | copy-start | bytes 1179652
  114.8 2.1 %copy-start.19 = (f32[24,1,4,8,128]{4,0,3,2,1:T(8,128)S(1)}, f32[24,1,4,8,128]{4,0,3,2,1:T(8,128)}, u32[]{:S(2)}) copy-start(f32[24,1,4,8,128]{4,0,3,2,1:T(8,128)} %get-tuple-element.129) | copy-start | bytes 1179652
  114.8 2.2 %copy-start.20 = (f32[24,1,4,8,128]{4,0,3,2,1:T(8,128)S(1)}, f32[24,1,4,8,128]{4,0,3,2,1:T(8,128)}, u32[]{:S(2)}) copy-start(f32[24,1,4,8,128]{4,0,3,2,1:T(8,128)} %get-tuple-element.130) | copy-start | bytes 1179652
  114.8 2.3 %copy-start.21 = (f32[24,1,4,8,128]{4,0,3,2,1:T(8,128)S(1)}, f32[24,1,4,8,128]{4,0,3,2,1:T(8,128)}, u32[]{:S(2)}) copy-start(f32[24,1,4,8,128]{4,0,3,2,1:T(8,128)} %get-tuple-element.131) | copy-start | bytes 1179652
  117.1 13.9 %copy-start.1 = (f32[1,64,64]{2,1,0:T(8,128)S(1)}, f32[1,64,64]{2,1,0:T(8,128)}, u32[]{:S(2)}) copy-start(f32[1,64,64]{2,1,0:T(8,128)} %param.9) | copy-start | bytes 49156

commit v2 on v1

v2 whole, which is shorter than its diff:
```python
import jax
import jax.numpy as jnp
from jax import lax
from jax.experimental import pallas as pl
from jax.experimental.pallas import tpu as pltpu
from jax.sharding import PartitionSpec as P

RELAX_WEIGHT = 0.7
MASS_SHIFT = 0.5
DIAGONAL_SLOPE = 0.6 + 0.4 / 3.0
BOND_TOTAL = 44.0 / 3.0

OFFSETS = [
    (step_p, step_x, step_y)
    for step_p in (-1, 0, 1)
    for step_x in (-1, 0, 1)
    for step_y in (-1, 0, 1)
    if (step_p, step_x, step_y) != (0, 0, 0)
]
OWN_ENTRIES = ((0, 0), (1, 1), (2, 2), (0, 1), (0, 2), (1, 2))


def butterfly_sum(x, axis):
    size = lax.axis_size(axis)
    step = 1
    while step < size:
        pairs = [(i, i ^ step) for i in range(size)]
        x = x + lax.ppermute(x, axis, pairs)
        step *= 2
    return x


def neighbour_shift(tile, row_lo, row_hi, col_lo, col_hi, step_x, step_y):
    rows, cols = tile.shape
    if step_x != 0:
        rolled = pltpu.roll(tile, (-step_x) % rows, 0)
        sub = lax.broadcasted_iota(jnp.int32, tile.shape, 0)
        edge = rows - 1 if step_x > 0 else 0
        halo = row_hi if step_x > 0 else row_lo
        tile = jnp.where(sub == edge, jnp.broadcast_to(halo, tile.shape), rolled)
    if step_y != 0:
        rolled = pltpu.roll(tile, (-step_y) % cols, 1)
        lane = lax.broadcasted_iota(jnp.int32, tile.shape, 1)
        edge = cols - 1 if step_y > 0 else 0
        halo = col_hi if step_y > 0 else col_lo
        tile = jnp.where(lane == edge, jnp.broadcast_to(halo, tile.shape), rolled)
    return tile


def smoother_kernel(
    sides_ref, rs_ref, mod_ref, rlo_ref, rhi_ref, clo_ref, chi_ref, out_ref, coef_ref, own_ref, inv_ref,
    frlo_ref, frhi_ref, fclo_ref, fchi_ref,
):
    channels, planes, rows, cols = rs_ref.shape
    loads = channels // 3
    mod_channel = channels
    shape = (rows, cols)
    sub = lax.broadcasted_iota(jnp.int32, shape, 0)
    lane = lax.broadcasted_iota(jnp.int32, shape, 1)
    one = jnp.ones(shape, jnp.float32)
    factor_x = {
        -1: jnp.where(sub == 0, sides_ref[0], one),
        0: None,
        1: jnp.where(sub == rows - 1, sides_ref[1], one),
    }
    factor_y = {
        -1: jnp.where(lane == 0, sides_ref[2], one),
        0: None,
        1: jnp.where(lane == cols - 1, sides_ref[3], one),
    }

    def halo_pieces(refs, channel, plane, step_x):
        row_lo = refs[0][channel, pl.ds(plane, 1), :]
        row_hi = refs[1][channel, pl.ds(plane, 1), :]
        col_lo = refs[2][channel, plane, pl.ds(1 + step_x, rows), :]
        col_hi = refs[3][channel, plane, pl.ds(1 + step_x, rows), :]
        return row_lo, row_hi, col_lo, col_hi

    raw_halos = (rlo_ref, rhi_ref, clo_ref, chi_ref)
    first_halos = (frlo_ref, frhi_ref, fclo_ref, fchi_ref)
    for raw, first in zip(raw_halos, first_halos):
        first[...] = RELAX_WEIGHT * raw[0:channels] / (
            MASS_SHIFT + DIAGONAL_SLOPE * raw[mod_channel : mod_channel + 1]
        )

    for plane in range(planes):
        own_modulus = mod_ref[plane]
        inv_ref[plane] = 1.0 / (MASS_SHIFT + DIAGONAL_SLOPE * own_modulus)
        own = [None] * 6
        for index, (step_p, step_x, step_y) in enumerate(OFFSETS):
            source = plane + step_p
            length = step_p * step_p + step_x * step_x + step_y * step_y
            weight = 1.0 / (length * BOND_TOTAL)
            if 0 <= source < planes:
                pieces = halo_pieces(raw_halos, mod_channel, source, step_x)
                near_modulus = neighbour_shift(mod_ref[source], *pieces, step_x, step_y)
                bond = (0.5 * weight) * (own_modulus + near_modulus)
                coefficient = bond
                if factor_x[step_x] is not None:
                    coefficient = coefficient * factor_x[step_x]
                if factor_y[step_y] is not None:
                    coefficient = coefficient * factor_y[step_y]
                coef_ref[0, index, plane] = 0.6 * coefficient
                coef_ref[1, index, plane] = (0.4 / length) * coefficient
            else:
                bond = (0.5 * weight) * own_modulus
            direction = (step_p, step_x, step_y)
            for entry, (a, b) in enumerate(OWN_ENTRIES):
                scale = 0.4 * direction[a] * direction[b] / length
                if a == b:
                    scale += 0.6
                if scale == 0.0:
                    continue
                term = scale * bond
                own[entry] = term if own[entry] is None else own[entry] + term
        for entry, (a, b) in enumerate(OWN_ENTRIES):
            value = own[entry]
            if a == b:
                value = value + MASS_SHIFT
            own_ref[entry, plane] = value

    def one_load(load, carry):
        base = load * 3
        first = [[None] * planes for _ in range(3)]
        for component in range(3):
            for plane in range(planes):
                first[component][plane] = (
                    RELAX_WEIGHT * rs_ref[base + component, plane] * inv_ref[plane]
                )
        applied = [[None] * 3 for _ in range(planes)]
        for plane in range(planes):
            f = [first[k][plane] for k in range(3)]
            own = [own_ref[e, plane] for e in range(6)]
            applied[plane][0] = own[0] * f[0] + own[3] * f[1] + own[4] * f[2]
            applied[plane][1] = own[3] * f[0] + own[1] * f[1] + own[5] * f[2]
            applied[plane][2] = own[4] * f[0] + own[5] * f[1] + own[2] * f[2]
        for source in range(planes):
            for step_x in (-1, 0, 1):
                for step_y in (-1, 0, 1):
                    targets = [
                        (source - step_p, step_p)
                        for step_p in (-1, 0, 1)
                        if 0 <= source - step_p < planes and (step_p, step_x, step_y) != (0, 0, 0)
                    ]
                    if not targets:
                        continue
                    near = []
                    for component in range(3):
                        pieces = halo_pieces(first_halos, base + component, source, step_x)
                        near.append(
                            neighbour_shift(first[component][source], *pieces, step_x, step_y)
                        )
                    for plane, step_p in targets:
                        direction = (step_p, step_x, step_y)
                        index = OFFSETS.index(direction)
                        projected = None
                        for component in range(3):
                            if direction[component] == 0:
                                continue
                            term = near[component]
                            if projected is None:
                                projected = term if direction[component] > 0 else -term
                            elif direction[component] > 0:
                                projected = projected + term
                            else:
                                projected = projected - term
                        along = coef_ref[1, index, plane] * projected
                        straight = coef_ref[0, index, plane]
                        for component in range(3):
                            value = applied[plane][component] - straight * near[component]
                            if direction[component] > 0:
                                value = value - along
                            elif direction[component] < 0:
                                value = value + along
                            applied[plane][component] = value
        for component in range(3):
            for plane in range(planes):
                load_tile = rs_ref[base + component, plane]
                out_ref[base + component, plane] = first[component][plane] + RELAX_WEIGHT * (
                    load_tile - applied[plane][component]
                ) * inv_ref[plane]
        return carry

    lax.fori_loop(0, loads, one_load, 0)


def smoother(sides, loads, modulus, row_lo, row_hi, col_lo, col_hi):
    channels, planes, rows, cols = loads.shape
    vmem = pltpu.MemorySpace.VMEM
    return pl.pallas_call(
        smoother_kernel,
        out_shape=jax.ShapeDtypeStruct(loads.shape, jnp.float32),
        in_specs=[pl.BlockSpec(memory_space=pltpu.MemorySpace.SMEM)]
        + [pl.BlockSpec(memory_space=vmem)] * 6,
        out_specs=pl.BlockSpec(memory_space=vmem),
        scratch_shapes=[
            pltpu.VMEM((2, len(OFFSETS), planes, rows, cols), jnp.float32),
            pltpu.VMEM((6, planes, rows, cols), jnp.float32),
            pltpu.VMEM((planes, rows, cols), jnp.float32),
            pltpu.VMEM((channels,) + row_lo.shape[1:], jnp.float32),
            pltpu.VMEM((channels,) + row_hi.shape[1:], jnp.float32),
            pltpu.VMEM((channels,) + col_lo.shape[1:], jnp.float32),
            pltpu.VMEM((channels,) + col_hi.shape[1:], jnp.float32),
        ],
    )(sides, loads, modulus, row_lo, row_hi, col_lo, col_hi)


def per_device(right_sides, modulus, margin_sides, coarse_vectors, coarse_inverse):
    load_count = right_sides.shape[0]
    plane_count = right_sides.shape[2]
    row_count = right_sides.shape[3]
    column_count = right_sides.shape[4]
    flat_vectors = coarse_vectors.reshape(coarse_vectors.shape[0], -1)
    flat_loads = right_sides.reshape(load_count, -1)
    partial_terms = lax.dot_general(
        flat_vectors, flat_loads, (((1,), (1,)), ((), ())), precision=lax.Precision.HIGHEST
    )
    restricted = butterfly_sum(partial_terms, "prow")

    loads = right_sides.reshape(load_count * 3, plane_count, row_count, column_count)
    stacked = jnp.concatenate([loads, modulus[None]], axis=0)
    prow_size = lax.axis_size("prow")
    up = [(i, i + 1) for i in range(prow_size - 1)]
    down = [(i + 1, i) for i in range(prow_size - 1)]
    row_lo = lax.ppermute(stacked[:, :, row_count - 1, :], "prow", up)
    row_hi = lax.ppermute(stacked[:, :, 0, :], "prow", down)
    pcol_size = lax.axis_size("pcol")
    up = [(i, i + 1) for i in range(pcol_size - 1)]
    down = [(i + 1, i) for i in range(pcol_size - 1)]
    last_column = jnp.concatenate(
        [row_lo[:, :, None, column_count - 1], stacked[:, :, :, column_count - 1], row_hi[:, :, None, column_count - 1]],
        axis=2,
    )
    first_column = jnp.concatenate(
        [row_lo[:, :, None, 0], stacked[:, :, :, 0], row_hi[:, :, None, 0]], axis=2
    )
    col_lo = lax.ppermute(last_column, "pcol", up)[..., None]
    col_hi = lax.ppermute(first_column, "pcol", down)[..., None]
    sides = margin_sides[0, 0].astype(jnp.float32)
    smoothed = smoother(sides, loads, modulus, row_lo, row_hi, col_lo, col_hi)

    solved = jnp.dot(coarse_inverse[0], restricted, precision=lax.Precision.HIGHEST)
    lifted = lax.dot_general(
        solved, flat_vectors, (((0,), (0,)), ((), ())), precision=lax.Precision.HIGHEST
    )
    return smoothed.reshape(right_sides.shape) + lifted.reshape(right_sides.shape)


def solution(mesh):
    in_specs = (
        P(None, None, None, "prow", "pcol"),
        P(None, "prow", "pcol"),
        P("prow", "pcol", None),
        P(None, None, None, "prow", "pcol"),
        P("pcol", None, None),
    )
    out_specs = P(None, None, None, "prow", "pcol")
    return jax.shard_map(
        per_device, mesh=mesh, in_specs=in_specs, out_specs=out_specs, check_vma=False
    )
```

time: 132 us -> 77.8 us (0.59)
  other arithmetic: 57.8 us -> 4.29 us
  Pallas kernels: 0 us -> 10.8 us
  matrix products: 19.8 us -> 12.3 us
  local copies, waits for them, and re-layouts: 29.5 us -> 22.2 us
  waiting for transfers between devices: 0.58 us -> 5.28 us
    add x26 -> x0, other arithmetic: 22.8 us -> none  [the longest x24 22.8 us: bond_sum(): piece = piece + 0.4 * direction[component] / length * projected]
    sub x4 -> x0, other arithmetic: 11.9 us -> none  [bond_sum(): difference = own_field - factor * near_field]
    pallas_call x0 -> x1, Pallas kernels: none -> 10.8 us  [smoother(): pl.pallas_call(smoother_kernel, out_shape=jax.ShapeDtypeStruct(loads.shap...]
    unnamed x58 -> x18, local copies, waits for them, and re-layouts: 12.7 us -> 2.7 us
    mul x13 -> x0, other arithmetic: 9.79 us -> none  [the longest x8 8.75 us: bond_sum(): piece = 0.6 * difference[..., component, :, :, :]]
    dot_general x1, matrix products: 12.6 us -> 5.15 us  [per_device(): lax.dot_general(solved, flat_vectors, (((0,), (0,)), ((), ())), precision...]
    broadcast_in_dim x0 -> x2, local copies, waits for them, and re-layouts: none -> 7.42 us  [the longest x1 4.1 us: per_device(): col_lo = lax.ppermute(last_column, 'pcol', up)[..., None]]
    ppermute x2 -> x0, local copies, waits for them, and re-layouts: 6.63 us -> none  [the longest x1 3.32 us: extended(): before = lax.ppermute(last, axis, up)]
  transfers between devices with their start and end apart: 8 -> 8, of which waited for: 1 -> 2; matrix products, arithmetic and copies ran while one was open for 15% -> 28% of each run, Pallas kernels for 0% -> 0%
where the time goes in v2:
time: 77.8 us; the launch traced here: 77.4 us
  starting transfers between devices  22.3 us (29%)
  local copies, waits for them, and re-layouts  22.2 us (29%)
  matrix products  12.3 us (16%)
  Pallas kernels  10.8 us (14%)
  waiting for transfers between devices  5.28 us (7%)
  other arithmetic  4.29 us (6%)
    pallas_call x1, Pallas kernels, smoother(): pl.pallas_call(smoother_kernel, out_shape=jax.ShapeDtypeStruct(loads.shap...  10.8 us
    ppermute x4, starting transfers between devices, butterfly_sum(): x = x + lax.ppermute(x, axis, pairs)  8.56 us
    dot_general x1, matrix products, per_device(): lax.dot_general(flat_vectors, flat_loads, (((1,), (1,)), ((), ())), preci...  6.95 us
    ppermute x1, starting transfers between devices, per_device(): col_lo = lax.ppermute(last_column, 'pcol', up)[..., None]  6.37 us
    dot_general x1, matrix products, per_device(): lax.dot_general(solved, flat_vectors, (((0,), (0,)), ((), ())), precision...  5.15 us
    broadcast_in_dim x1, local copies, waits for them, and re-layouts, per_device(): col_lo = lax.ppermute(last_column, 'pcol', up)[..., None]  4.1 us
    ppermute x1, starting transfers between devices, per_device(): row_lo = lax.ppermute(stacked[:, :, row_count - 1, :], 'prow', up)  3.99 us
    broadcast_in_dim x1, local copies, waits for them, and re-layouts, per_device(): col_hi = lax.ppermute(first_column, 'pcol', down)[..., None]  3.31 us
  transfers between devices with their start and end apart: 8, of which 2 were waited for; matrix products, arithmetic and copies ran while one was open for 28% of the time, Pallas kernels for 0%

profile of v2, /device:TPU:1, one launch (start us, length us, event | category | flops | bytes accessed | tf_op | source)
XLA Modules:
  0.0 77.4 jit_solution(18419925799293268000)
XLA Ops:
  0.0 0.0 copy-start
  0.0 0.0 copy-start.2
  0.0 6.9 %fusion.5 = f32[64,24]{0,1:T(8,128)S(1)} fusion(f32[24,3,4,8,128]{4,3,2,1,0:T(8,128)} %param.5, f32[64,3,4,8,128]{4,3,2,1,0:T(8,128)} %param.8), kind=kOutput, calls=%fused_computation.9 | convolution fusion | flops 226492416 | bytes 4331520 | tf_op jit(solution)/shard_map/dot_general | solution.py:215
  7.0 0.0 copy-start.5
  7.0 2.1 %collective-permute-start.4 = (f32[64,24]{0,1:T(8,128)S(1)}, f32[64,24]{0,1:T(8,128)S(1)}, u32[]{:S(2)}, u32[]{:S(2)}) collective-permute-start(f32[64,24]{0,1:T(8,128)S(1)} %fusion.5), channel_id=1, source_target_pairs={{0,8},{8,0},{16,24},{24,16},{32,40},{40,32},{48,56},{56,48},{64,72... | collective-permute-start | bytes 18440 | tf_op jit(solution)/shard_map/ppermute | solution.py:28
  9.1 0.0 copy-done.2
  9.1 0.3 copy.34
  9.4 0.0 copy-done.5
  9.4 0.0 copy-start.6
  9.4 0.8 %maximum_bitcast_fusion = (f32[73,4,128]{2,1,0:T(4,128)}, f32[73,4,128]{2,1,0:T(4,128)}) fusion(f32[1,4,8,128]{3,1,0,2:T(4,128)S(1)} %bitcast.46, f32[72,4,8,128]{3,1,0,2:T(4,128)S(1)} %bitcast.40), kind=kLoop, calls=%fused_computation.11 | loop fusion | flops 74752 | bytes 1495040 | tf_op jit(solution)/shard_map/squeeze | solution.py:226
  10.2 1.3 %collective-permute-start.1 = (f32[73,4,128]{2,1,0:T(4,128)}, f32[73,4,128]{2,1,0:T(4,128)S(1)}, u32[]{:S(2)}, u32[]{:S(2)}) collective-permute-start(f32[73,4,128]{2,1,0:T(4,128)} %get-tuple-element.7), channel_id=1, source_target_pairs={{8,0},{16,8},{24,16},{32,24},{40,32},{48,40},{56,48},{64,56},{72,6... | collective-permute-start | bytes 448520 | tf_op jit(solution)/shard_map/ppermute | solution.py:226
  11.5 4.0 %collective-permute-start = (f32[73,4,128]{2,1,0:T(4,128)}, f32[73,4,128]{2,1,0:T(4,128)S(1)}, u32[]{:S(2)}, u32[]{:S(2)}) collective-permute-start(f32[73,4,128]{2,1,0:T(4,128)} %get-tuple-element.8), channel_id=1, source_target_pairs={{0,8},{8,16},{16,24},{24,32},{32,40},{40,48},{48,56},{56,64},{64,7... | collective-permute-start | bytes 448520 | tf_op jit(solution)/shard_map/ppermute | solution.py:225
  15.5 0.0 collective-permute-done.4
  15.5 2.5 %collective-permute-start.5 = (f32[64,24]{0,1:T(8,128)S(1)}, f32[64,24]{0,1:T(8,128)S(1)}, u32[]{:S(2)}, u32[]{:S(2)}) collective-permute-start(f32[64,24]{0,1:T(8,128)S(1)} %add.15), channel_id=1, source_target_pairs={{0,16},{8,24},{16,0},{24,8},{32,48},{40,56},{48,32},{56,40},{64,80... | collective-permute-start | bytes 18440 | tf_op jit(solution)/shard_map/ppermute | solution.py:28
  18.1 0.0 copy-done.6
  18.1 0.5 convert_bitcast_fusion.sides_ref
  18.6 2.3 %collective-permute-done.5 = f32[64,24]{0,1:T(8,128)S(1)} collective-permute-done((f32[64,24]{0,1:T(8,128)S(1)}, f32[64,24]{0,1:T(8,128)S(1)}, u32[]{:S(2)}, u32[]{:S(2)}) %collective-permute-start.5) | collective-permute-done | bytes 6176 | tf_op jit(solution)/shard_map/ppermute | solution.py:28
  20.9 1.3 %collective-permute-start.6 = (f32[64,24]{0,1:T(8,128)S(1)}, f32[64,24]{0,1:T(8,128)S(1)}, u32[]{:S(2)}, u32[]{:S(2)}) collective-permute-start(f32[64,24]{0,1:T(8,128)S(1)} %add.16), channel_id=1, source_target_pairs={{0,32},{8,40},{16,48},{24,56},{32,0},{40,8},{48,16},{56,24},{64,96... | collective-permute-start | bytes 18440 | tf_op jit(solution)/shard_map/ppermute | solution.py:28
  22.2 2.3 %pad_maximum_fusion = (f32[73,4,8,1]{3,1,0,2:T(4,128)}, f32[73,4,8,1]{3,1,0,2:T(4,128)}) fusion(f32[1,4,8,128]{3,1,0,2:T(4,128)S(1)} %bitcast.47, f32[72,4,8,128]{3,1,0,2:T(4,128)S(1)} %bitcast.41), kind=kLoop, calls=%fused_computation.5 | loop fusion | flops 4672 | bytes 1214720 | tf_op jit(solution)/shard_map/concatenate | solution.py:221
  24.5 0.0 copy-start.1
  24.5 1.7 %copy.44.rs_ref = f32[72,4,8,128]{3,2,1,0:T(8,128)} copy(f32[72,4,8,128]{3,1,0,2:T(4,128)S(1)} %bitcast.42) | data formatting | bytes 2359296 | tf_op jit(solution)/shard_map/reshape | solution.py:220
  26.2 1.7 %copy.40 = f32[73,4,8,1]{0,2,3,1:T(8,128)S(1)} copy(f32[73,4,8,1]{3,1,0,2:T(4,128)} %get-tuple-element.5) | data formatting | bytes 18688 | tf_op jit(solution)/shard_map/slice | solution.py:235
  28.0 1.7 %copy.36 = f32[73,4,8,1]{0,2,3,1:T(8,128)S(1)} copy(f32[73,4,8,1]{3,1,0,2:T(4,128)} %get-tuple-element.6) | data formatting | bytes 18688 | tf_op jit(solution)/shard_map/slice | solution.py:231
  29.7 0.0 copy-done.1
  29.7 1.8 %copy.75 = f32[8,8,96,128]{3,1,2,0:T(8,128)S(1)} copy(f32[8,8,96,128]{3,2,1,0:T(8,128)S(1)} %bitcast.43) | data formatting | bytes 6291456
  31.5 0.6 copy.59
  32.1 0.0 collective-permute-done.6
  32.1 2.6 %collective-permute-start.7 = (f32[64,24]{0,1:T(8,128)S(1)}, f32[64,24]{0,1:T(8,128)S(1)}, u32[]{:S(2)}, u32[]{:S(2)}) collective-permute-start(f32[64,24]{0,1:T(8,128)S(1)} %add.17), channel_id=1, source_target_pairs={{0,64},{8,72},{16,80},{24,88},{32,96},{40,104},{48,112},{56,120},{... | collective-permute-start | bytes 18440 | tf_op jit(solution)/shard_map/ppermute | solution.py:28
  34.7 0.0 collective-permute-done.rlo_ref
  34.7 0.0 copy-start.4
  34.7 0.8 %fusion.12 = (f32[73,4,1]{2,1,0:T(4,128)}, f32[73,4,1]{2,1,0:T(4,128)}) fusion(f32[73,4,128]{2,1,0:T(4,128)S(1)} %collective-permute-done.rlo_ref), kind=kLoop, calls=%fused_computation.19 | loop fusion | bytes 4672 | tf_op jit(solution)/shard_map/slice | solution.py:235
  35.6 1.0 %copy.41 = f32[73,4,1]{0,2,1:T(1,128)S(1)} copy(f32[73,4,1]{2,1,0:T(4,128)} %get-tuple-element.9) | data formatting | bytes 2336 | tf_op jit(solution)/shard_map/slice | solution.py:235
  36.6 1.0 %copy.37 = f32[73,4,1]{0,2,1:T(1,128)S(1)} copy(f32[73,4,1]{2,1,0:T(4,128)} %get-tuple-element.10) | data formatting | bytes 2336 | tf_op jit(solution)/shard_map/slice | solution.py:231
  37.6 0.0 collective-permute-done.1.rhi_ref
  37.6 0.0 copy-start.3
  37.6 0.8 %fusion.13 = (f32[73,4,1]{2,1,0:T(4,128)}, f32[73,4,1]{2,1,0:T(4,128)}) fusion(f32[73,4,128]{2,1,0:T(4,128)S(1)} %collective-permute-done.1.rhi_ref), kind=kLoop, calls=%fused_computation.20 | loop fusion | bytes 4672 | tf_op jit(solution)/shard_map/slice | solution.py:235
  38.4 1.0 %copy.42 = f32[73,4,1]{0,2,1:T(1,128)S(1)} copy(f32[73,4,1]{2,1,0:T(4,128)} %get-tuple-element.11) | data formatting | bytes 2336 | tf_op jit(solution)/shard_map/slice | solution.py:235
  39.4 1.0 %copy.38 = f32[73,4,1]{0,2,1:T(1,128)S(1)} copy(f32[73,4,1]{2,1,0:T(4,128)} %get-tuple-element.12) | data formatting | bytes 2336 | tf_op jit(solution)/shard_map/slice | solution.py:231
  40.5 0.6 pad_maximum_fusion.1
  41.1 6.4 %collective-permute-start.2 = (f32[73,4,10]{0,2,1:T(8,128)}, f32[73,4,10]{0,2,1:T(8,128)}, u32[]{:S(2)}, u32[]{:S(2)}) collective-permute-start(f32[73,4,10]{0,2,1:T(8,128)} %pad_maximum_fusion.1), channel_id=1, source_target_pairs={{0,1},{1,2},{2,3},{3,4},{4,5},{5,6},{6,7},{8,9},{9,10},{10,11},{11... | collective-permute-start | bytes 35048 | tf_op jit(solution)/shard_map/ppermute | solution.py:237
  47.5 2.1 %collective-permute-start.3 = (f32[73,4,10]{0,2,1:T(8,128)S(1)}, f32[73,4,10]{0,2,1:T(8,128)S(1)}, u32[]{:S(2)}, u32[]{:S(2)}) collective-permute-start(f32[73,4,10]{0,2,1:T(8,128)S(1)} %pad_maximum_fusion.2), channel_id=1, source_target_pairs={{1,0},{2,1},{3,2},{4,3},{5,4},{6,5},{7,6},{9,8},{10,9},{11,10},{12... | collective-permute-start | bytes 35048 | tf_op jit(solution)/shard_map/ppermute | solution.py:238
  49.6 0.0 collective-permute-done.7
  49.6 0.0 copy-done
  49.6 0.2 convolution_bitcast_fusion
  49.8 2.9 %collective-permute-done.3 = f32[73,4,10]{0,2,1:T(8,128)S(1)} collective-permute-done((f32[73,4,10]{0,2,1:T(8,128)S(1)}, f32[73,4,10]{0,2,1:T(8,128)S(1)}, u32[]{:S(2)}, u32[]{:S(2)}) %collective-permute-start.3) | collective-permute-done | bytes 11712 | tf_op jit(solution)/shard_map/ppermute | solution.py:238
  52.8 3.3 %copy.46.chi_ref = f32[73,4,10,1]{3,2,1,0:T(8,128)} copy(f32[73,4,10,1]{0,2,1,3:T(8,128)S(1)} %bitcast.50) | data formatting | bytes 23360 | tf_op jit(solution)/shard_map/broadcast_in_dim | solution.py:238
  56.1 0.0 copy-done.4
  56.1 0.0 copy-done.3
  56.1 0.0 collective-permute-done.2
  56.1 4.1 %copy.45.clo_ref = f32[73,4,10,1]{3,2,1,0:T(8,128)} copy(f32[73,4,10,1]{0,2,1,3:T(8,128)} %bitcast.6) | data formatting | bytes 23360 | tf_op jit(solution)/shard_map/broadcast_in_dim | solution.py:237
  60.2 10.8 %shard_map.55 = f32[72,4,8,128]{3,2,1,0:T(8,128)} custom-call(f32[4]{0:T(128)} %convert_bitcast_fusion.sides_ref, f32[72,4,8,128]{3,2,1,0:T(8,128)} %copy.44.rs_ref, f32[4,8,128]{2,1,0:T(8,128)} %mod_ref.1, f32[73,4,128]{2,1,0:T(4,128)} %copy-done.4, f32[73,4,128]{2,1,0:T(4,128)} %copy-done.3, f32[73,4,10,1]{3,2,1,0:T(8,128)} %copy.45.clo_ref, ...), custom_call_target="tpu_custom_call" | custom-call | tf_op jit(solution)/shard_map/pallas_call | solution.py:190
  71.0 5.1 %copy_add_fusion = f32[24,3,4,8,128]{4,0,3,2,1:T(8,128)S(1)} fusion(f32[24,3,4,8,128]{4,3,2,1,0:T(8,128)} %bitcast.45, f32[24,64,1,1,1]{1,0,4,3,2:T(8,128)S(1)} %convolution_bitcast_fusion, f32[3,4,8,128,64]{3,2,1,0,4:T(8,128)S(1)} %bitcast.44), kind=kOutput, calls=%fused_computation.7 | convolution fusion | flops 226787328 | bytes 5511168 | tf_op jit(solution)/shard_map/dot_general | solution.py:243
  76.2 1.2 %copy.51 = f32[24,3,4,8,128]{4,3,2,1,0:T(8,128)} copy(f32[24,3,4,8,128]{4,0,3,2,1:T(8,128)S(1)} %copy_add_fusion) | data formatting | bytes 2359296 | tf_op jit(solution)/shard_map/add | solution.py:246
  (5 shorter events, 0.0 us)
Async XLA Ops:
  0.0 49.6 %copy-start = (f32[1,64,64]{2,1,0:T(8,128)S(1)}, f32[1,64,64]{2,1,0:T(8,128)}, u32[]{:S(2)}) copy-start(f32[1,64,64]{2,1,0:T(8,128)} %param.9) | copy-start | bytes 49156
  0.0 9.1 %copy-start.2 = (f32[24,3,4,8,128]{4,3,2,1,0:T(8,128)S(1)}, f32[24,3,4,8,128]{4,3,2,1,0:T(8,128)}, u32[]{:S(2)}) copy-start(f32[24,3,4,8,128]{4,3,2,1,0:T(8,128)} %param.5) | copy-start | bytes 3538948
  7.0 2.4 %copy-start.5 = (f32[4,8,128]{2,1,0:T(8,128)S(1)}, f32[4,8,128]{2,1,0:T(8,128)}, u32[]{:S(2)}) copy-start(f32[4,8,128]{2,1,0:T(8,128)} %mod_ref.1) | copy-start | bytes 49156
  7.0 8.5 %collective-permute-start.4 = (f32[64,24]{0,1:T(8,128)S(1)}, f32[64,24]{0,1:T(8,128)S(1)}, u32[]{:S(2)}, u32[]{:S(2)}) collective-permute-start(f32[64,24]{0,1:T(8,128)S(1)} %fusion.5), channel_id=1, source_target_pairs={{0,8},{8,0},{16,24},{24,16},{32,40},{40,32},{48,56},{56,48},{64,72... | collective-permute-start | bytes 18440 | tf_op jit(solution)/shard_map/ppermute | solution.py:28
  9.4 8.7 %copy-start.6 = (s32[1,1,4]{2,1,0:T(1,128)S(1)}, s32[1,1,4]{2,1,0:T(1,128)}, u32[]{:S(2)}) copy-start(s32[1,1,4]{2,1,0:T(1,128)} %param.7) | copy-start | bytes 52
  10.2 27.4 %collective-permute-start.1 = (f32[73,4,128]{2,1,0:T(4,128)}, f32[73,4,128]{2,1,0:T(4,128)S(1)}, u32[]{:S(2)}, u32[]{:S(2)}) collective-permute-start(f32[73,4,128]{2,1,0:T(4,128)} %get-tuple-element.7), channel_id=1, source_target_pairs={{8,0},{16,8},{24,16},{32,24},{40,32},{48,40},{56,48},{64,56},{72,6... | collective-permute-start | bytes 448520 | tf_op jit(solution)/shard_map/ppermute | solution.py:226
  11.5 23.2 %collective-permute-start = (f32[73,4,128]{2,1,0:T(4,128)}, f32[73,4,128]{2,1,0:T(4,128)S(1)}, u32[]{:S(2)}, u32[]{:S(2)}) collective-permute-start(f32[73,4,128]{2,1,0:T(4,128)} %get-tuple-element.8), channel_id=1, source_target_pairs={{0,8},{8,16},{16,24},{24,32},{32,40},{40,48},{48,56},{56,64},{64,7... | collective-permute-start | bytes 448520 | tf_op jit(solution)/shard_map/ppermute | solution.py:225
  15.5 5.4 %collective-permute-start.5 = (f32[64,24]{0,1:T(8,128)S(1)}, f32[64,24]{0,1:T(8,128)S(1)}, u32[]{:S(2)}, u32[]{:S(2)}) collective-permute-start(f32[64,24]{0,1:T(8,128)S(1)} %add.15), channel_id=1, source_target_pairs={{0,16},{8,24},{16,0},{24,8},{32,48},{40,56},{48,32},{56,40},{64,80... | collective-permute-start | bytes 18440 | tf_op jit(solution)/shard_map/ppermute | solution.py:28
  20.9 11.2 %collective-permute-start.6 = (f32[64,24]{0,1:T(8,128)S(1)}, f32[64,24]{0,1:T(8,128)S(1)}, u32[]{:S(2)}, u32[]{:S(2)}) collective-permute-start(f32[64,24]{0,1:T(8,128)S(1)} %add.16), channel_id=1, source_target_pairs={{0,32},{8,40},{16,48},{24,56},{32,0},{40,8},{48,16},{56,24},{64,96... | collective-permute-start | bytes 18440 | tf_op jit(solution)/shard_map/ppermute | solution.py:28
  24.5 5.2 %copy-start.1 = (f32[64,3,4,8,128]{4,3,2,1,0:T(8,128)S(1)}, f32[64,3,4,8,128]{4,3,2,1,0:T(8,128)}, u32[]{:S(2)}) copy-start(f32[64,3,4,8,128]{4,3,2,1,0:T(8,128)} %param.8) | copy-start | bytes 9437188
  32.1 17.5 %collective-permute-start.7 = (f32[64,24]{0,1:T(8,128)S(1)}, f32[64,24]{0,1:T(8,128)S(1)}, u32[]{:S(2)}, u32[]{:S(2)}) collective-permute-start(f32[64,24]{0,1:T(8,128)S(1)} %add.17), channel_id=1, source_target_pairs={{0,64},{8,72},{16,80},{24,88},{32,96},{40,104},{48,112},{56,120},{... | collective-permute-start | bytes 18440 | tf_op jit(solution)/shard_map/ppermute | solution.py:28
  34.7 21.3 %copy-start.4 = (f32[73,4,128]{2,1,0:T(4,128)}, f32[73,4,128]{2,1,0:T(4,128)S(1)}, u32[]{:S(2)}) copy-start(f32[73,4,128]{2,1,0:T(4,128)S(1)} %collective-permute-done.rlo_ref) | copy-start | bytes 448516
  37.6 18.5 %copy-start.3 = (f32[73,4,128]{2,1,0:T(4,128)}, f32[73,4,128]{2,1,0:T(4,128)S(1)}, u32[]{:S(2)}) copy-start(f32[73,4,128]{2,1,0:T(4,128)S(1)} %collective-permute-done.1.rhi_ref) | copy-start | bytes 448516
  41.1 15.0 %collective-permute-start.2 = (f32[73,4,10]{0,2,1:T(8,128)}, f32[73,4,10]{0,2,1:T(8,128)}, u32[]{:S(2)}, u32[]{:S(2)}) collective-permute-start(f32[73,4,10]{0,2,1:T(8,128)} %pad_maximum_fusion.1), channel_id=1, source_target_pairs={{0,1},{1,2},{2,3},{3,4},{4,5},{5,6},{6,7},{8,9},{9,10},{10,11},{11... | collective-permute-start | bytes 35048 | tf_op jit(solution)/shard_map/ppermute | solution.py:237
  47.5 5.2 %collective-permute-start.3 = (f32[73,4,10]{0,2,1:T(8,128)S(1)}, f32[73,4,10]{0,2,1:T(8,128)S(1)}, u32[]{:S(2)}, u32[]{:S(2)}) collective-permute-start(f32[73,4,10]{0,2,1:T(8,128)S(1)} %pad_maximum_fusion.2), channel_id=1, source_target_pairs={{1,0},{2,1},{3,2},{4,3},{5,4},{6,5},{7,6},{9,8},{10,9},{11,10},{12... | collective-permute-start | bytes 35048 | tf_op jit(solution)/shard_map/ppermute | solution.py:238

commit v3 on v2

--- a/solution.py
+++ b/solution.py
@@ -47,9 +47,50 @@
     return tile
 
 
+def pack_kernel(rs_ref, mod_ref, row_first_ref, row_last_ref, col_first_ref, col_last_ref):
+    channels, planes, rows, cols = rs_ref.shape
+    lane = lax.broadcasted_iota(jnp.int32, (rows, cols), 1)
+    tiles = col_first_ref.shape[1] // cols
+    first = [jnp.zeros((rows, cols), jnp.float32) for _ in range(tiles)]
+    last = [jnp.zeros((rows, cols), jnp.float32) for _ in range(tiles)]
+    for channel in range(channels + 1):
+        for plane in range(planes):
+            tile = rs_ref[channel, plane] if channel < channels else mod_ref[plane]
+            j = channel * planes + plane
+            row_first_ref[pl.ds(j, 1), :] = tile[0:1, :]
+            row_last_ref[pl.ds(j, 1), :] = tile[rows - 1 : rows, :]
+            group, place = divmod(j, cols)
+            first[group] = jnp.where(lane == place, pltpu.roll(tile, place, 1), first[group])
+            last[group] = jnp.where(
+                lane == place, pltpu.roll(tile, (place + 1) % cols, 1), last[group]
+            )
+    for group in range(tiles):
+        col_first_ref[:, pl.ds(group * cols, cols)] = first[group]
+        col_last_ref[:, pl.ds(group * cols, cols)] = last[group]
+
+
+def pack(loads, modulus):
+    channels, planes, rows, cols = loads.shape
+    count = (channels + 1) * planes
+    lanes = -(-count // cols) * cols
+    vmem = pltpu.MemorySpace.VMEM
+    return pl.pallas_call(
+        pack_kernel,
+        out_shape=[
+            jax.ShapeDtypeStruct((count, cols), jnp.float32),
+            jax.ShapeDtypeStruct((count, cols), jnp.float32),
+            jax.ShapeDtypeStruct((rows, lanes), jnp.float32),
+            jax.ShapeDtypeStruct((rows, lanes), jnp.float32),
+        ],
+        in_specs=[pl.BlockSpec(memory_space=vmem)] * 2,
+        out_specs=[pl.BlockSpec(memory_space=vmem)] * 4,
+    )(loads, modulus)
+
+
 def smoother_kernel(
-    sides_ref, rs_ref, mod_ref, rlo_ref, rhi_ref, clo_ref, chi_ref, out_ref, coef_ref, own_ref, inv_ref,
-    frlo_ref, frhi_ref, fclo_ref, fchi_ref,
+    sides_ref, rs_ref, mod_ref, rlo_ref, rhi_ref, clo_ref, chi_ref,
+    cll_ref, clh_ref, chl_ref, chh_ref,
+    out_ref, coef_ref, own_ref, inv_ref, row_ref, col_ref,
 ):
     channels, planes, rows, cols = rs_ref.shape
     loads = channels // 3
@@ -69,19 +110,37 @@
         1: jnp.where(lane == cols - 1, sides_ref[3], one),
     }
 
-    def halo_pieces(refs, channel, plane, step_x):
-        row_lo = refs[0][channel, pl.ds(plane, 1), :]
-        row_hi = refs[1][channel, pl.ds(plane, 1), :]
-        col_lo = refs[2][channel, plane, pl.ds(1 + step_x, rows), :]
-        col_hi = refs[3][channel, plane, pl.ds(1 + step_x, rows), :]
+    def halo_pieces(channel, plane, step_x):
+        row_lo = row_ref[0, channel, pl.ds(plane, 1), :]
+        row_hi = row_ref[1, channel, pl.ds(plane, 1), :]
+        col_lo = col_ref[0, channel, plane, pl.ds(1 + step_x, rows), :]
+        col_hi = col_ref[1, channel, plane, pl.ds(1 + step_x, rows), :]
         return row_lo, row_hi, col_lo, col_hi
 
-    raw_halos = (rlo_ref, rhi_ref, clo_ref, chi_ref)
-    first_halos = (frlo_ref, frhi_ref, fclo_ref, fchi_ref)
-    for raw, first in zip(raw_halos, first_halos):
-        first[...] = RELAX_WEIGHT * raw[0:channels] / (
-            MASS_SHIFT + DIAGONAL_SLOPE * raw[mod_channel : mod_channel + 1]
-        )
+    for channel in range(channels + 1):
+        row_ref[0, channel] = rlo_ref[pl.ds(channel * planes, planes), :]
+        row_ref[1, channel] = rhi_ref[pl.ds(channel * planes, planes), :]
+        for plane in range(planes):
+            j = channel * planes + plane
+            group, place = divmod(j, cols)
+            window = pl.ds(group * cols, cols)
+            for side, (edge, column, corner_lo, corner_hi) in enumerate(
+                ((0, clo_ref, cll_ref, chl_ref), (cols - 1, chi_ref, clh_ref, chh_ref))
+            ):
+                shift = (edge - place) % cols
+                col_ref[side, channel, plane, pl.ds(1, rows), :] = pltpu.roll(
+                    column[:, window], shift, 1
+                )
+                col_ref[side, channel, plane, pl.ds(0, 1), :] = pltpu.roll(
+                    corner_lo[pl.ds(rows - 1, 1), window], shift, 1
+                )
+                col_ref[side, channel, plane, pl.ds(rows + 1, 1), :] = pltpu.roll(
+                    corner_hi[pl.ds(0, 1), window], shift, 1
+                )
+    row_inverse = RELAX_WEIGHT / (MASS_SHIFT + DIAGONAL_SLOPE * row_ref[:, mod_channel : mod_channel + 1])
+    row_ref[:, 0:channels] = row_ref[:, 0:channels] * row_inverse
+    col_inverse = RELAX_WEIGHT / (MASS_SHIFT + DIAGONAL_SLOPE * col_ref[:, mod_channel : mod_channel + 1, :, 0 : rows + 2])
+    col_ref[:, 0:channels, :, 0 : rows + 2] = col_ref[:, 0:channels, :, 0 : rows + 2] * col_inverse
 
     for plane in range(planes):
         own_modulus = mod_ref[plane]
@@ -92,7 +151,7 @@
             length = step_p * step_p + step_x * step_x + step_y * step_y
             weight = 1.0 / (length * BOND_TOTAL)
             if 0 <= source < planes:
-                pieces = halo_pieces(raw_halos, mod_channel, source, step_x)
+                pieces = halo_pieces(mod_channel, source, step_x)
                 near_modulus = neighbour_shift(mod_ref[source], *pieces, step_x, step_y)
                 bond = (0.5 * weight) * (own_modulus + near_modulus)
                 coefficient = bond
@@ -146,7 +205,7 @@
                         continue
                     near = []
                     for component in range(3):
-                        pieces = halo_pieces(first_halos, base + component, source, step_x)
+                        pieces = halo_pieces(base + component, source, step_x)
                         near.append(
                             neighbour_shift(first[component][source], *pieces, step_x, step_y)
                         )
@@ -184,25 +243,23 @@
     lax.fori_loop(0, loads, one_load, 0)
 
 
-def smoother(sides, loads, modulus, row_lo, row_hi, col_lo, col_hi):
+def smoother(sides, loads, modulus, halos):
     channels, planes, rows, cols = loads.shape
     vmem = pltpu.MemorySpace.VMEM
     return pl.pallas_call(
         smoother_kernel,
         out_shape=jax.ShapeDtypeStruct(loads.shape, jnp.float32),
         in_specs=[pl.BlockSpec(memory_space=pltpu.MemorySpace.SMEM)]
-        + [pl.BlockSpec(memory_space=vmem)] * 6,
+        + [pl.BlockSpec(memory_space=vmem)] * (2 + len(halos)),
         out_specs=pl.BlockSpec(memory_space=vmem),
         scratch_shapes=[
             pltpu.VMEM((2, len(OFFSETS), planes, rows, cols), jnp.float32),
             pltpu.VMEM((6, planes, rows, cols), jnp.float32),
             pltpu.VMEM((planes, rows, cols), jnp.float32),
-            pltpu.VMEM((channels,) + row_lo.shape[1:], jnp.float32),
-            pltpu.VMEM((channels,) + row_hi.shape[1:], jnp.float32),
-            pltpu.VMEM((channels,) + col_lo.shape[1:], jnp.float32),
-            pltpu.VMEM((channels,) + col_hi.shape[1:], jnp.float32),
+            pltpu.VMEM((2, channels + 1, planes, cols), jnp.float32),
+            pltpu.VMEM((2, channels + 1, planes, 2 * rows, cols), jnp.float32),
         ],
-    )(sides, loads, modulus, row_lo, row_hi, col_lo, col_hi)
+    )(sides, loads, modulus, *halos)
 
 
 def per_device(right_sides, modulus, margin_sides, coarse_vectors, coarse_inverse):
@@ -210,40 +267,47 @@
     plane_count = right_sides.shape[2]
     row_count = right_sides.shape[3]
     column_count = right_sides.shape[4]
-    flat_vectors = coarse_vectors.reshape(coarse_vectors.shape[0], -1)
-    flat_loads = right_sides.reshape(load_count, -1)
+    cell_dims = (1, 2, 3, 4)
     partial_terms = lax.dot_general(
-        flat_vectors, flat_loads, (((1,), (1,)), ((), ())), precision=lax.Precision.HIGHEST
+        coarse_vectors, right_sides, ((cell_dims, cell_dims), ((), ())), precision=lax.Precision.HIGHEST
     )
     restricted = butterfly_sum(partial_terms, "prow")
 
     loads = right_sides.reshape(load_count * 3, plane_count, row_count, column_count)
-    stacked = jnp.concatenate([loads, modulus[None]], axis=0)
-    prow_size = lax.axis_size("prow")
-    up = [(i, i + 1) for i in range(prow_size - 1)]
-    down = [(i + 1, i) for i in range(prow_size - 1)]
-    row_lo = lax.ppermute(stacked[:, :, row_count - 1, :], "prow", up)
-    row_hi = lax.ppermute(stacked[:, :, 0, :], "prow", down)
-    pcol_size = lax.axis_size("pcol")
-    up = [(i, i + 1) for i in range(pcol_size - 1)]
-    down = [(i + 1, i) for i in range(pcol_size - 1)]
-    last_column = jnp.concatenate(
-        [row_lo[:, :, None, column_count - 1], stacked[:, :, :, column_count - 1], row_hi[:, :, None, column_count - 1]],
-        axis=2,
-    )
-    first_column = jnp.concatenate(
-        [row_lo[:, :, None, 0], stacked[:, :, :, 0], row_hi[:, :, None, 0]], axis=2
-    )
-    col_lo = lax.ppermute(last_column, "pcol", up)[..., None]
-    col_hi = lax.ppermute(first_column, "pcol", down)[..., None]
+    row_first, row_last, col_first, col_last = pack(loads, modulus)
+    rows_n = lax.axis_size("prow")
+    cols_n = lax.axis_size("pcol")
+
+    def line(source, axis, size, step):
+        pairs = [(i, i + step) for i in range(size) if 0 <= i + step < size]
+        return lax.ppermute(source, axis, pairs)
+
+    def diagonal(source, step_row, step_col):
+        pairs = []
+        for a in range(rows_n):
+            for b in range(cols_n):
+                if 0 <= a + step_row < rows_n and 0 <= b + step_col < cols_n:
+                    pairs.append((a * cols_n + b, (a + step_row) * cols_n + b + step_col))
+        return lax.ppermute(source, ("prow", "pcol"), pairs)
+
+    halos = (
+        line(row_last, "prow", rows_n, 1),
+        line(row_first, "prow", rows_n, -1),
+        line(col_last, "pcol", cols_n, 1),
+        line(col_first, "pcol", cols_n, -1),
+        diagonal(col_last, 1, 1),
+        diagonal(col_first, 1, -1),
+        diagonal(col_last, -1, 1),
+        diagonal(col_first, -1, -1),
+    )
     sides = margin_sides[0, 0].astype(jnp.float32)
-    smoothed = smoother(sides, loads, modulus, row_lo, row_hi, col_lo, col_hi)
+    smoothed = smoother(sides, loads, modulus, halos)
 
     solved = jnp.dot(coarse_inverse[0], restricted, precision=lax.Precision.HIGHEST)
     lifted = lax.dot_general(
-        solved, flat_vectors, (((0,), (0,)), ((), ())), precision=lax.Precision.HIGHEST
-    )
-    return smoothed.reshape(right_sides.shape) + lifted.reshape(right_sides.shape)
+        solved, coarse_vectors, (((0,), (0,)), ((), ())), precision=lax.Precision.HIGHEST
+    )
+    return smoothed.reshape(right_sides.shape) + lifted
 
 
 def solution(mesh):

time: 77.8 us -> 69.3 us (0.89)
  local copies, waits for them, and re-layouts: 22.2 us -> 3.12 us
  starting transfers between devices: 22.3 us -> 33.7 us
  other arithmetic: 4.29 us -> 0.55 us
  Pallas kernels: 10.8 us -> 13.5 us
    slice x8 -> x0, local copies, waits for them, and re-layouts: 9.2 us -> none  [the longest x2 1.84 us: per_device(): row_hi[:, :, None, 0]]
    ppermute x4, starting transfers between devices: 8.56 us -> 17.8 us  [butterfly_sum(): x = x + lax.ppermute(x, axis, pairs)]
    broadcast_in_dim x2 -> x0, local copies, waits for them, and re-layouts: 7.42 us -> none  [the longest x1 4.1 us: per_device(): col_lo = lax.ppermute(last_column, 'pcol', up)[..., None]]
    concatenate x3 -> x0, other arithmetic: 2.95 us -> none  [the longest x1 2.29 us: per_device(): stacked = jnp.concatenate([loads, modulus[None]], axis=0)]
    pallas_call x0 -> x1, Pallas kernels: none -> 2.74 us  [pack(): pl.pallas_call(pack_kernel, out_shape=[jax.ShapeDtypeStruct((count, cols)...]
    ppermute x4 -> x8, starting transfers between devices: 13.7 us -> 15.9 us  [the longest x4 10.3 us: line(): return lax.ppermute(source, axis, pairs)]
    reshape x1 -> x0, local copies, waits for them, and re-layouts: 1.7 us -> none  [per_device(): right_sides.reshape(load_count * 3, plane_count, row_count, column_count)]
    ppermute x4 -> x8, waiting for transfers between devices: 2.94 us -> 4.27 us  [the longest x4 3.05 us: line(): return lax.ppermute(source, axis, pairs)]
  transfers between devices with their start and end apart: 8 -> 12, of which waited for: 2 -> 3; matrix products, arithmetic and copies ran while one was open for 28% -> 1% of each run, Pallas kernels for 0% -> 4%
where the time goes in v3:
time: 69.3 us; the launch traced here: 68.5 us
  starting transfers between devices  33.7 us (49%)
  Pallas kernels  13.5 us (19%)
  matrix products  12.2 us (18%)
  waiting for transfers between devices  5.36 us (8%)
  local copies, waits for them, and re-layouts  3.12 us (5%)
    ppermute x4, starting transfers between devices, butterfly_sum(): x = x + lax.ppermute(x, axis, pairs)  17.8 us
    pallas_call x1, Pallas kernels, smoother(): pl.pallas_call(smoother_kernel, out_shape=jax.ShapeDtypeStruct(loads.shap...  10.7 us
    ppermute x4, starting transfers between devices, line(): return lax.ppermute(source, axis, pairs)  10.3 us
    dot_general x1, matrix products, per_device(): lax.dot_general(coarse_vectors, right_sides, ((cell_dims, cell_dims), (()...  6.86 us
    ppermute x4, starting transfers between devices, diagonal(): return lax.ppermute(source, ('prow', 'pcol'), pairs)  5.6 us
    dot_general x1, matrix products, per_device(): lax.dot_general(solved, coarse_vectors, (((0,), (0,)), ((), ())), precisi...  5.15 us
    ppermute x4, waiting for transfers between devices, line(): return lax.ppermute(source, axis, pairs)  3.05 us
    pallas_call x1, Pallas kernels, pack(): pl.pallas_call(pack_kernel, out_shape=[jax.ShapeDtypeStruct((count, cols)...  2.74 us
  transfers between devices with their start and end apart: 12, of which 3 were waited for; matrix products, arithmetic and copies ran while one was open for 1% of the time, Pallas kernels for 4%

profile of v3, /device:TPU:1, one launch (start us, length us, event | category | flops | bytes accessed | tf_op | source)
XLA Modules:
  0.0 68.5 jit_solution(11623065242566955018)
XLA Ops:
  0.0 0.0 copy-start
  0.0 6.9 %fusion.5 = f32[64,24]{0,1:T(8,128)S(1)} fusion(f32[24,3,4,8,128]{4,3,2,1,0:T(8,128)} %param.5, f32[64,3,4,8,128]{4,3,2,1,0:T(8,128)} %param.8), kind=kOutput, calls=%fused_computation.6 | convolution fusion | flops 226492416 | bytes 4331520 | tf_op jit(solution)/shard_map/dot_general | solution.py:271
  6.9 0.0 copy-start.10
  6.9 2.1 %collective-permute-start.8 = (f32[64,24]{0,1:T(8,128)S(1)}, f32[64,24]{0,1:T(8,128)S(1)}, u32[]{:S(2)}, u32[]{:S(2)}) collective-permute-start(f32[64,24]{0,1:T(8,128)S(1)} %fusion.5), channel_id=1, source_target_pairs={{0,8},{8,0},{16,24},{24,16},{32,40},{40,32},{48,56},{56,48},{64,72... | collective-permute-start | bytes 18440 | tf_op jit(solution)/shard_map/ppermute | solution.py:28
  9.0 1.1 %collective-permute-done.8 = f32[64,24]{0,1:T(8,128)S(1)} collective-permute-done((f32[64,24]{0,1:T(8,128)S(1)}, f32[64,24]{0,1:T(8,128)S(1)}, u32[]{:S(2)}, u32[]{:S(2)}) %collective-permute-start.8) | collective-permute-done | bytes 6176 | tf_op jit(solution)/shard_map/ppermute | solution.py:28
  10.1 3.0 %collective-permute-start.9 = (f32[64,24]{0,1:T(8,128)S(1)}, f32[64,24]{0,1:T(8,128)S(1)}, u32[]{:S(2)}, u32[]{:S(2)}) collective-permute-start(f32[64,24]{0,1:T(8,128)S(1)} %add.15), channel_id=1, source_target_pairs={{0,16},{8,24},{16,0},{24,8},{32,48},{40,56},{48,32},{56,40},{64,80... | collective-permute-start | bytes 18440 | tf_op jit(solution)/shard_map/ppermute | solution.py:28
  13.1 0.0 copy-start.1
  13.1 2.7 %shard_map.55 = (f32[292,128]{1,0:T(8,128)}, f32[292,128]{1,0:T(8,128)}, f32[8,384]{1,0:T(8,128)}, f32[8,384]{1,0:T(8,128)}) custom-call(f32[72,4,8,128]{3,2,1,0:T(8,128)} %bitcast.16, f32[4,8,128]{2,1,0:T(8,128)} %mod_ref.3), custom_call_target="tpu_custom_call" | custom-call | tf_op jit(solution)/shard_map/pallas_call | solution.py:77
  15.8 1.3 %collective-permute-start.6 = (f32[8,384]{1,0:T(8,128)}, f32[8,384]{1,0:T(8,128)S(1)}, u32[]{:S(2)}, u32[]{:S(2)}) collective-permute-start(f32[8,384]{1,0:T(8,128)} %get-tuple-element.11), channel_id=1, source_target_pairs={{8,1},{9,2},{10,3},{11,4},{12,5},{13,6},{14,7},{16,9},{17,10},{18,... | collective-permute-start | bytes 36872 | tf_op jit(solution)/shard_map/ppermute | solution.py:291
  17.1 0.0 collective-permute-done.9
  17.1 6.1 %collective-permute-start.10 = (f32[64,24]{0,1:T(8,128)S(1)}, f32[64,24]{0,1:T(8,128)S(1)}, u32[]{:S(2)}, u32[]{:S(2)}) collective-permute-start(f32[64,24]{0,1:T(8,128)S(1)} %add.16), channel_id=1, source_target_pairs={{0,32},{8,40},{16,48},{24,56},{32,0},{40,8},{48,16},{56,24},{64,96... | collective-permute-start | bytes 18440 | tf_op jit(solution)/shard_map/ppermute | solution.py:28
  23.2 1.8 %collective-permute-start.4 = (f32[8,384]{1,0:T(8,128)}, f32[8,384]{1,0:T(8,128)S(1)}, u32[]{:S(2)}, u32[]{:S(2)}) collective-permute-start(f32[8,384]{1,0:T(8,128)} %get-tuple-element.11), channel_id=1, source_target_pairs={{0,9},{1,10},{2,11},{3,12},{4,13},{5,14},{6,15},{8,17},{9,18},{10,... | collective-permute-start | bytes 36872 | tf_op jit(solution)/shard_map/ppermute | solution.py:291
  25.0 4.7 %collective-permute-start.2 = (f32[8,384]{1,0:T(8,128)}, f32[8,384]{1,0:T(8,128)S(1)}, u32[]{:S(2)}, u32[]{:S(2)}) collective-permute-start(f32[8,384]{1,0:T(8,128)} %get-tuple-element.11), channel_id=1, source_target_pairs={{0,1},{1,2},{2,3},{3,4},{4,5},{5,6},{6,7},{8,9},{9,10},{10,11},{11... | collective-permute-start | bytes 36872 | tf_op jit(solution)/shard_map/ppermute | solution.py:283
  29.7 2.2 %collective-permute-start = (f32[292,128]{1,0:T(8,128)}, f32[292,128]{1,0:T(8,128)S(1)}, u32[]{:S(2)}, u32[]{:S(2)}) collective-permute-start(f32[292,128]{1,0:T(8,128)} %get-tuple-element.9), channel_id=1, source_target_pairs={{0,8},{8,16},{16,24},{24,32},{32,40},{40,48},{48,56},{56,64},{64,7... | collective-permute-start | bytes 448520 | tf_op jit(solution)/shard_map/ppermute | solution.py:283
  31.9 0.0 collective-permute-done.10
  31.9 1.3 %collective-permute-start.1 = (f32[292,128]{1,0:T(8,128)}, f32[292,128]{1,0:T(8,128)S(1)}, u32[]{:S(2)}, u32[]{:S(2)}) collective-permute-start(f32[292,128]{1,0:T(8,128)} %get-tuple-element.10), channel_id=1, source_target_pairs={{8,0},{16,8},{24,16},{32,24},{40,32},{48,40},{56,48},{64,56},{72,6... | collective-permute-start | bytes 448520 | tf_op jit(solution)/shard_map/ppermute | solution.py:283
  33.2 0.0 collective-permute-done.6.chl_ref
  33.2 0.0 copy-start.4
  33.3 6.6 %collective-permute-start.11 = (f32[64,24]{0,1:T(8,128)S(1)}, f32[64,24]{0,1:T(8,128)S(1)}, u32[]{:S(2)}, u32[]{:S(2)}) collective-permute-start(f32[64,24]{0,1:T(8,128)S(1)} %add.17), channel_id=1, source_target_pairs={{0,64},{8,72},{16,80},{24,88},{32,96},{40,104},{48,112},{56,120},{... | collective-permute-start | bytes 18440 | tf_op jit(solution)/shard_map/ppermute | solution.py:28
  39.8 0.0 copy-done.10
  39.8 0.5 convert_bitcast_fusion.sides_ref
  40.4 0.0 collective-permute-done.4.cll_ref
  40.4 0.0 copy-start.5
  40.4 1.3 %collective-permute-start.7 = (f32[8,384]{1,0:T(8,128)}, f32[8,384]{1,0:T(8,128)S(1)}, u32[]{:S(2)}, u32[]{:S(2)}) collective-permute-start(f32[8,384]{1,0:T(8,128)} %get-tuple-element.12), channel_id=1, source_target_pairs={{9,0},{10,1},{11,2},{12,3},{13,4},{14,5},{15,6},{17,8},{18,9},{19,... | collective-permute-start | bytes 36872 | tf_op jit(solution)/shard_map/ppermute | solution.py:291
  41.7 0.0 collective-permute-done.2.clo_ref
  41.7 0.0 copy-start.6
  41.7 1.3 %collective-permute-start.5 = (f32[8,384]{1,0:T(8,128)}, f32[8,384]{1,0:T(8,128)S(1)}, u32[]{:S(2)}, u32[]{:S(2)}) collective-permute-start(f32[8,384]{1,0:T(8,128)} %get-tuple-element.12), channel_id=1, source_target_pairs={{1,8},{2,9},{3,10},{4,11},{5,12},{6,13},{7,14},{9,16},{10,17},{11,... | collective-permute-start | bytes 36872 | tf_op jit(solution)/shard_map/ppermute | solution.py:291
  43.0 0.0 collective-permute-done.11
  43.0 2.1 %collective-permute-start.3 = (f32[8,384]{1,0:T(8,128)}, f32[8,384]{1,0:T(8,128)S(1)}, u32[]{:S(2)}, u32[]{:S(2)}) collective-permute-start(f32[8,384]{1,0:T(8,128)} %get-tuple-element.12), channel_id=1, source_target_pairs={{1,0},{2,1},{3,2},{4,3},{5,4},{6,5},{7,6},{9,8},{10,9},{11,10},{12... | collective-permute-start | bytes 36872 | tf_op jit(solution)/shard_map/ppermute | solution.py:283
  45.1 0.0 copy-done
  45.1 0.2 convolution_bitcast_fusion
  45.3 1.2 %collective-permute-done.7.chh_ref = f32[8,384]{1,0:T(8,128)S(1)} collective-permute-done((f32[8,384]{1,0:T(8,128)}, f32[8,384]{1,0:T(8,128)S(1)}, u32[]{:S(2)}, u32[]{:S(2)}) %collective-permute-start.7) | collective-permute-done | bytes 12320 | tf_op jit(solution)/shard_map/ppermute | solution.py:291
  46.5 0.0 copy-start.7
  46.5 0.0 collective-permute-done.5.clh_ref
  46.5 0.0 copy-start.8
  46.5 3.0 %collective-permute-done.3.chi_ref = f32[8,384]{1,0:T(8,128)S(1)} collective-permute-done((f32[8,384]{1,0:T(8,128)}, f32[8,384]{1,0:T(8,128)S(1)}, u32[]{:S(2)}, u32[]{:S(2)}) %collective-permute-start.3) | collective-permute-done | bytes 12320 | tf_op jit(solution)/shard_map/ppermute | solution.py:283
  49.5 0.0 copy-start.9
  49.5 0.0 collective-permute-done.rlo_ref
  49.5 0.6 copy-done.9
  50.1 0.0 copy-start.2
  50.1 0.0 collective-permute-done.1.rhi_ref
  50.1 0.0 copy-done.4
  50.1 0.0 copy-done.5
  50.1 0.0 copy-done.6
  50.2 0.0 copy-done.7
  50.2 0.0 copy-done.8
  50.2 0.6 copy-done.2
  50.8 0.0 copy-start.3
  50.8 0.7 copy-done.3
  51.4 10.7 %shard_map.56 = f32[72,4,8,128]{3,2,1,0:T(8,128)} custom-call(f32[4]{0:T(128)} %convert_bitcast_fusion.sides_ref, f32[72,4,8,128]{3,2,1,0:T(8,128)} %bitcast.17, f32[4,8,128]{2,1,0:T(8,128)} %mod_ref.3, f32[292,128]{1,0:T(8,128)} %copy-done.2, f32[292,128]{1,0:T(8,128)} %copy-done.3, f32[8,384]{1,0:T(8,128)} %copy-done.6, f32[8,384]{1,0:T(8,128)} %copy-done.9, ...), custom_call_target="tpu_custom_call" | custom-call | tf_op jit(solution)/shard_map/pallas_call | solution.py:249
  62.1 0.0 copy-done.1
  62.2 5.1 %copy_add_fusion = f32[24,3,4,8,128]{4,0,3,2,1:T(8,128)S(1)} fusion(f32[24,3,4,8,128]{4,3,2,1,0:T(8,128)} %bitcast.18, f32[24,64,1,1,1]{1,0,4,3,2:T(8,128)S(1)} %convolution_bitcast_fusion, f32[64,3,4,8,128]{4,3,2,1,0:T(8,128)S(1)} %copy-done.1), kind=kOutput, calls=%fused_computation.4 | convolution fusion | flops 226787328 | bytes 5511168 | tf_op jit(solution)/shard_map/dot_general | solution.py:307
  67.3 1.2 %copy.10 = f32[24,3,4,8,128]{4,3,2,1,0:T(8,128)} copy(f32[24,3,4,8,128]{4,0,3,2,1:T(8,128)S(1)} %copy_add_fusion) | data formatting | bytes 2359296 | tf_op jit(solution)/shard_map/add | solution.py:310
  (3 shorter events, 0.0 us)
Async XLA Ops:
  0.0 45.1 %copy-start = (f32[1,64,64]{2,1,0:T(8,128)S(1)}, f32[1,64,64]{2,1,0:T(8,128)}, u32[]{:S(2)}) copy-start(f32[1,64,64]{2,1,0:T(8,128)} %param.9) | copy-start | bytes 49156
  6.9 33.0 %copy-start.10 = (s32[1,1,4]{2,1,0:T(1,128)S(1)}, s32[1,1,4]{2,1,0:T(1,128)}, u32[]{:S(2)}) copy-start(s32[1,1,4]{2,1,0:T(1,128)} %param.7) | copy-start | bytes 52
  6.9 3.2 %collective-permute-start.8 = (f32[64,24]{0,1:T(8,128)S(1)}, f32[64,24]{0,1:T(8,128)S(1)}, u32[]{:S(2)}, u32[]{:S(2)}) collective-permute-start(f32[64,24]{0,1:T(8,128)S(1)} %fusion.5), channel_id=1, source_target_pairs={{0,8},{8,0},{16,24},{24,16},{32,40},{40,32},{48,56},{56,48},{64,72... | collective-permute-start | bytes 18440 | tf_op jit(solution)/shard_map/ppermute | solution.py:28
  10.1 7.0 %collective-permute-start.9 = (f32[64,24]{0,1:T(8,128)S(1)}, f32[64,24]{0,1:T(8,128)S(1)}, u32[]{:S(2)}, u32[]{:S(2)}) collective-permute-start(f32[64,24]{0,1:T(8,128)S(1)} %add.15), channel_id=1, source_target_pairs={{0,16},{8,24},{16,0},{24,8},{32,48},{40,56},{48,32},{56,40},{64,80... | collective-permute-start | bytes 18440 | tf_op jit(solution)/shard_map/ppermute | solution.py:28
  13.1 49.1 %copy-start.1 = (f32[64,3,4,8,128]{4,3,2,1,0:T(8,128)S(1)}, f32[64,3,4,8,128]{4,3,2,1,0:T(8,128)}, u32[]{:S(2)}) copy-start(f32[64,3,4,8,128]{4,3,2,1,0:T(8,128)} %param.8) | copy-start | bytes 9437188
  15.8 17.4 %collective-permute-start.6 = (f32[8,384]{1,0:T(8,128)}, f32[8,384]{1,0:T(8,128)S(1)}, u32[]{:S(2)}, u32[]{:S(2)}) collective-permute-start(f32[8,384]{1,0:T(8,128)} %get-tuple-element.11), channel_id=1, source_target_pairs={{8,1},{9,2},{10,3},{11,4},{12,5},{13,6},{14,7},{16,9},{17,10},{18,... | collective-permute-start | bytes 36872 | tf_op jit(solution)/shard_map/ppermute | solution.py:291
  17.1 14.8 %collective-permute-start.10 = (f32[64,24]{0,1:T(8,128)S(1)}, f32[64,24]{0,1:T(8,128)S(1)}, u32[]{:S(2)}, u32[]{:S(2)}) collective-permute-start(f32[64,24]{0,1:T(8,128)S(1)} %add.16), channel_id=1, source_target_pairs={{0,32},{8,40},{16,48},{24,56},{32,0},{40,8},{48,16},{56,24},{64,96... | collective-permute-start | bytes 18440 | tf_op jit(solution)/shard_map/ppermute | solution.py:28
  23.2 17.1 %collective-permute-start.4 = (f32[8,384]{1,0:T(8,128)}, f32[8,384]{1,0:T(8,128)S(1)}, u32[]{:S(2)}, u32[]{:S(2)}) collective-permute-start(f32[8,384]{1,0:T(8,128)} %get-tuple-element.11), channel_id=1, source_target_pairs={{0,9},{1,10},{2,11},{3,12},{4,13},{5,14},{6,15},{8,17},{9,18},{10,... | collective-permute-start | bytes 36872 | tf_op jit(solution)/shard_map/ppermute | solution.py:291
  25.0 16.7 %collective-permute-start.2 = (f32[8,384]{1,0:T(8,128)}, f32[8,384]{1,0:T(8,128)S(1)}, u32[]{:S(2)}, u32[]{:S(2)}) collective-permute-start(f32[8,384]{1,0:T(8,128)} %get-tuple-element.11), channel_id=1, source_target_pairs={{0,1},{1,2},{2,3},{3,4},{4,5},{5,6},{6,7},{8,9},{9,10},{10,11},{11... | collective-permute-start | bytes 36872 | tf_op jit(solution)/shard_map/ppermute | solution.py:283
  29.7 19.9 %collective-permute-start = (f32[292,128]{1,0:T(8,128)}, f32[292,128]{1,0:T(8,128)S(1)}, u32[]{:S(2)}, u32[]{:S(2)}) collective-permute-start(f32[292,128]{1,0:T(8,128)} %get-tuple-element.9), channel_id=1, source_target_pairs={{0,8},{8,16},{16,24},{24,32},{32,40},{40,48},{48,56},{56,64},{64,7... | collective-permute-start | bytes 448520 | tf_op jit(solution)/shard_map/ppermute | solution.py:283
  31.9 18.2 %collective-permute-start.1 = (f32[292,128]{1,0:T(8,128)}, f32[292,128]{1,0:T(8,128)S(1)}, u32[]{:S(2)}, u32[]{:S(2)}) collective-permute-start(f32[292,128]{1,0:T(8,128)} %get-tuple-element.10), channel_id=1, source_target_pairs={{8,0},{16,8},{24,16},{32,24},{40,32},{48,40},{56,48},{64,56},{72,6... | collective-permute-start | bytes 448520 | tf_op jit(solution)/shard_map/ppermute | solution.py:283
  33.2 16.9 %copy-start.4 = (f32[8,384]{1,0:T(8,128)}, f32[8,384]{1,0:T(8,128)S(1)}, u32[]{:S(2)}) copy-start(f32[8,384]{1,0:T(8,128)S(1)} %collective-permute-done.6.chl_ref) | copy-start | bytes 36868
  33.3 9.7 %collective-permute-start.11 = (f32[64,24]{0,1:T(8,128)S(1)}, f32[64,24]{0,1:T(8,128)S(1)}, u32[]{:S(2)}, u32[]{:S(2)}) collective-permute-start(f32[64,24]{0,1:T(8,128)S(1)} %add.17), channel_id=1, source_target_pairs={{0,64},{8,72},{16,80},{24,88},{32,96},{40,104},{48,112},{56,120},{... | collective-permute-start | bytes 18440 | tf_op jit(solution)/shard_map/ppermute | solution.py:28
  40.4 9.8 %copy-start.5 = (f32[8,384]{1,0:T(8,128)}, f32[8,384]{1,0:T(8,128)S(1)}, u32[]{:S(2)}) copy-start(f32[8,384]{1,0:T(8,128)S(1)} %collective-permute-done.4.cll_ref) | copy-start | bytes 36868
  40.4 6.1 %collective-permute-start.7 = (f32[8,384]{1,0:T(8,128)}, f32[8,384]{1,0:T(8,128)S(1)}, u32[]{:S(2)}, u32[]{:S(2)}) collective-permute-start(f32[8,384]{1,0:T(8,128)} %get-tuple-element.12), channel_id=1, source_target_pairs={{9,0},{10,1},{11,2},{12,3},{13,4},{14,5},{15,6},{17,8},{18,9},{19,... | collective-permute-start | bytes 36872 | tf_op jit(solution)/shard_map/ppermute | solution.py:291
  41.7 8.5 %copy-start.6 = (f32[8,384]{1,0:T(8,128)}, f32[8,384]{1,0:T(8,128)S(1)}, u32[]{:S(2)}) copy-start(f32[8,384]{1,0:T(8,128)S(1)} %collective-permute-done.2.clo_ref) | copy-start | bytes 36868
  41.7 4.8 %collective-permute-start.5 = (f32[8,384]{1,0:T(8,128)}, f32[8,384]{1,0:T(8,128)S(1)}, u32[]{:S(2)}, u32[]{:S(2)}) collective-permute-start(f32[8,384]{1,0:T(8,128)} %get-tuple-element.12), channel_id=1, source_target_pairs={{1,8},{2,9},{3,10},{4,11},{5,12},{6,13},{7,14},{9,16},{10,17},{11,... | collective-permute-start | bytes 36872 | tf_op jit(solution)/shard_map/ppermute | solution.py:291
  43.0 6.5 %collective-permute-start.3 = (f32[8,384]{1,0:T(8,128)}, f32[8,384]{1,0:T(8,128)S(1)}, u32[]{:S(2)}, u32[]{:S(2)}) collective-permute-start(f32[8,384]{1,0:T(8,128)} %get-tuple-element.12), channel_id=1, source_target_pairs={{1,0},{2,1},{3,2},{4,3},{5,4},{6,5},{7,6},{9,8},{10,9},{11,10},{12... | collective-permute-start | bytes 36872 | tf_op jit(solution)/shard_map/ppermute | solution.py:283
  46.5 3.7 %copy-start.7 = (f32[8,384]{1,0:T(8,128)}, f32[8,384]{1,0:T(8,128)S(1)}, u32[]{:S(2)}) copy-start(f32[8,384]{1,0:T(8,128)S(1)} %collective-permute-done.7.chh_ref) | copy-start | bytes 36868
  46.5 3.7 %copy-start.8 = (f32[8,384]{1,0:T(8,128)}, f32[8,384]{1,0:T(8,128)S(1)}, u32[]{:S(2)}) copy-start(f32[8,384]{1,0:T(8,128)S(1)} %collective-permute-done.5.clh_ref) | copy-start | bytes 36868
  49.5 0.6 copy-start.9
  50.1 0.7 copy-start.2
  50.8 0.7 copy-start.3

commit v4 on v3

--- a/solution.py
+++ b/solution.py
@@ -269,7 +269,7 @@
     column_count = right_sides.shape[4]
     cell_dims = (1, 2, 3, 4)
     partial_terms = lax.dot_general(
-        coarse_vectors, right_sides, ((cell_dims, cell_dims), ((), ())), precision=lax.Precision.HIGHEST
+        coarse_vectors, right_sides, ((cell_dims, cell_dims), ((), ())), precision=lax.Precision.HIGH
     )
     restricted = butterfly_sum(partial_terms, "prow")
 
@@ -305,7 +305,7 @@
 
     solved = jnp.dot(coarse_inverse[0], restricted, precision=lax.Precision.HIGHEST)
     lifted = lax.dot_general(
-        solved, coarse_vectors, (((0,), (0,)), ((), ())), precision=lax.Precision.HIGHEST
+        solved, coarse_vectors, (((0,), (0,)), ((), ())), precision=lax.Precision.HIGH
     )
     return smoothed.reshape(right_sides.shape) + lifted
 

time: 69.3 us -> 67.3 us (0.971)
  matrix products: 12.2 us -> 10.2 us
    dot_general x1, matrix products: 6.86 us -> 5.7 us  [per_device(): lax.dot_general(coarse_vectors, right_sides, ((cell_dims, cell_dims), (()...]
    dot_general x1, matrix products: 5.15 us -> 4.34 us  [per_device(): lax.dot_general(solved, coarse_vectors, (((0,), (0,)), ((), ())), precisi...]
where the time goes in v4:
time: 67.3 us; the launch traced here: 66.6 us
  starting transfers between devices  33.5 us (50%)
  Pallas kernels  13.5 us (20%)
  matrix products  10.2 us (15%)
  waiting for transfers between devices  5.54 us (8%)
  local copies, waits for them, and re-layouts  3.12 us (5%)
    ppermute x4, starting transfers between devices, butterfly_sum(): x = x + lax.ppermute(x, axis, pairs)  17.8 us
    pallas_call x1, Pallas kernels, smoother(): pl.pallas_call(smoother_kernel, out_shape=jax.ShapeDtypeStruct(loads.shap...  10.7 us
    ppermute x4, starting transfers between devices, line(): return lax.ppermute(source, axis, pairs)  10.1 us
    dot_general x1, matrix products, per_device(): lax.dot_general(coarse_vectors, right_sides, ((cell_dims, cell_dims), (()...  5.7 us
    ppermute x4, starting transfers between devices, diagonal(): return lax.ppermute(source, ('prow', 'pcol'), pairs)  5.6 us
    dot_general x1, matrix products, per_device(): lax.dot_general(solved, coarse_vectors, (((0,), (0,)), ((), ())), precisi...  4.34 us
    ppermute x4, waiting for transfers between devices, line(): return lax.ppermute(source, axis, pairs)  3.05 us
    pallas_call x1, Pallas kernels, pack(): pl.pallas_call(pack_kernel, out_shape=[jax.ShapeDtypeStruct((count, cols)...  2.74 us
  transfers between devices with their start and end apart: 12, of which 3 were waited for; matrix products, arithmetic and copies ran while one was open for 1% of the time, Pallas kernels for 4%

profile of v4, /device:TPU:1, one launch (start us, length us, event | category | flops | bytes accessed | tf_op | source)
XLA Modules:
  0.0 66.6 jit_solution(10318346163349009983)
XLA Ops:
  0.0 0.0 copy-start
  0.0 5.7 %fusion.5 = f32[64,24]{0,1:T(8,128)S(1)} fusion(f32[24,3,4,8,128]{4,3,2,1,0:T(8,128)} %param.5, f32[64,3,4,8,128]{4,3,2,1,0:T(8,128)} %param.8), kind=kOutput, calls=%fused_computation.6 | convolution fusion | flops 113246208 | bytes 4331520 | tf_op jit(solution)/shard_map/dot_general | solution.py:271
  5.7 0.0 copy-start.10
  5.7 2.1 %collective-permute-start.8 = (f32[64,24]{0,1:T(8,128)S(1)}, f32[64,24]{0,1:T(8,128)S(1)}, u32[]{:S(2)}, u32[]{:S(2)}) collective-permute-start(f32[64,24]{0,1:T(8,128)S(1)} %fusion.5), channel_id=1, source_target_pairs={{0,8},{8,0},{16,24},{24,16},{32,40},{40,32},{48,56},{56,48},{64,72... | collective-permute-start | bytes 18440 | tf_op jit(solution)/shard_map/ppermute | solution.py:28
  7.8 1.1 %collective-permute-done.8 = f32[64,24]{0,1:T(8,128)S(1)} collective-permute-done((f32[64,24]{0,1:T(8,128)S(1)}, f32[64,24]{0,1:T(8,128)S(1)}, u32[]{:S(2)}, u32[]{:S(2)}) %collective-permute-start.8) | collective-permute-done | bytes 6176 | tf_op jit(solution)/shard_map/ppermute | solution.py:28
  8.9 3.0 %collective-permute-start.9 = (f32[64,24]{0,1:T(8,128)S(1)}, f32[64,24]{0,1:T(8,128)S(1)}, u32[]{:S(2)}, u32[]{:S(2)}) collective-permute-start(f32[64,24]{0,1:T(8,128)S(1)} %add.15), channel_id=1, source_target_pairs={{0,16},{8,24},{16,0},{24,8},{32,48},{40,56},{48,32},{56,40},{64,80... | collective-permute-start | bytes 18440 | tf_op jit(solution)/shard_map/ppermute | solution.py:28
  11.9 0.0 copy-start.1
  11.9 2.7 %shard_map.55 = (f32[292,128]{1,0:T(8,128)}, f32[292,128]{1,0:T(8,128)}, f32[8,384]{1,0:T(8,128)}, f32[8,384]{1,0:T(8,128)}) custom-call(f32[72,4,8,128]{3,2,1,0:T(8,128)} %bitcast.16, f32[4,8,128]{2,1,0:T(8,128)} %mod_ref.3), custom_call_target="tpu_custom_call" | custom-call | tf_op jit(solution)/shard_map/pallas_call | solution.py:77
  14.7 1.3 %collective-permute-start.6 = (f32[8,384]{1,0:T(8,128)}, f32[8,384]{1,0:T(8,128)S(1)}, u32[]{:S(2)}, u32[]{:S(2)}) collective-permute-start(f32[8,384]{1,0:T(8,128)} %get-tuple-element.11), channel_id=1, source_target_pairs={{8,1},{9,2},{10,3},{11,4},{12,5},{13,6},{14,7},{16,9},{17,10},{18,... | collective-permute-start | bytes 36872 | tf_op jit(solution)/shard_map/ppermute | solution.py:291
  16.0 0.0 collective-permute-done.9
  16.0 6.1 %collective-permute-start.10 = (f32[64,24]{0,1:T(8,128)S(1)}, f32[64,24]{0,1:T(8,128)S(1)}, u32[]{:S(2)}, u32[]{:S(2)}) collective-permute-start(f32[64,24]{0,1:T(8,128)S(1)} %add.16), channel_id=1, source_target_pairs={{0,32},{8,40},{16,48},{24,56},{32,0},{40,8},{48,16},{56,24},{64,96... | collective-permute-start | bytes 18440 | tf_op jit(solution)/shard_map/ppermute | solution.py:28
  22.1 1.8 %collective-permute-start.4 = (f32[8,384]{1,0:T(8,128)}, f32[8,384]{1,0:T(8,128)S(1)}, u32[]{:S(2)}, u32[]{:S(2)}) collective-permute-start(f32[8,384]{1,0:T(8,128)} %get-tuple-element.11), channel_id=1, source_target_pairs={{0,9},{1,10},{2,11},{3,12},{4,13},{5,14},{6,15},{8,17},{9,18},{10,... | collective-permute-start | bytes 36872 | tf_op jit(solution)/shard_map/ppermute | solution.py:291
  23.8 4.7 %collective-permute-start.2 = (f32[8,384]{1,0:T(8,128)}, f32[8,384]{1,0:T(8,128)S(1)}, u32[]{:S(2)}, u32[]{:S(2)}) collective-permute-start(f32[8,384]{1,0:T(8,128)} %get-tuple-element.11), channel_id=1, source_target_pairs={{0,1},{1,2},{2,3},{3,4},{4,5},{5,6},{6,7},{8,9},{9,10},{10,11},{11... | collective-permute-start | bytes 36872 | tf_op jit(solution)/shard_map/ppermute | solution.py:283
  28.5 2.2 %collective-permute-start = (f32[292,128]{1,0:T(8,128)}, f32[292,128]{1,0:T(8,128)S(1)}, u32[]{:S(2)}, u32[]{:S(2)}) collective-permute-start(f32[292,128]{1,0:T(8,128)} %get-tuple-element.9), channel_id=1, source_target_pairs={{0,8},{8,16},{16,24},{24,32},{32,40},{40,48},{48,56},{56,64},{64,7... | collective-permute-start | bytes 448520 | tf_op jit(solution)/shard_map/ppermute | solution.py:283
  30.8 0.0 collective-permute-done.10
  30.8 1.3 %collective-permute-start.1 = (f32[292,128]{1,0:T(8,128)}, f32[292,128]{1,0:T(8,128)S(1)}, u32[]{:S(2)}, u32[]{:S(2)}) collective-permute-start(f32[292,128]{1,0:T(8,128)} %get-tuple-element.10), channel_id=1, source_target_pairs={{8,0},{16,8},{24,16},{32,24},{40,32},{48,40},{56,48},{64,56},{72,6... | collective-permute-start | bytes 448520 | tf_op jit(solution)/shard_map/ppermute | solution.py:283
  32.1 0.0 collective-permute-done.6.chl_ref
  32.1 0.0 copy-start.4
  32.1 6.6 %collective-permute-start.11 = (f32[64,24]{0,1:T(8,128)S(1)}, f32[64,24]{0,1:T(8,128)S(1)}, u32[]{:S(2)}, u32[]{:S(2)}) collective-permute-start(f32[64,24]{0,1:T(8,128)S(1)} %add.17), channel_id=1, source_target_pairs={{0,64},{8,72},{16,80},{24,88},{32,96},{40,104},{48,112},{56,120},{... | collective-permute-start | bytes 18440 | tf_op jit(solution)/shard_map/ppermute | solution.py:28
  38.7 0.0 copy-done.10
  38.7 0.5 convert_bitcast_fusion.sides_ref
  39.2 0.0 collective-permute-done.4.cll_ref
  39.2 0.0 copy-start.5
  39.2 1.3 %collective-permute-start.7 = (f32[8,384]{1,0:T(8,128)}, f32[8,384]{1,0:T(8,128)S(1)}, u32[]{:S(2)}, u32[]{:S(2)}) collective-permute-start(f32[8,384]{1,0:T(8,128)} %get-tuple-element.12), channel_id=1, source_target_pairs={{9,0},{10,1},{11,2},{12,3},{13,4},{14,5},{15,6},{17,8},{18,9},{19,... | collective-permute-start | bytes 36872 | tf_op jit(solution)/shard_map/ppermute | solution.py:291
  40.5 0.0 collective-permute-done.2.clo_ref
  40.5 0.0 copy-start.6
  40.5 1.3 %collective-permute-start.5 = (f32[8,384]{1,0:T(8,128)}, f32[8,384]{1,0:T(8,128)S(1)}, u32[]{:S(2)}, u32[]{:S(2)}) collective-permute-start(f32[8,384]{1,0:T(8,128)} %get-tuple-element.12), channel_id=1, source_target_pairs={{1,8},{2,9},{3,10},{4,11},{5,12},{6,13},{7,14},{9,16},{10,17},{11,... | collective-permute-start | bytes 36872 | tf_op jit(solution)/shard_map/ppermute | solution.py:291
  41.8 0.0 collective-permute-done.11
  41.8 1.9 %collective-permute-start.3 = (f32[8,384]{1,0:T(8,128)}, f32[8,384]{1,0:T(8,128)S(1)}, u32[]{:S(2)}, u32[]{:S(2)}) collective-permute-start(f32[8,384]{1,0:T(8,128)} %get-tuple-element.12), channel_id=1, source_target_pairs={{1,0},{2,1},{3,2},{4,3},{5,4},{6,5},{7,6},{9,8},{10,9},{11,10},{12... | collective-permute-start | bytes 36872 | tf_op jit(solution)/shard_map/ppermute | solution.py:283
  43.8 0.0 copy-done
  43.8 0.2 convolution_bitcast_fusion
  43.9 1.4 %collective-permute-done.7.chh_ref = f32[8,384]{1,0:T(8,128)S(1)} collective-permute-done((f32[8,384]{1,0:T(8,128)}, f32[8,384]{1,0:T(8,128)S(1)}, u32[]{:S(2)}, u32[]{:S(2)}) %collective-permute-start.7) | collective-permute-done | bytes 12320 | tf_op jit(solution)/shard_map/ppermute | solution.py:291
  45.3 0.0 copy-start.7
  45.3 0.0 collective-permute-done.5.clh_ref
  45.3 0.0 copy-start.8
  45.3 3.0 %collective-permute-done.3.chi_ref = f32[8,384]{1,0:T(8,128)S(1)} collective-permute-done((f32[8,384]{1,0:T(8,128)}, f32[8,384]{1,0:T(8,128)S(1)}, u32[]{:S(2)}, u32[]{:S(2)}) %collective-permute-start.3) | collective-permute-done | bytes 12320 | tf_op jit(solution)/shard_map/ppermute | solution.py:283
  48.4 0.0 copy-start.9
  48.4 0.0 collective-permute-done.rlo_ref
  48.4 0.6 copy-done.9
  49.0 0.0 copy-start.2
  49.0 0.0 collective-permute-done.1.rhi_ref
  49.0 0.0 copy-done.4
  49.0 0.0 copy-done.5
  49.0 0.0 copy-done.6
  49.0 0.0 copy-done.7
  49.0 0.0 copy-done.8
  49.0 0.6 copy-done.2
  49.6 0.0 copy-start.3
  49.6 0.7 copy-done.3
  50.3 10.7 %shard_map.56 = f32[72,4,8,128]{3,2,1,0:T(8,128)} custom-call(f32[4]{0:T(128)} %convert_bitcast_fusion.sides_ref, f32[72,4,8,128]{3,2,1,0:T(8,128)} %bitcast.17, f32[4,8,128]{2,1,0:T(8,128)} %mod_ref.3, f32[292,128]{1,0:T(8,128)} %copy-done.2, f32[292,128]{1,0:T(8,128)} %copy-done.3, f32[8,384]{1,0:T(8,128)} %copy-done.6, f32[8,384]{1,0:T(8,128)} %copy-done.9, ...), custom_call_target="tpu_custom_call" | custom-call | tf_op jit(solution)/shard_map/pallas_call | solution.py:249
  61.0 0.0 copy-done.1
  61.0 4.3 %copy_add_fusion = f32[24,3,4,8,128]{4,0,3,2,1:T(8,128)S(1)} fusion(f32[24,3,4,8,128]{4,3,2,1,0:T(8,128)} %bitcast.18, f32[24,64,1,1,1]{1,0,4,3,2:T(8,128)S(1)} %convolution_bitcast_fusion, f32[64,3,4,8,128]{4,3,2,1,0:T(8,128)S(1)} %copy-done.1), kind=kOutput, calls=%fused_computation.4 | convolution fusion | flops 113541120 | bytes 5511168 | tf_op jit(solution)/shard_map/dot_general | solution.py:307
  65.3 1.2 %copy.10 = f32[24,3,4,8,128]{4,3,2,1,0:T(8,128)} copy(f32[24,3,4,8,128]{4,0,3,2,1:T(8,128)S(1)} %copy_add_fusion) | data formatting | bytes 2359296 | tf_op jit(solution)/shard_map/add | solution.py:310
  (3 shorter events, 0.0 us)
Async XLA Ops:
  0.0 43.8 %copy-start = (f32[1,64,64]{2,1,0:T(8,128)S(1)}, f32[1,64,64]{2,1,0:T(8,128)}, u32[]{:S(2)}) copy-start(f32[1,64,64]{2,1,0:T(8,128)} %param.9) | copy-start | bytes 49156
  5.7 33.0 %copy-start.10 = (s32[1,1,4]{2,1,0:T(1,128)S(1)}, s32[1,1,4]{2,1,0:T(1,128)}, u32[]{:S(2)}) copy-start(s32[1,1,4]{2,1,0:T(1,128)} %param.7) | copy-start | bytes 52
  5.7 3.2 %collective-permute-start.8 = (f32[64,24]{0,1:T(8,128)S(1)}, f32[64,24]{0,1:T(8,128)S(1)}, u32[]{:S(2)}, u32[]{:S(2)}) collective-permute-start(f32[64,24]{0,1:T(8,128)S(1)} %fusion.5), channel_id=1, source_target_pairs={{0,8},{8,0},{16,24},{24,16},{32,40},{40,32},{48,56},{56,48},{64,72... | collective-permute-start | bytes 18440 | tf_op jit(solution)/shard_map/ppermute | solution.py:28
  8.9 7.0 %collective-permute-start.9 = (f32[64,24]{0,1:T(8,128)S(1)}, f32[64,24]{0,1:T(8,128)S(1)}, u32[]{:S(2)}, u32[]{:S(2)}) collective-permute-start(f32[64,24]{0,1:T(8,128)S(1)} %add.15), channel_id=1, source_target_pairs={{0,16},{8,24},{16,0},{24,8},{32,48},{40,56},{48,32},{56,40},{64,80... | collective-permute-start | bytes 18440 | tf_op jit(solution)/shard_map/ppermute | solution.py:28
  11.9 49.1 %copy-start.1 = (f32[64,3,4,8,128]{4,3,2,1,0:T(8,128)S(1)}, f32[64,3,4,8,128]{4,3,2,1,0:T(8,128)}, u32[]{:S(2)}) copy-start(f32[64,3,4,8,128]{4,3,2,1,0:T(8,128)} %param.8) | copy-start | bytes 9437188
  14.7 17.4 %collective-permute-start.6 = (f32[8,384]{1,0:T(8,128)}, f32[8,384]{1,0:T(8,128)S(1)}, u32[]{:S(2)}, u32[]{:S(2)}) collective-permute-start(f32[8,384]{1,0:T(8,128)} %get-tuple-element.11), channel_id=1, source_target_pairs={{8,1},{9,2},{10,3},{11,4},{12,5},{13,6},{14,7},{16,9},{17,10},{18,... | collective-permute-start | bytes 36872 | tf_op jit(solution)/shard_map/ppermute | solution.py:291
  16.0 14.8 %collective-permute-start.10 = (f32[64,24]{0,1:T(8,128)S(1)}, f32[64,24]{0,1:T(8,128)S(1)}, u32[]{:S(2)}, u32[]{:S(2)}) collective-permute-start(f32[64,24]{0,1:T(8,128)S(1)} %add.16), channel_id=1, source_target_pairs={{0,32},{8,40},{16,48},{24,56},{32,0},{40,8},{48,16},{56,24},{64,96... | collective-permute-start | bytes 18440 | tf_op jit(solution)/shard_map/ppermute | solution.py:28
  22.1 17.1 %collective-permute-start.4 = (f32[8,384]{1,0:T(8,128)}, f32[8,384]{1,0:T(8,128)S(1)}, u32[]{:S(2)}, u32[]{:S(2)}) collective-permute-start(f32[8,384]{1,0:T(8,128)} %get-tuple-element.11), channel_id=1, source_target_pairs={{0,9},{1,10},{2,11},{3,12},{4,13},{5,14},{6,15},{8,17},{9,18},{10,... | collective-permute-start | bytes 36872 | tf_op jit(solution)/shard_map/ppermute | solution.py:291
  23.8 16.7 %collective-permute-start.2 = (f32[8,384]{1,0:T(8,128)}, f32[8,384]{1,0:T(8,128)S(1)}, u32[]{:S(2)}, u32[]{:S(2)}) collective-permute-start(f32[8,384]{1,0:T(8,128)} %get-tuple-element.11), channel_id=1, source_target_pairs={{0,1},{1,2},{2,3},{3,4},{4,5},{5,6},{6,7},{8,9},{9,10},{10,11},{11... | collective-permute-start | bytes 36872 | tf_op jit(solution)/shard_map/ppermute | solution.py:283
  28.5 19.9 %collective-permute-start = (f32[292,128]{1,0:T(8,128)}, f32[292,128]{1,0:T(8,128)S(1)}, u32[]{:S(2)}, u32[]{:S(2)}) collective-permute-start(f32[292,128]{1,0:T(8,128)} %get-tuple-element.9), channel_id=1, source_target_pairs={{0,8},{8,16},{16,24},{24,32},{32,40},{40,48},{48,56},{56,64},{64,7... | collective-permute-start | bytes 448520 | tf_op jit(solution)/shard_map/ppermute | solution.py:283
  30.8 18.2 %collective-permute-start.1 = (f32[292,128]{1,0:T(8,128)}, f32[292,128]{1,0:T(8,128)S(1)}, u32[]{:S(2)}, u32[]{:S(2)}) collective-permute-start(f32[292,128]{1,0:T(8,128)} %get-tuple-element.10), channel_id=1, source_target_pairs={{8,0},{16,8},{24,16},{32,24},{40,32},{48,40},{56,48},{64,56},{72,6... | collective-permute-start | bytes 448520 | tf_op jit(solution)/shard_map/ppermute | solution.py:283
  32.1 16.9 %copy-start.4 = (f32[8,384]{1,0:T(8,128)}, f32[8,384]{1,0:T(8,128)S(1)}, u32[]{:S(2)}) copy-start(f32[8,384]{1,0:T(8,128)S(1)} %collective-permute-done.6.chl_ref) | copy-start | bytes 36868
  32.1 9.7 %collective-permute-start.11 = (f32[64,24]{0,1:T(8,128)S(1)}, f32[64,24]{0,1:T(8,128)S(1)}, u32[]{:S(2)}, u32[]{:S(2)}) collective-permute-start(f32[64,24]{0,1:T(8,128)S(1)} %add.17), channel_id=1, source_target_pairs={{0,64},{8,72},{16,80},{24,88},{32,96},{40,104},{48,112},{56,120},{... | collective-permute-start | bytes 18440 | tf_op jit(solution)/shard_map/ppermute | solution.py:28
  39.2 9.8 %copy-start.5 = (f32[8,384]{1,0:T(8,128)}, f32[8,384]{1,0:T(8,128)S(1)}, u32[]{:S(2)}) copy-start(f32[8,384]{1,0:T(8,128)S(1)} %collective-permute-done.4.cll_ref) | copy-start | bytes 36868
  39.2 6.1 %collective-permute-start.7 = (f32[8,384]{1,0:T(8,128)}, f32[8,384]{1,0:T(8,128)S(1)}, u32[]{:S(2)}, u32[]{:S(2)}) collective-permute-start(f32[8,384]{1,0:T(8,128)} %get-tuple-element.12), channel_id=1, source_target_pairs={{9,0},{10,1},{11,2},{12,3},{13,4},{14,5},{15,6},{17,8},{18,9},{19,... | collective-permute-start | bytes 36872 | tf_op jit(solution)/shard_map/ppermute | solution.py:291
  40.5 8.5 %copy-start.6 = (f32[8,384]{1,0:T(8,128)}, f32[8,384]{1,0:T(8,128)S(1)}, u32[]{:S(2)}) copy-start(f32[8,384]{1,0:T(8,128)S(1)} %collective-permute-done.2.clo_ref) | copy-start | bytes 36868
  40.5 4.8 %collective-permute-start.5 = (f32[8,384]{1,0:T(8,128)}, f32[8,384]{1,0:T(8,128)S(1)}, u32[]{:S(2)}, u32[]{:S(2)}) collective-permute-start(f32[8,384]{1,0:T(8,128)} %get-tuple-element.12), channel_id=1, source_target_pairs={{1,8},{2,9},{3,10},{4,11},{5,12},{6,13},{7,14},{9,16},{10,17},{11,... | collective-permute-start | bytes 36872 | tf_op jit(solution)/shard_map/ppermute | solution.py:291
  41.8 6.5 %collective-permute-start.3 = (f32[8,384]{1,0:T(8,128)}, f32[8,384]{1,0:T(8,128)S(1)}, u32[]{:S(2)}, u32[]{:S(2)}) collective-permute-start(f32[8,384]{1,0:T(8,128)} %get-tuple-element.12), channel_id=1, source_target_pairs={{1,0},{2,1},{3,2},{4,3},{5,4},{6,5},{7,6},{9,8},{10,9},{11,10},{12... | collective-permute-start | bytes 36872 | tf_op jit(solution)/shard_map/ppermute | solution.py:283
  45.3 3.7 %copy-start.7 = (f32[8,384]{1,0:T(8,128)}, f32[8,384]{1,0:T(8,128)S(1)}, u32[]{:S(2)}) copy-start(f32[8,384]{1,0:T(8,128)S(1)} %collective-permute-done.7.chh_ref) | copy-start | bytes 36868
  45.3 3.7 %copy-start.8 = (f32[8,384]{1,0:T(8,128)}, f32[8,384]{1,0:T(8,128)S(1)}, u32[]{:S(2)}) copy-start(f32[8,384]{1,0:T(8,128)S(1)} %collective-permute-done.5.clh_ref) | copy-start | bytes 36868
  48.4 0.6 copy-start.9
  49.0 0.7 copy-start.2
  49.6 0.7 copy-start.3

commit v5 on v3

--- a/solution.py
+++ b/solution.py
@@ -20,9 +20,8 @@
 OWN_ENTRIES = ((0, 0), (1, 1), (2, 2), (0, 1), (0, 2), (1, 2))
 
 
-def butterfly_sum(x, axis):
+def butterfly_sum(x, axis, step=1):
     size = lax.axis_size(axis)
-    step = 1
     while step < size:
         pairs = [(i, i ^ step) for i in range(size)]
         x = x + lax.ppermute(x, axis, pairs)
@@ -47,10 +46,15 @@
     return tile
 
 
-def pack_kernel(rs_ref, mod_ref, row_first_ref, row_last_ref, col_first_ref, col_last_ref):
+def pack_kernel(rs_ref, mod_ref, partial_ref, row_first_ref, row_last_ref, col_first_ref, col_last_ref):
     channels, planes, rows, cols = rs_ref.shape
+    count = (channels + 1) * planes
     lane = lax.broadcasted_iota(jnp.int32, (rows, cols), 1)
     tiles = col_first_ref.shape[1] // cols
+    pad_from = count // rows * rows
+    padding = jnp.zeros((row_first_ref.shape[0] - pad_from, cols), jnp.float32)
+    row_first_ref[pl.ds(pad_from, padding.shape[0]), :] = padding
+    row_last_ref[pl.ds(pad_from, padding.shape[0]), :] = padding
     first = [jnp.zeros((rows, cols), jnp.float32) for _ in range(tiles)]
     last = [jnp.zeros((rows, cols), jnp.float32) for _ in range(tiles)]
     for channel in range(channels + 1):
@@ -67,29 +71,57 @@
     for group in range(tiles):
         col_first_ref[:, pl.ds(group * cols, cols)] = first[group]
         col_last_ref[:, pl.ds(group * cols, cols)] = last[group]
-
-
-def pack(loads, modulus):
+    vectors, terms = partial_ref.shape
+    start = row_first_ref.shape[0] - vectors
+    row_first_ref[pl.ds(start, vectors), pl.ds(0, terms)] = partial_ref[...]
+    row_last_ref[pl.ds(start, vectors), pl.ds(0, terms)] = partial_ref[...]
+
+
+def pack(loads, modulus, partial):
     channels, planes, rows, cols = loads.shape
     count = (channels + 1) * planes
     lanes = -(-count // cols) * cols
+    height = -(-(count + partial.shape[0]) // cols) * cols
     vmem = pltpu.MemorySpace.VMEM
     return pl.pallas_call(
         pack_kernel,
         out_shape=[
-            jax.ShapeDtypeStruct((count, cols), jnp.float32),
-            jax.ShapeDtypeStruct((count, cols), jnp.float32),
+            jax.ShapeDtypeStruct((height, cols), jnp.float32),
+            jax.ShapeDtypeStruct((height, cols), jnp.float32),
             jax.ShapeDtypeStruct((rows, lanes), jnp.float32),
             jax.ShapeDtypeStruct((rows, lanes), jnp.float32),
         ],
-        in_specs=[pl.BlockSpec(memory_space=vmem)] * 2,
+        in_specs=[pl.BlockSpec(memory_space=vmem)] * 3,
         out_specs=[pl.BlockSpec(memory_space=vmem)] * 4,
-    )(loads, modulus)
+    )(loads, modulus, partial)
+
+
+def edge_kernel(rlo_ref, rhi_ref, col_first_ref, col_last_ref, ext_first_ref, ext_last_ref):
+    rows, lanes = col_first_ref.shape
+    cols = rlo_ref.shape[1]
+    low = jnp.transpose(rlo_ref[...])[:, 0:lanes]
+    high = jnp.transpose(rhi_ref[...])[:, 0:lanes]
+    zeros = jnp.zeros((ext_first_ref.shape[0] - rows - 2, lanes), jnp.float32)
+    for out_ref, column, lane in ((ext_first_ref, col_first_ref, 0), (ext_last_ref, col_last_ref, cols - 1)):
+        out_ref[pl.ds(0, 1), :] = low[lane : lane + 1, :]
+        out_ref[pl.ds(1, rows), :] = column[...]
+        out_ref[pl.ds(rows + 1, 1), :] = high[lane : lane + 1, :]
+        out_ref[pl.ds(rows + 2, zeros.shape[0]), :] = zeros
+
+
+def edges(row_lo, row_hi, col_first, col_last):
+    rows, lanes = col_first.shape
+    vmem = pltpu.MemorySpace.VMEM
+    return pl.pallas_call(
+        edge_kernel,
+        out_shape=[jax.ShapeDtypeStruct((2 * rows, lanes), jnp.float32)] * 2,
+        in_specs=[pl.BlockSpec(memory_space=vmem)] * 4,
+        out_specs=[pl.BlockSpec(memory_space=vmem)] * 2,
+    )(row_lo, row_hi, col_first, col_last)
 
 
 def smoother_kernel(
     sides_ref, rs_ref, mod_ref, rlo_ref, rhi_ref, clo_ref, chi_ref,
-    cll_ref, clh_ref, chl_ref, chh_ref,
     out_ref, coef_ref, own_ref, inv_ref, row_ref, col_ref,
 ):
     channels, planes, rows, cols = rs_ref.shape
@@ -124,18 +156,9 @@
             j = channel * planes + plane
             group, place = divmod(j, cols)
             window = pl.ds(group * cols, cols)
-            for side, (edge, column, corner_lo, corner_hi) in enumerate(
-                ((0, clo_ref, cll_ref, chl_ref), (cols - 1, chi_ref, clh_ref, chh_ref))
-            ):
-                shift = (edge - place) % cols
-                col_ref[side, channel, plane, pl.ds(1, rows), :] = pltpu.roll(
-                    column[:, window], shift, 1
-                )
-                col_ref[side, channel, plane, pl.ds(0, 1), :] = pltpu.roll(
-                    corner_lo[pl.ds(rows - 1, 1), window], shift, 1
-                )
-                col_ref[side, channel, plane, pl.ds(rows + 1, 1), :] = pltpu.roll(
-                    corner_hi[pl.ds(0, 1), window], shift, 1
+            for side, (edge, column) in enumerate(((0, clo_ref), (cols - 1, chi_ref))):
+                col_ref[side, channel, plane] = pltpu.roll(
+                    column[:, window], (edge - place) % cols, 1
                 )
     row_inverse = RELAX_WEIGHT / (MASS_SHIFT + DIAGONAL_SLOPE * row_ref[:, mod_channel : mod_channel + 1])
     row_ref[:, 0:channels] = row_ref[:, 0:channels] * row_inverse
@@ -271,10 +294,9 @@
     partial_terms = lax.dot_general(
         coarse_vectors, right_sides, ((cell_dims, cell_dims), ((), ())), precision=lax.Precision.HIGHEST
     )
-    restricted = butterfly_sum(partial_terms, "prow")
 
     loads = right_sides.reshape(load_count * 3, plane_count, row_count, column_count)
-    row_first, row_last, col_first, col_last = pack(loads, modulus)
+    row_first, row_last, col_first, col_last = pack(loads, modulus, partial_terms)
     rows_n = lax.axis_size("prow")
     cols_n = lax.axis_size("pcol")
 
@@ -282,23 +304,18 @@
         pairs = [(i, i + step) for i in range(size) if 0 <= i + step < size]
         return lax.ppermute(source, axis, pairs)
 
-    def diagonal(source, step_row, step_col):
-        pairs = []
-        for a in range(rows_n):
-            for b in range(cols_n):
-                if 0 <= a + step_row < rows_n and 0 <= b + step_col < cols_n:
-                    pairs.append((a * cols_n + b, (a + step_row) * cols_n + b + step_col))
-        return lax.ppermute(source, ("prow", "pcol"), pairs)
-
+    row_lo = line(row_last, "prow", rows_n, 1)
+    row_hi = line(row_first, "prow", rows_n, -1)
+    vectors, terms = partial_terms.shape
+    even = lax.axis_index("prow") % 2 == 0
+    partner = jnp.where(even, row_hi[-vectors:, :terms], row_lo[-vectors:, :terms])
+    restricted = butterfly_sum(partial_terms + partner, "prow", 2)
+    ext_first, ext_last = edges(row_lo, row_hi, col_first, col_last)
     halos = (
-        line(row_last, "prow", rows_n, 1),
-        line(row_first, "prow", rows_n, -1),
-        line(col_last, "pcol", cols_n, 1),
-        line(col_first, "pcol", cols_n, -1),
-        diagonal(col_last, 1, 1),
-        diagonal(col_first, 1, -1),
-        diagonal(col_last, -1, 1),
-        diagonal(col_first, -1, -1),
+        row_lo,
+        row_hi,
+        line(ext_last, "pcol", cols_n, 1),
+        line(ext_first, "pcol", cols_n, -1),
     )
     sides = margin_sides[0, 0].astype(jnp.float32)
     smoothed = smoother(sides, loads, modulus, halos)

time: 69.3 us -> 65.9 us (0.951)
  starting transfers between devices: 33.7 us -> 22.5 us
  waiting for transfers between devices: 5.36 us -> 12.4 us
  local copies, waits for them, and re-layouts: 3.12 us -> 1.86 us
  Pallas kernels: 13.5 us -> 14.4 us
  matrix products: 12.2 us -> 13 us
    ppermute x4 -> x3, starting transfers between devices: 17.8 us -> 7.16 us  [butterfly_sum(): x = x + lax.ppermute(x, axis, pairs)]
    ppermute x4, waiting for transfers between devices: 3.05 us -> 9.29 us  [line(): return lax.ppermute(source, axis, pairs)]
    ppermute x4 -> x0, starting transfers between devices: 5.6 us -> none  [diagonal(): return lax.ppermute(source, ('prow', 'pcol'), pairs)]
    ppermute x4, starting transfers between devices: 10.3 us -> 15.3 us  [line(): return lax.ppermute(source, axis, pairs)]
    ppermute x4 -> x3, waiting for transfers between devices: 1.09 us -> 3.13 us  [butterfly_sum(): x = x + lax.ppermute(x, axis, pairs)]
    pallas_call x1 -> x2, Pallas kernels: 2.74 us -> 4.6 us  [the longest x1 2.66 us: pack(): pl.pallas_call(pack_kernel, out_shape=[jax.ShapeDtypeStruct((height, cols...]
    unnamed x22 -> x16, local copies, waits for them, and re-layouts: 1.89 us -> 0.63 us
    ppermute x4 -> x0, waiting for transfers between devices: 1.22 us -> none  [diagonal(): return lax.ppermute(source, ('prow', 'pcol'), pairs)]
  transfers between devices with their start and end apart: 12 -> 7, of which waited for: 3 -> 5; matrix products, arithmetic and copies ran while one was open for 1% -> 1% of each run, Pallas kernels for 4% -> 3%
where the time goes in v5:
time: 65.9 us; the launch traced here: 64.8 us
  starting transfers between devices  22.5 us (34%)
  Pallas kernels  14.4 us (22%)
  matrix products  13 us (20%)
  waiting for transfers between devices  12.4 us (19%)
  local copies, waits for them, and re-layouts  1.86 us (3%)
    ppermute x4, starting transfers between devices, line(): return lax.ppermute(source, axis, pairs)  15.3 us
    pallas_call x1, Pallas kernels, smoother(): pl.pallas_call(smoother_kernel, out_shape=jax.ShapeDtypeStruct(loads.shap...  9.84 us
    ppermute x4, waiting for transfers between devices, line(): return lax.ppermute(source, axis, pairs)  9.29 us
    dot_general x1, matrix products, per_device(): lax.dot_general(coarse_vectors, right_sides, ((cell_dims, cell_dims), (()...  7.6 us
    ppermute x3, starting transfers between devices, butterfly_sum(): x = x + lax.ppermute(x, axis, pairs)  7.16 us
    dot_general x1, matrix products, per_device(): lax.dot_general(solved, coarse_vectors, (((0,), (0,)), ((), ())), precisi...  5.15 us
    ppermute x3, waiting for transfers between devices, butterfly_sum(): x = x + lax.ppermute(x, axis, pairs)  3.13 us
    pallas_call x1, Pallas kernels, pack(): pl.pallas_call(pack_kernel, out_shape=[jax.ShapeDtypeStruct((height, cols...  2.66 us
  transfers between devices with their start and end apart: 7, of which 5 were waited for; matrix products, arithmetic and copies ran while one was open for 1% of the time, Pallas kernels for 3%

profile of v5, /device:TPU:1, one launch (start us, length us, event | category | flops | bytes accessed | tf_op | source)
XLA Modules:
  0.0 64.8 jit_solution(14935002517213188306)
XLA Ops:
  0.0 0.0 copy-start
  0.0 7.6 %fusion.5.partial_ref = f32[64,24]{1,0:T(8,128)} fusion(f32[24,3,4,8,128]{4,3,2,1,0:T(8,128)} %param.5, f32[64,3,4,8,128]{4,3,2,1,0:T(8,128)} %param.8), kind=kOutput, calls=%fused_computation.6 | convolution fusion | flops 226492416 | bytes 4331520 | tf_op jit(solution)/shard_map/dot_general | solution.py:294
  7.6 0.0 copy-start.4
  7.6 0.0 copy-start.7
  7.6 2.7 %shard_map.55 = (f32[384,128]{1,0:T(8,128)}, f32[384,128]{1,0:T(8,128)}, f32[8,384]{1,0:T(8,128)}, f32[8,384]{1,0:T(8,128)}) custom-call(f32[72,4,8,128]{3,2,1,0:T(8,128)} %bitcast.16, f32[4,8,128]{2,1,0:T(8,128)} %mod_ref.3, f32[64,24]{1,0:T(8,128)} %fusion.5.partial_ref), custom_call_target="tpu_custom_call" | custom-call | tf_op jit(solution)/shard_map/pallas_call | solution.py:86
  10.3 3.9 %collective-permute-start = (f32[384,128]{1,0:T(8,128)}, f32[384,128]{1,0:T(8,128)S(1)}, u32[]{:S(2)}, u32[]{:S(2)}) collective-permute-start(f32[384,128]{1,0:T(8,128)} %get-tuple-element.11), channel_id=1, source_target_pairs={{0,8},{8,16},{16,24},{24,32},{32,40},{40,48},{48,56},{56,64},{64,7... | collective-permute-start | bytes 589832 | tf_op jit(solution)/shard_map/ppermute | solution.py:305
  14.2 1.3 %collective-permute-start.1 = (f32[384,128]{1,0:T(8,128)}, f32[384,128]{1,0:T(8,128)S(1)}, u32[]{:S(2)}, u32[]{:S(2)}) collective-permute-start(f32[384,128]{1,0:T(8,128)} %get-tuple-element.12), channel_id=1, source_target_pairs={{8,0},{16,8},{24,16},{32,24},{40,32},{48,40},{56,48},{64,56},{72,6... | collective-permute-start | bytes 589832 | tf_op jit(solution)/shard_map/ppermute | solution.py:305
  15.5 2.6 %collective-permute-done.rlo_ref = f32[384,128]{1,0:T(8,128)S(1)} collective-permute-done((f32[384,128]{1,0:T(8,128)}, f32[384,128]{1,0:T(8,128)S(1)}, u32[]{:S(2)}, u32[]{:S(2)}) %collective-permute-start) | collective-permute-done | bytes 196640 | tf_op jit(solution)/shard_map/ppermute | solution.py:305
  18.1 0.0 copy-start.2
  18.1 3.7 %collective-permute-done.1.rhi_ref = f32[384,128]{1,0:T(8,128)S(1)} collective-permute-done((f32[384,128]{1,0:T(8,128)}, f32[384,128]{1,0:T(8,128)S(1)}, u32[]{:S(2)}, u32[]{:S(2)}) %collective-permute-start.1) | collective-permute-done | bytes 196640 | tf_op jit(solution)/shard_map/ppermute | solution.py:305
  21.8 0.0 copy-done.4
  21.8 0.0 copy-start.3
  21.8 2.5 %collective-permute-start.4 = (f32[64,24]{1,0:T(8,128)S(1)}, f32[64,24]{1,0:T(8,128)S(1)}, u32[]{:S(2)}, u32[]{:S(2)}) collective-permute-start(f32[64,24]{1,0:T(8,128)S(1)} %fusion.10), channel_id=1, source_target_pairs={{0,16},{8,24},{16,0},{24,8},{32,48},{40,56},{48,32},{56,40},{64,80... | collective-permute-start | bytes 18440 | tf_op jit(solution)/shard_map/ppermute | solution.py:27
  24.4 1.8 %collective-permute-done.4 = f32[64,24]{1,0:T(8,128)S(1)} collective-permute-done((f32[64,24]{1,0:T(8,128)S(1)}, f32[64,24]{1,0:T(8,128)S(1)}, u32[]{:S(2)}, u32[]{:S(2)}) %collective-permute-start.4) | collective-permute-done | bytes 6176 | tf_op jit(solution)/shard_map/ppermute | solution.py:27
  26.2 1.6 %collective-permute-start.5 = (f32[64,24]{1,0:T(8,128)S(1)}, f32[64,24]{1,0:T(8,128)S(1)}, u32[]{:S(2)}, u32[]{:S(2)}) collective-permute-start(f32[64,24]{1,0:T(8,128)S(1)} %add.21), channel_id=1, source_target_pairs={{0,32},{8,40},{16,48},{24,56},{32,0},{40,8},{48,16},{56,24},{64,96... | collective-permute-start | bytes 18440 | tf_op jit(solution)/shard_map/ppermute | solution.py:27
  27.7 1.3 %collective-permute-done.5 = f32[64,24]{1,0:T(8,128)S(1)} collective-permute-done((f32[64,24]{1,0:T(8,128)S(1)}, f32[64,24]{1,0:T(8,128)S(1)}, u32[]{:S(2)}, u32[]{:S(2)}) %collective-permute-start.5) | collective-permute-done | bytes 6176 | tf_op jit(solution)/shard_map/ppermute | solution.py:27
  29.1 3.1 %collective-permute-start.6 = (f32[64,24]{1,0:T(8,128)S(1)}, f32[64,24]{1,0:T(8,128)S(1)}, u32[]{:S(2)}, u32[]{:S(2)}) collective-permute-start(f32[64,24]{1,0:T(8,128)S(1)} %add.22), channel_id=1, source_target_pairs={{0,64},{8,72},{16,80},{24,88},{32,96},{40,104},{48,112},{56,120},{... | collective-permute-start | bytes 18440 | tf_op jit(solution)/shard_map/ppermute | solution.py:27
  32.1 0.0 copy-done.7
  32.1 0.5 convert_bitcast_fusion.sides_ref
  32.7 0.0 copy-done.3
  32.7 0.0 copy-done.2
  32.7 0.0 copy-start.1
  32.7 1.9 %shard_map.56 = (f32[16,384]{1,0:T(8,128)}, f32[16,384]{1,0:T(8,128)}) custom-call(f32[384,128]{1,0:T(8,128)} %copy-done.2, f32[384,128]{1,0:T(8,128)} %copy-done.3, f32[8,384]{1,0:T(8,128)} %get-tuple-element.13.col_first_ref, f32[8,384]{1,0:T(8,128)} %get-tuple-element.14.col_last_ref), custom_call_target="tpu_custom_call" | custom-call | tf_op jit(solution)/shard_map/pallas_call | solution.py:115
  34.6 8.0 %collective-permute-start.2 = (f32[16,384]{1,0:T(8,128)}, f32[16,384]{1,0:T(8,128)S(1)}, u32[]{:S(2)}, u32[]{:S(2)}) collective-permute-start(f32[16,384]{1,0:T(8,128)} %get-tuple-element.15), channel_id=1, source_target_pairs={{0,1},{1,2},{2,3},{3,4},{4,5},{5,6},{6,7},{8,9},{9,10},{10,11},{11... | collective-permute-start | bytes 73736 | tf_op jit(solution)/shard_map/ppermute | solution.py:305
  42.6 2.1 %collective-permute-start.3 = (f32[16,384]{1,0:T(8,128)}, f32[16,384]{1,0:T(8,128)S(1)}, u32[]{:S(2)}, u32[]{:S(2)}) collective-permute-start(f32[16,384]{1,0:T(8,128)} %get-tuple-element.16), channel_id=1, source_target_pairs={{1,0},{2,1},{3,2},{4,3},{5,4},{6,5},{7,6},{9,8},{10,9},{11,10},{12... | collective-permute-start | bytes 73736 | tf_op jit(solution)/shard_map/ppermute | solution.py:305
  44.7 0.0 collective-permute-done.6
  44.7 0.0 copy-done
  44.8 0.2 convolution_bitcast_fusion
  45.0 0.0 collective-permute-done.2.clo_ref
  45.0 0.0 copy-start.5
  45.0 3.0 %collective-permute-done.3.chi_ref = f32[16,384]{1,0:T(8,128)S(1)} collective-permute-done((f32[16,384]{1,0:T(8,128)}, f32[16,384]{1,0:T(8,128)S(1)}, u32[]{:S(2)}, u32[]{:S(2)}) %collective-permute-start.3) | collective-permute-done | bytes 24608 | tf_op jit(solution)/shard_map/ppermute | solution.py:305
  48.0 0.0 copy-done.5
  48.0 0.0 copy-start.6
  48.0 0.6 copy-done.6
  48.6 9.8 %shard_map.57 = f32[72,4,8,128]{3,2,1,0:T(8,128)} custom-call(f32[4]{0:T(128)} %convert_bitcast_fusion.sides_ref, f32[72,4,8,128]{3,2,1,0:T(8,128)} %bitcast.17, f32[4,8,128]{2,1,0:T(8,128)} %mod_ref.3, f32[384,128]{1,0:T(8,128)} %copy-done.2, f32[384,128]{1,0:T(8,128)} %copy-done.3, f32[16,384]{1,0:T(8,128)} %copy-done.5, f32[16,384]{1,0:T(8,128)} %copy-done.6), custom_call_target="tpu_custom_call" | custom-call | tf_op jit(solution)/shard_map/pallas_call | solution.py:272
  58.4 0.0 copy-done.1
  58.4 5.1 %copy_add_fusion = f32[24,3,4,8,128]{4,0,3,2,1:T(8,128)S(1)} fusion(f32[24,3,4,8,128]{4,3,2,1,0:T(8,128)} %bitcast.18, f32[24,64,1,1,1]{1,0,4,3,2:T(8,128)S(1)} %convolution_bitcast_fusion, f32[64,3,4,8,128]{4,3,2,1,0:T(8,128)S(1)} %copy-done.1), kind=kOutput, calls=%fused_computation.4 | convolution fusion | flops 226787328 | bytes 5511168 | tf_op jit(solution)/shard_map/dot_general | solution.py:324
  63.6 1.2 %copy.12 = f32[24,3,4,8,128]{4,3,2,1,0:T(8,128)} copy(f32[24,3,4,8,128]{4,0,3,2,1:T(8,128)S(1)} %copy_add_fusion) | data formatting | bytes 2359296 | tf_op jit(solution)/shard_map/add | solution.py:327
  (3 shorter events, 0.0 us)
Async XLA Ops:
  0.0 44.7 %copy-start = (f32[1,64,64]{2,1,0:T(8,128)S(1)}, f32[1,64,64]{2,1,0:T(8,128)}, u32[]{:S(2)}) copy-start(f32[1,64,64]{2,1,0:T(8,128)} %param.9) | copy-start | bytes 49156
  7.6 14.2 %copy-start.4 = (f32[64,24]{1,0:T(8,128)S(1)}, f32[64,24]{1,0:T(8,128)}, u32[]{:S(2)}) copy-start(f32[64,24]{1,0:T(8,128)} %fusion.5.partial_ref) | copy-start | bytes 18436
  7.6 24.5 %copy-start.7 = (s32[1,1,4]{2,1,0:T(1,128)S(1)}, s32[1,1,4]{2,1,0:T(1,128)}, u32[]{:S(2)}) copy-start(s32[1,1,4]{2,1,0:T(1,128)} %param.7) | copy-start | bytes 52
  10.3 7.8 %collective-permute-start = (f32[384,128]{1,0:T(8,128)}, f32[384,128]{1,0:T(8,128)S(1)}, u32[]{:S(2)}, u32[]{:S(2)}) collective-permute-start(f32[384,128]{1,0:T(8,128)} %get-tuple-element.11), channel_id=1, source_target_pairs={{0,8},{8,16},{16,24},{24,32},{32,40},{40,48},{48,56},{56,64},{64,7... | collective-permute-start | bytes 589832 | tf_op jit(solution)/shard_map/ppermute | solution.py:305
  14.2 7.6 %collective-permute-start.1 = (f32[384,128]{1,0:T(8,128)}, f32[384,128]{1,0:T(8,128)S(1)}, u32[]{:S(2)}, u32[]{:S(2)}) collective-permute-start(f32[384,128]{1,0:T(8,128)} %get-tuple-element.12), channel_id=1, source_target_pairs={{8,0},{16,8},{24,16},{32,24},{40,32},{48,40},{56,48},{64,56},{72,6... | collective-permute-start | bytes 589832 | tf_op jit(solution)/shard_map/ppermute | solution.py:305
  18.1 14.6 %copy-start.2 = (f32[384,128]{1,0:T(8,128)}, f32[384,128]{1,0:T(8,128)S(1)}, u32[]{:S(2)}) copy-start(f32[384,128]{1,0:T(8,128)S(1)} %collective-permute-done.rlo_ref) | copy-start | bytes 589828
  21.8 10.8 %copy-start.3 = (f32[384,128]{1,0:T(8,128)}, f32[384,128]{1,0:T(8,128)S(1)}, u32[]{:S(2)}) copy-start(f32[384,128]{1,0:T(8,128)S(1)} %collective-permute-done.1.rhi_ref) | copy-start | bytes 589828
  21.8 4.3 %collective-permute-start.4 = (f32[64,24]{1,0:T(8,128)S(1)}, f32[64,24]{1,0:T(8,128)S(1)}, u32[]{:S(2)}, u32[]{:S(2)}) collective-permute-start(f32[64,24]{1,0:T(8,128)S(1)} %fusion.10), channel_id=1, source_target_pairs={{0,16},{8,24},{16,0},{24,8},{32,48},{40,56},{48,32},{56,40},{64,80... | collective-permute-start | bytes 18440 | tf_op jit(solution)/shard_map/ppermute | solution.py:27
  26.2 2.9 %collective-permute-start.5 = (f32[64,24]{1,0:T(8,128)S(1)}, f32[64,24]{1,0:T(8,128)S(1)}, u32[]{:S(2)}, u32[]{:S(2)}) collective-permute-start(f32[64,24]{1,0:T(8,128)S(1)} %add.21), channel_id=1, source_target_pairs={{0,32},{8,40},{16,48},{24,56},{32,0},{40,8},{48,16},{56,24},{64,96... | collective-permute-start | bytes 18440 | tf_op jit(solution)/shard_map/ppermute | solution.py:27
  29.1 15.7 %collective-permute-start.6 = (f32[64,24]{1,0:T(8,128)S(1)}, f32[64,24]{1,0:T(8,128)S(1)}, u32[]{:S(2)}, u32[]{:S(2)}) collective-permute-start(f32[64,24]{1,0:T(8,128)S(1)} %add.22), channel_id=1, source_target_pairs={{0,64},{8,72},{16,80},{24,88},{32,96},{40,104},{48,112},{56,120},{... | collective-permute-start | bytes 18440 | tf_op jit(solution)/shard_map/ppermute | solution.py:27
  32.7 25.8 %copy-start.1 = (f32[64,3,4,8,128]{4,3,2,1,0:T(8,128)S(1)}, f32[64,3,4,8,128]{4,3,2,1,0:T(8,128)}, u32[]{:S(2)}) copy-start(f32[64,3,4,8,128]{4,3,2,1,0:T(8,128)} %param.8) | copy-start | bytes 9437188
  34.6 10.4 %collective-permute-start.2 = (f32[16,384]{1,0:T(8,128)}, f32[16,384]{1,0:T(8,128)S(1)}, u32[]{:S(2)}, u32[]{:S(2)}) collective-permute-start(f32[16,384]{1,0:T(8,128)} %get-tuple-element.15), channel_id=1, source_target_pairs={{0,1},{1,2},{2,3},{3,4},{4,5},{5,6},{6,7},{8,9},{9,10},{10,11},{11... | collective-permute-start | bytes 73736 | tf_op jit(solution)/shard_map/ppermute | solution.py:305
  42.6 5.4 %collective-permute-start.3 = (f32[16,384]{1,0:T(8,128)}, f32[16,384]{1,0:T(8,128)S(1)}, u32[]{:S(2)}, u32[]{:S(2)}) collective-permute-start(f32[16,384]{1,0:T(8,128)} %get-tuple-element.16), channel_id=1, source_target_pairs={{1,0},{2,1},{3,2},{4,3},{5,4},{6,5},{7,6},{9,8},{10,9},{11,10},{12... | collective-permute-start | bytes 73736 | tf_op jit(solution)/shard_map/ppermute | solution.py:305
  45.0 3.0 %copy-start.5 = (f32[16,384]{1,0:T(8,128)}, f32[16,384]{1,0:T(8,128)S(1)}, u32[]{:S(2)}) copy-start(f32[16,384]{1,0:T(8,128)S(1)} %collective-permute-done.2.clo_ref) | copy-start | bytes 73732
  48.0 0.6 copy-start.6

commit v6 on v5

--- a/solution.py
+++ b/solution.py
@@ -4,6 +4,7 @@
 from jax.experimental import pallas as pl
 from jax.experimental.pallas import tpu as pltpu
 from jax.sharding import PartitionSpec as P
+
 
 RELAX_WEIGHT = 0.7
 MASS_SHIFT = 0.5
@@ -285,7 +286,7 @@
     )(sides, loads, modulus, *halos)
 
 
-def per_device(right_sides, modulus, margin_sides, coarse_vectors, coarse_inverse):
+def per_device_body(right_sides, modulus, margin_sides, coarse_vectors, coarse_inverse):
     load_count = right_sides.shape[0]
     plane_count = right_sides.shape[2]
     row_count = right_sides.shape[3]
@@ -311,12 +312,7 @@
     partner = jnp.where(even, row_hi[-vectors:, :terms], row_lo[-vectors:, :terms])
     restricted = butterfly_sum(partial_terms + partner, "prow", 2)
     ext_first, ext_last = edges(row_lo, row_hi, col_first, col_last)
-    halos = (
-        row_lo,
-        row_hi,
-        line(ext_last, "pcol", cols_n, 1),
-        line(ext_first, "pcol", cols_n, -1),
-    )
+    halos = (row_lo, row_hi, line(ext_last, "pcol", cols_n, 1), line(ext_first, "pcol", cols_n, -1))
     sides = margin_sides[0, 0].astype(jnp.float32)
     smoothed = smoother(sides, loads, modulus, halos)
 
@@ -337,5 +333,5 @@
     )
     out_specs = P(None, None, None, "prow", "pcol")
     return jax.shard_map(
-        per_device, mesh=mesh, in_specs=in_specs, out_specs=out_specs, check_vma=False
+        per_device_body, mesh=mesh, in_specs=in_specs, out_specs=out_specs, check_vma=False
     )

time: 65.9 us -> 65.9 us (level)
  no operation moved by 1% of the time
where the time goes in v6:
time: 65.9 us; the launch traced here: 64.8 us
  starting transfers between devices  22.5 us (34%)
  Pallas kernels  14.4 us (22%)
  matrix products  13 us (20%)
  waiting for transfers between devices  12.4 us (19%)
  local copies, waits for them, and re-layouts  1.86 us (3%)
    ppermute x4, starting transfers between devices, line(): return lax.ppermute(source, axis, pairs)  15.3 us
    pallas_call x1, Pallas kernels, smoother(): pl.pallas_call(smoother_kernel, out_shape=jax.ShapeDtypeStruct(loads.shap...  9.84 us
    ppermute x4, waiting for transfers between devices, line(): return lax.ppermute(source, axis, pairs)  9.29 us
    dot_general x1, matrix products, per_device_body(): lax.dot_general(coarse_vectors, right_sides, ((cell_dims, cell_dims), (()...  7.6 us
    ppermute x3, starting transfers between devices, butterfly_sum(): x = x + lax.ppermute(x, axis, pairs)  7.16 us
    dot_general x1, matrix products, per_device_body(): lax.dot_general(solved, coarse_vectors, (((0,), (0,)), ((), ())), precisi...  5.15 us
    ppermute x3, waiting for transfers between devices, butterfly_sum(): x = x + lax.ppermute(x, axis, pairs)  3.13 us
    pallas_call x1, Pallas kernels, pack(): pl.pallas_call(pack_kernel, out_shape=[jax.ShapeDtypeStruct((height, cols...  2.66 us
  transfers between devices with their start and end apart: 7, of which 5 were waited for; matrix products, arithmetic and copies ran while one was open for 1% of the time, Pallas kernels for 3%

profile of v6, /device:TPU:1, one launch (start us, length us, event | category | flops | bytes accessed | tf_op | source)
XLA Modules:
  0.0 64.8 jit_solution(14935002517213188306)
XLA Ops:
  0.0 0.0 copy-start
  0.0 7.6 %fusion.5.partial_ref = f32[64,24]{1,0:T(8,128)} fusion(f32[24,3,4,8,128]{4,3,2,1,0:T(8,128)} %param.5, f32[64,3,4,8,128]{4,3,2,1,0:T(8,128)} %param.8), kind=kOutput, calls=%fused_computation.6 | convolution fusion | flops 226492416 | bytes 4331520 | tf_op jit(solution)/shard_map/dot_general | solution.py:295
  7.6 0.0 copy-start.4
  7.6 0.0 copy-start.7
  7.6 2.7 %shard_map.55 = (f32[384,128]{1,0:T(8,128)}, f32[384,128]{1,0:T(8,128)}, f32[8,384]{1,0:T(8,128)}, f32[8,384]{1,0:T(8,128)}) custom-call(f32[72,4,8,128]{3,2,1,0:T(8,128)} %bitcast.16, f32[4,8,128]{2,1,0:T(8,128)} %mod_ref.3, f32[64,24]{1,0:T(8,128)} %fusion.5.partial_ref), custom_call_target="tpu_custom_call" | custom-call | tf_op jit(solution)/shard_map/pallas_call | solution.py:87
  10.3 3.9 %collective-permute-start = (f32[384,128]{1,0:T(8,128)}, f32[384,128]{1,0:T(8,128)S(1)}, u32[]{:S(2)}, u32[]{:S(2)}) collective-permute-start(f32[384,128]{1,0:T(8,128)} %get-tuple-element.11), channel_id=1, source_target_pairs={{0,8},{8,16},{16,24},{24,32},{32,40},{40,48},{48,56},{56,64},{64,7... | collective-permute-start | bytes 589832 | tf_op jit(solution)/shard_map/ppermute | solution.py:306
  14.2 1.3 %collective-permute-start.1 = (f32[384,128]{1,0:T(8,128)}, f32[384,128]{1,0:T(8,128)S(1)}, u32[]{:S(2)}, u32[]{:S(2)}) collective-permute-start(f32[384,128]{1,0:T(8,128)} %get-tuple-element.12), channel_id=1, source_target_pairs={{8,0},{16,8},{24,16},{32,24},{40,32},{48,40},{56,48},{64,56},{72,6... | collective-permute-start | bytes 589832 | tf_op jit(solution)/shard_map/ppermute | solution.py:306
  15.5 2.6 %collective-permute-done.rlo_ref = f32[384,128]{1,0:T(8,128)S(1)} collective-permute-done((f32[384,128]{1,0:T(8,128)}, f32[384,128]{1,0:T(8,128)S(1)}, u32[]{:S(2)}, u32[]{:S(2)}) %collective-permute-start) | collective-permute-done | bytes 196640 | tf_op jit(solution)/shard_map/ppermute | solution.py:306
  18.1 0.0 copy-start.2
  18.1 3.7 %collective-permute-done.1.rhi_ref = f32[384,128]{1,0:T(8,128)S(1)} collective-permute-done((f32[384,128]{1,0:T(8,128)}, f32[384,128]{1,0:T(8,128)S(1)}, u32[]{:S(2)}, u32[]{:S(2)}) %collective-permute-start.1) | collective-permute-done | bytes 196640 | tf_op jit(solution)/shard_map/ppermute | solution.py:306
  21.8 0.0 copy-done.4
  21.8 0.0 copy-start.3
  21.8 2.5 %collective-permute-start.4 = (f32[64,24]{1,0:T(8,128)S(1)}, f32[64,24]{1,0:T(8,128)S(1)}, u32[]{:S(2)}, u32[]{:S(2)}) collective-permute-start(f32[64,24]{1,0:T(8,128)S(1)} %fusion.10), channel_id=1, source_target_pairs={{0,16},{8,24},{16,0},{24,8},{32,48},{40,56},{48,32},{56,40},{64,80... | collective-permute-start | bytes 18440 | tf_op jit(solution)/shard_map/ppermute | solution.py:28
  24.4 1.8 %collective-permute-done.4 = f32[64,24]{1,0:T(8,128)S(1)} collective-permute-done((f32[64,24]{1,0:T(8,128)S(1)}, f32[64,24]{1,0:T(8,128)S(1)}, u32[]{:S(2)}, u32[]{:S(2)}) %collective-permute-start.4) | collective-permute-done | bytes 6176 | tf_op jit(solution)/shard_map/ppermute | solution.py:28
  26.2 1.6 %collective-permute-start.5 = (f32[64,24]{1,0:T(8,128)S(1)}, f32[64,24]{1,0:T(8,128)S(1)}, u32[]{:S(2)}, u32[]{:S(2)}) collective-permute-start(f32[64,24]{1,0:T(8,128)S(1)} %add.21), channel_id=1, source_target_pairs={{0,32},{8,40},{16,48},{24,56},{32,0},{40,8},{48,16},{56,24},{64,96... | collective-permute-start | bytes 18440 | tf_op jit(solution)/shard_map/ppermute | solution.py:28
  27.7 1.3 %collective-permute-done.5 = f32[64,24]{1,0:T(8,128)S(1)} collective-permute-done((f32[64,24]{1,0:T(8,128)S(1)}, f32[64,24]{1,0:T(8,128)S(1)}, u32[]{:S(2)}, u32[]{:S(2)}) %collective-permute-start.5) | collective-permute-done | bytes 6176 | tf_op jit(solution)/shard_map/ppermute | solution.py:28
  29.1 3.1 %collective-permute-start.6 = (f32[64,24]{1,0:T(8,128)S(1)}, f32[64,24]{1,0:T(8,128)S(1)}, u32[]{:S(2)}, u32[]{:S(2)}) collective-permute-start(f32[64,24]{1,0:T(8,128)S(1)} %add.22), channel_id=1, source_target_pairs={{0,64},{8,72},{16,80},{24,88},{32,96},{40,104},{48,112},{56,120},{... | collective-permute-start | bytes 18440 | tf_op jit(solution)/shard_map/ppermute | solution.py:28
  32.1 0.0 copy-done.7
  32.1 0.5 convert_bitcast_fusion.sides_ref
  32.7 0.0 copy-done.3
  32.7 0.0 copy-done.2
  32.7 0.0 copy-start.1
  32.7 1.9 %shard_map.56 = (f32[16,384]{1,0:T(8,128)}, f32[16,384]{1,0:T(8,128)}) custom-call(f32[384,128]{1,0:T(8,128)} %copy-done.2, f32[384,128]{1,0:T(8,128)} %copy-done.3, f32[8,384]{1,0:T(8,128)} %get-tuple-element.13.col_first_ref, f32[8,384]{1,0:T(8,128)} %get-tuple-element.14.col_last_ref), custom_call_target="tpu_custom_call" | custom-call | tf_op jit(solution)/shard_map/pallas_call | solution.py:116
  34.6 8.0 %collective-permute-start.2 = (f32[16,384]{1,0:T(8,128)}, f32[16,384]{1,0:T(8,128)S(1)}, u32[]{:S(2)}, u32[]{:S(2)}) collective-permute-start(f32[16,384]{1,0:T(8,128)} %get-tuple-element.15), channel_id=1, source_target_pairs={{0,1},{1,2},{2,3},{3,4},{4,5},{5,6},{6,7},{8,9},{9,10},{10,11},{11... | collective-permute-start | bytes 73736 | tf_op jit(solution)/shard_map/ppermute | solution.py:306
  42.6 2.1 %collective-permute-start.3 = (f32[16,384]{1,0:T(8,128)}, f32[16,384]{1,0:T(8,128)S(1)}, u32[]{:S(2)}, u32[]{:S(2)}) collective-permute-start(f32[16,384]{1,0:T(8,128)} %get-tuple-element.16), channel_id=1, source_target_pairs={{1,0},{2,1},{3,2},{4,3},{5,4},{6,5},{7,6},{9,8},{10,9},{11,10},{12... | collective-permute-start | bytes 73736 | tf_op jit(solution)/shard_map/ppermute | solution.py:306
  44.7 0.0 collective-permute-done.6
  44.7 0.0 copy-done
  44.8 0.2 convolution_bitcast_fusion
  45.0 0.0 collective-permute-done.2.clo_ref
  45.0 0.0 copy-start.5
  45.0 3.0 %collective-permute-done.3.chi_ref = f32[16,384]{1,0:T(8,128)S(1)} collective-permute-done((f32[16,384]{1,0:T(8,128)}, f32[16,384]{1,0:T(8,128)S(1)}, u32[]{:S(2)}, u32[]{:S(2)}) %collective-permute-start.3) | collective-permute-done | bytes 24608 | tf_op jit(solution)/shard_map/ppermute | solution.py:306
  48.0 0.0 copy-done.5
  48.0 0.0 copy-start.6
  48.0 0.6 copy-done.6
  48.6 9.8 %shard_map.57 = f32[72,4,8,128]{3,2,1,0:T(8,128)} custom-call(f32[4]{0:T(128)} %convert_bitcast_fusion.sides_ref, f32[72,4,8,128]{3,2,1,0:T(8,128)} %bitcast.17, f32[4,8,128]{2,1,0:T(8,128)} %mod_ref.3, f32[384,128]{1,0:T(8,128)} %copy-done.2, f32[384,128]{1,0:T(8,128)} %copy-done.3, f32[16,384]{1,0:T(8,128)} %copy-done.5, f32[16,384]{1,0:T(8,128)} %copy-done.6), custom_call_target="tpu_custom_call" | custom-call | tf_op jit(solution)/shard_map/pallas_call | solution.py:273
  58.4 0.0 copy-done.1
  58.4 5.1 %copy_add_fusion = f32[24,3,4,8,128]{4,0,3,2,1:T(8,128)S(1)} fusion(f32[24,3,4,8,128]{4,3,2,1,0:T(8,128)} %bitcast.18, f32[24,64,1,1,1]{1,0,4,3,2:T(8,128)S(1)} %convolution_bitcast_fusion, f32[64,3,4,8,128]{4,3,2,1,0:T(8,128)S(1)} %copy-done.1), kind=kOutput, calls=%fused_computation.4 | convolution fusion | flops 226787328 | bytes 5511168 | tf_op jit(solution)/shard_map/dot_general | solution.py:320
  63.6 1.2 %copy.12 = f32[24,3,4,8,128]{4,3,2,1,0:T(8,128)} copy(f32[24,3,4,8,128]{4,0,3,2,1:T(8,128)S(1)} %copy_add_fusion) | data formatting | bytes 2359296 | tf_op jit(solution)/shard_map/add | solution.py:323
  (3 shorter events, 0.0 us)
Async XLA Ops:
  0.0 44.7 %copy-start = (f32[1,64,64]{2,1,0:T(8,128)S(1)}, f32[1,64,64]{2,1,0:T(8,128)}, u32[]{:S(2)}) copy-start(f32[1,64,64]{2,1,0:T(8,128)} %param.9) | copy-start | bytes 49156
  7.6 14.2 %copy-start.4 = (f32[64,24]{1,0:T(8,128)S(1)}, f32[64,24]{1,0:T(8,128)}, u32[]{:S(2)}) copy-start(f32[64,24]{1,0:T(8,128)} %fusion.5.partial_ref) | copy-start | bytes 18436
  7.6 24.5 %copy-start.7 = (s32[1,1,4]{2,1,0:T(1,128)S(1)}, s32[1,1,4]{2,1,0:T(1,128)}, u32[]{:S(2)}) copy-start(s32[1,1,4]{2,1,0:T(1,128)} %param.7) | copy-start | bytes 52
  10.3 7.8 %collective-permute-start = (f32[384,128]{1,0:T(8,128)}, f32[384,128]{1,0:T(8,128)S(1)}, u32[]{:S(2)}, u32[]{:S(2)}) collective-permute-start(f32[384,128]{1,0:T(8,128)} %get-tuple-element.11), channel_id=1, source_target_pairs={{0,8},{8,16},{16,24},{24,32},{32,40},{40,48},{48,56},{56,64},{64,7... | collective-permute-start | bytes 589832 | tf_op jit(solution)/shard_map/ppermute | solution.py:306
  14.2 7.6 %collective-permute-start.1 = (f32[384,128]{1,0:T(8,128)}, f32[384,128]{1,0:T(8,128)S(1)}, u32[]{:S(2)}, u32[]{:S(2)}) collective-permute-start(f32[384,128]{1,0:T(8,128)} %get-tuple-element.12), channel_id=1, source_target_pairs={{8,0},{16,8},{24,16},{32,24},{40,32},{48,40},{56,48},{64,56},{72,6... | collective-permute-start | bytes 589832 | tf_op jit(solution)/shard_map/ppermute | solution.py:306
  18.1 14.6 %copy-start.2 = (f32[384,128]{1,0:T(8,128)}, f32[384,128]{1,0:T(8,128)S(1)}, u32[]{:S(2)}) copy-start(f32[384,128]{1,0:T(8,128)S(1)} %collective-permute-done.rlo_ref) | copy-start | bytes 589828
  21.8 10.8 %copy-start.3 = (f32[384,128]{1,0:T(8,128)}, f32[384,128]{1,0:T(8,128)S(1)}, u32[]{:S(2)}) copy-start(f32[384,128]{1,0:T(8,128)S(1)} %collective-permute-done.1.rhi_ref) | copy-start | bytes 589828
  21.8 4.3 %collective-permute-start.4 = (f32[64,24]{1,0:T(8,128)S(1)}, f32[64,24]{1,0:T(8,128)S(1)}, u32[]{:S(2)}, u32[]{:S(2)}) collective-permute-start(f32[64,24]{1,0:T(8,128)S(1)} %fusion.10), channel_id=1, source_target_pairs={{0,16},{8,24},{16,0},{24,8},{32,48},{40,56},{48,32},{56,40},{64,80... | collective-permute-start | bytes 18440 | tf_op jit(solution)/shard_map/ppermute | solution.py:28
  26.2 2.9 %collective-permute-start.5 = (f32[64,24]{1,0:T(8,128)S(1)}, f32[64,24]{1,0:T(8,128)S(1)}, u32[]{:S(2)}, u32[]{:S(2)}) collective-permute-start(f32[64,24]{1,0:T(8,128)S(1)} %add.21), channel_id=1, source_target_pairs={{0,32},{8,40},{16,48},{24,56},{32,0},{40,8},{48,16},{56,24},{64,96... | collective-permute-start | bytes 18440 | tf_op jit(solution)/shard_map/ppermute | solution.py:28
  29.1 15.7 %collective-permute-start.6 = (f32[64,24]{1,0:T(8,128)S(1)}, f32[64,24]{1,0:T(8,128)S(1)}, u32[]{:S(2)}, u32[]{:S(2)}) collective-permute-start(f32[64,24]{1,0:T(8,128)S(1)} %add.22), channel_id=1, source_target_pairs={{0,64},{8,72},{16,80},{24,88},{32,96},{40,104},{48,112},{56,120},{... | collective-permute-start | bytes 18440 | tf_op jit(solution)/shard_map/ppermute | solution.py:28
  32.7 25.8 %copy-start.1 = (f32[64,3,4,8,128]{4,3,2,1,0:T(8,128)S(1)}, f32[64,3,4,8,128]{4,3,2,1,0:T(8,128)}, u32[]{:S(2)}) copy-start(f32[64,3,4,8,128]{4,3,2,1,0:T(8,128)} %param.8) | copy-start | bytes 9437188
  34.6 10.4 %collective-permute-start.2 = (f32[16,384]{1,0:T(8,128)}, f32[16,384]{1,0:T(8,128)S(1)}, u32[]{:S(2)}, u32[]{:S(2)}) collective-permute-start(f32[16,384]{1,0:T(8,128)} %get-tuple-element.15), channel_id=1, source_target_pairs={{0,1},{1,2},{2,3},{3,4},{4,5},{5,6},{6,7},{8,9},{9,10},{10,11},{11... | collective-permute-start | bytes 73736 | tf_op jit(solution)/shard_map/ppermute | solution.py:306
  42.6 5.4 %collective-permute-start.3 = (f32[16,384]{1,0:T(8,128)}, f32[16,384]{1,0:T(8,128)S(1)}, u32[]{:S(2)}, u32[]{:S(2)}) collective-permute-start(f32[16,384]{1,0:T(8,128)} %get-tuple-element.16), channel_id=1, source_target_pairs={{1,0},{2,1},{3,2},{4,3},{5,4},{6,5},{7,6},{9,8},{10,9},{11,10},{12... | collective-permute-start | bytes 73736 | tf_op jit(solution)/shard_map/ppermute | solution.py:306
  45.0 3.0 %copy-start.5 = (f32[16,384]{1,0:T(8,128)}, f32[16,384]{1,0:T(8,128)S(1)}, u32[]{:S(2)}) copy-start(f32[16,384]{1,0:T(8,128)S(1)} %collective-permute-done.2.clo_ref) | copy-start | bytes 73732
  48.0 0.6 copy-start.6

commit v7 on v6

--- a/solution.py
+++ b/solution.py
@@ -21,13 +21,17 @@
 OWN_ENTRIES = ((0, 0), (1, 1), (2, 2), (0, 1), (0, 2), (1, 2))
 
 
-def butterfly_sum(x, axis, step=1):
+def butterfly_sum(x, axis, step=1, after_first=None):
     size = lax.axis_size(axis)
     while step < size:
         pairs = [(i, i ^ step) for i in range(size)]
         x = x + lax.ppermute(x, axis, pairs)
+        if after_first is not None:
+            x, after_first = lax.optimization_barrier((x, after_first()))
+            held = after_first
+            after_first = None
         step *= 2
-    return x
+    return x, held
 
 
 def neighbour_shift(tile, row_lo, row_hi, col_lo, col_hi, step_x, step_y):
@@ -310,11 +314,14 @@
     vectors, terms = partial_terms.shape
     even = lax.axis_index("prow") % 2 == 0
     partner = jnp.where(even, row_hi[-vectors:, :terms], row_lo[-vectors:, :terms])
-    restricted = butterfly_sum(partial_terms + partner, "prow", 2)
     ext_first, ext_last = edges(row_lo, row_hi, col_first, col_last)
     halos = (row_lo, row_hi, line(ext_last, "pcol", cols_n, 1), line(ext_first, "pcol", cols_n, -1))
     sides = margin_sides[0, 0].astype(jnp.float32)
-    smoothed = smoother(sides, loads, modulus, halos)
+
+    def smooth():
+        return smoother(sides, loads, modulus, halos)
+
+    restricted, smoothed = butterfly_sum(partial_terms + partner, "prow", 2, smooth)
 
     solved = jnp.dot(coarse_inverse[0], restricted, precision=lax.Precision.HIGHEST)
     lifted = lax.dot_general(

time: 65.9 us -> 67.4 us (1.023)
  the two profiles are of different devices: /device:TPU:1 before, /device:TPU:56 now
where the time goes in v7:
time: 67.4 us; the launch traced here: 67.2 us
  waiting for transfers between devices  21.4 us (32%)
  Pallas kernels  14.3 us (21%)
  starting transfers between devices  13.7 us (20%)
  matrix products  13 us (19%)
  local copies, waits for them, and re-layouts  3.13 us (5%)
  other arithmetic  1.51 us (2%)
    ppermute x3, waiting for transfers between devices, butterfly_sum(): x = x + lax.ppermute(x, axis, pairs)  12.8 us
    ppermute x4, starting transfers between devices, line(): return lax.ppermute(source, axis, pairs)  12.3 us
    pallas_call x1, Pallas kernels, smoother(): pl.pallas_call(smoother_kernel, out_shape=jax.ShapeDtypeStruct(loads.shap...  9.84 us
    ppermute x4, waiting for transfers between devices, line(): return lax.ppermute(source, axis, pairs)  8.64 us
    dot_general x1, matrix products, per_device_body(): lax.dot_general(coarse_vectors, right_sides, ((cell_dims, cell_dims), (()...  7.6 us
    dot_general x1, matrix products, per_device_body(): lax.dot_general(solved, coarse_vectors, (((0,), (0,)), ((), ())), precisi...  5.16 us
    pallas_call x1, Pallas kernels, pack(): pl.pallas_call(pack_kernel, out_shape=[jax.ShapeDtypeStruct((height, cols...  2.66 us
    unnamed x16, local copies, waits for them, and re-layouts  1.9 us
  transfers between devices with their start and end apart: 7, of which 5 were waited for; matrix products, arithmetic and copies ran while one was open for 2% of the time, Pallas kernels for 0%

profile of v7, /device:TPU:56, one launch (start us, length us, event | category | flops | bytes accessed | tf_op | source)
XLA Modules:
  0.0 67.2 jit_solution(472922733473308153)
XLA Ops:
  0.0 0.0 copy-start
  0.0 7.6 %fusion.8.partial_ref = f32[64,24]{1,0:T(8,128)} fusion(f32[24,3,4,8,128]{4,3,2,1,0:T(8,128)} %param.5, f32[64,3,4,8,128]{4,3,2,1,0:T(8,128)} %param.8), kind=kOutput, calls=%fused_computation.6 | convolution fusion | flops 226492416 | bytes 4331520 | tf_op jit(solution)/shard_map/dot_general | solution.py:299
  7.6 0.0 copy-start.4
  7.6 0.0 copy-start.7
  7.6 2.7 %shard_map.55 = (f32[384,128]{1,0:T(8,128)}, f32[384,128]{1,0:T(8,128)}, f32[8,384]{1,0:T(8,128)}, f32[8,384]{1,0:T(8,128)}) custom-call(f32[72,4,8,128]{3,2,1,0:T(8,128)} %bitcast.16, f32[4,8,128]{2,1,0:T(8,128)} %mod_ref.3, f32[64,24]{1,0:T(8,128)} %fusion.8.partial_ref), custom_call_target="tpu_custom_call" | custom-call | tf_op jit(solution)/shard_map/pallas_call | solution.py:91
  10.3 4.8 %collective-permute-start = (f32[384,128]{1,0:T(8,128)}, f32[384,128]{1,0:T(8,128)S(1)}, u32[]{:S(2)}, u32[]{:S(2)}) collective-permute-start(f32[384,128]{1,0:T(8,128)} %get-tuple-element.13), channel_id=1, source_target_pairs={{8,0},{16,8},{24,16},{32,24},{40,32},{48,40},{56,48},{64,56},{72,6... | collective-permute-start | bytes 589832 | tf_op jit(solution)/shard_map/ppermute | solution.py:310
  15.1 1.9 %collective-permute-start.1 = (f32[384,128]{1,0:T(8,128)}, f32[384,128]{1,0:T(8,128)S(1)}, u32[]{:S(2)}, u32[]{:S(2)}) collective-permute-start(f32[384,128]{1,0:T(8,128)} %get-tuple-element.14), channel_id=1, source_target_pairs={{0,8},{8,16},{16,24},{24,32},{32,40},{40,48},{48,56},{56,64},{64,7... | collective-permute-start | bytes 589832 | tf_op jit(solution)/shard_map/ppermute | solution.py:310
  17.1 2.5 %collective-permute-done.rhi_ref = f32[384,128]{1,0:T(8,128)S(1)} collective-permute-done((f32[384,128]{1,0:T(8,128)}, f32[384,128]{1,0:T(8,128)S(1)}, u32[]{:S(2)}, u32[]{:S(2)}) %collective-permute-start) | collective-permute-done | bytes 196640 | tf_op jit(solution)/shard_map/ppermute | solution.py:310
  19.6 0.0 copy-start.2
  19.6 6.1 %collective-permute-done.1.rlo_ref = f32[384,128]{1,0:T(8,128)S(1)} collective-permute-done((f32[384,128]{1,0:T(8,128)}, f32[384,128]{1,0:T(8,128)S(1)}, u32[]{:S(2)}, u32[]{:S(2)}) %collective-permute-start.1) | collective-permute-done | bytes 196640 | tf_op jit(solution)/shard_map/ppermute | solution.py:310
  25.7 0.0 copy-start.3
  25.7 0.0 copy-done.2
  25.7 0.7 %copy-done.3 = f32[384,128]{1,0:T(8,128)} copy-done((f32[384,128]{1,0:T(8,128)}, f32[384,128]{1,0:T(8,128)S(1)}, u32[]{:S(2)}) %copy-start.3) | copy-done | bytes 196632
  26.4 1.8 %shard_map.56 = (f32[16,384]{1,0:T(8,128)}, f32[16,384]{1,0:T(8,128)}) custom-call(f32[384,128]{1,0:T(8,128)} %copy-done.3, f32[384,128]{1,0:T(8,128)} %copy-done.2, f32[8,384]{1,0:T(8,128)} %get-tuple-element.15.col_first_ref, f32[8,384]{1,0:T(8,128)} %get-tuple-element.16.col_last_ref), custom_call_target="tpu_custom_call" | custom-call | tf_op jit(solution)/shard_map/pallas_call | solution.py:120
  28.2 1.9 %collective-permute-start.3 = (f32[16,384]{1,0:T(8,128)}, f32[16,384]{1,0:T(8,128)S(1)}, u32[]{:S(2)}, u32[]{:S(2)}) collective-permute-start(f32[16,384]{1,0:T(8,128)} %get-tuple-element.17), channel_id=1, source_target_pairs={{0,1},{1,2},{2,3},{3,4},{4,5},{5,6},{6,7},{8,9},{9,10},{10,11},{11... | collective-permute-start | bytes 73736 | tf_op jit(solution)/shard_map/ppermute | solution.py:310
  30.1 3.6 %collective-permute-start.4 = (f32[16,384]{1,0:T(8,128)}, f32[16,384]{1,0:T(8,128)S(1)}, u32[]{:S(2)}, u32[]{:S(2)}) collective-permute-start(f32[16,384]{1,0:T(8,128)} %get-tuple-element.18), channel_id=1, source_target_pairs={{1,0},{2,1},{3,2},{4,3},{5,4},{6,5},{7,6},{9,8},{10,9},{11,10},{12... | collective-permute-start | bytes 73736 | tf_op jit(solution)/shard_map/ppermute | solution.py:310
  33.7 0.0 copy-done.4
  33.8 0.0 copy-start.1
  33.8 0.9 %fusion.13 = f32[64,24]{1,0:T(8,128)S(1)} fusion(f32[64,24]{1,0:T(8,128)S(1)} %copy-done.4, f32[384,128]{1,0:T(8,128)} %copy-done.3, f32[384,128]{1,0:T(8,128)} %copy-done.2, pred[]{:T(512)S(6)} %eq.5), kind=kLoop, calls=%fused_computation.9 | loop fusion | flops 3072 | bytes 24577 | tf_op jit(solution)/shard_map/add | solution.py:324
  34.7 0.0 collective-permute-start.2
  34.7 0.0 copy-done.7
  34.7 0.6 convert_bitcast_fusion.sides_ref
  35.3 4.8 %collective-permute-done.2 = f32[64,24]{1,0:T(8,128)S(1)} collective-permute-done((f32[64,24]{1,0:T(8,128)S(1)}, f32[64,24]{1,0:T(8,128)S(1)}, u32[]{:S(2)}, u32[]{:S(2)}) %collective-permute-start.2) | collective-permute-done | bytes 6176 | tf_op jit(solution)/shard_map/ppermute | solution.py:28
  40.1 0.0 collective-permute-done.3.clo_ref
  40.1 0.0 copy-start.5
  40.1 0.0 collective-permute-done.4.chi_ref
  40.2 0.6 copy-done.5
  40.7 0.0 copy-start.6
  40.7 0.6 copy-done.6
  41.3 9.8 %shard_map.57 = f32[72,4,8,128]{3,2,1,0:T(8,128)} custom-call(f32[4]{0:T(128)} %convert_bitcast_fusion.sides_ref, f32[72,4,8,128]{3,2,1,0:T(8,128)} %bitcast.17, f32[4,8,128]{2,1,0:T(8,128)} %mod_ref.3, f32[384,128]{1,0:T(8,128)} %copy-done.3, f32[384,128]{1,0:T(8,128)} %copy-done.2, f32[16,384]{1,0:T(8,128)} %copy-done.5, f32[16,384]{1,0:T(8,128)} %copy-done.6), custom_call_target="tpu_custom_call" | custom-call | tf_op jit(solution)/shard_map/pallas_call | solution.py:277
  51.2 0.4 collective-permute-start.5
  51.6 3.5 %collective-permute-done.5 = f32[64,24]{1,0:T(8,128)S(1)} collective-permute-done((f32[64,24]{1,0:T(8,128)S(1)}, f32[64,24]{1,0:T(8,128)S(1)}, u32[]{:S(2)}, u32[]{:S(2)}) %collective-permute-start.5) | collective-permute-done | bytes 6176 | tf_op jit(solution)/shard_map/ppermute | solution.py:28
  55.1 0.9 %collective-permute-start.6 = (f32[64,24]{1,0:T(8,128)S(1)}, f32[64,24]{1,0:T(8,128)S(1)}, u32[]{:S(2)}, u32[]{:S(2)}) collective-permute-start(f32[64,24]{1,0:T(8,128)S(1)} %add.22), channel_id=1, source_target_pairs={{0,64},{8,72},{16,80},{24,88},{32,96},{40,104},{48,112},{56,120},{... | collective-permute-start | bytes 18440 | tf_op jit(solution)/shard_map/ppermute | solution.py:28
  56.0 4.5 %collective-permute-done.6 = f32[64,24]{1,0:T(8,128)S(1)} collective-permute-done((f32[64,24]{1,0:T(8,128)S(1)}, f32[64,24]{1,0:T(8,128)S(1)}, u32[]{:S(2)}, u32[]{:S(2)}) %collective-permute-start.6) | collective-permute-done | bytes 6176 | tf_op jit(solution)/shard_map/ppermute | solution.py:28
  60.5 0.0 copy-done
  60.5 0.2 convolution_bitcast_fusion
  60.8 0.0 copy-done.1
  60.8 5.2 %fusion.4 = f32[24,3,4,8,128]{4,0,3,2,1:T(8,128)S(1)} fusion(f32[24,64,1,1,1]{1,0,4,3,2:T(8,128)S(1)} %convolution_bitcast_fusion, f32[64,3,4,8,128]{4,3,2,1,0:T(8,128)S(1)} %copy-done.1, f32[24,3,4,8,128]{4,3,2,1,0:T(8,128)} %bitcast.18), kind=kOutput, calls=%fused_computation.4 | convolution fusion | flops 226787328 | bytes 5511168 | tf_op jit(solution)/shard_map/dot_general | solution.py:327
  65.9 1.2 %copy.12 = f32[24,3,4,8,128]{4,3,2,1,0:T(8,128)} copy(f32[24,3,4,8,128]{4,0,3,2,1:T(8,128)S(1)} %fusion.4) | data formatting | bytes 2359296 | tf_op jit(solution)/shard_map/add | solution.py:330
  (2 shorter events, 0.0 us)
Async XLA Ops:
  0.0 60.5 %copy-start = (f32[1,64,64]{2,1,0:T(8,128)S(1)}, f32[1,64,64]{2,1,0:T(8,128)}, u32[]{:S(2)}) copy-start(f32[1,64,64]{2,1,0:T(8,128)} %param.9) | copy-start | bytes 49156
  7.6 26.1 %copy-start.4 = (f32[64,24]{1,0:T(8,128)S(1)}, f32[64,24]{1,0:T(8,128)}, u32[]{:S(2)}) copy-start(f32[64,24]{1,0:T(8,128)} %fusion.8.partial_ref) | copy-start | bytes 18436
  7.6 27.1 %copy-start.7 = (s32[1,1,4]{2,1,0:T(1,128)S(1)}, s32[1,1,4]{2,1,0:T(1,128)}, u32[]{:S(2)}) copy-start(s32[1,1,4]{2,1,0:T(1,128)} %param.7) | copy-start | bytes 52
  10.3 9.3 %collective-permute-start = (f32[384,128]{1,0:T(8,128)}, f32[384,128]{1,0:T(8,128)S(1)}, u32[]{:S(2)}, u32[]{:S(2)}) collective-permute-start(f32[384,128]{1,0:T(8,128)} %get-tuple-element.13), channel_id=1, source_target_pairs={{8,0},{16,8},{24,16},{32,24},{40,32},{48,40},{56,48},{64,56},{72,6... | collective-permute-start | bytes 589832 | tf_op jit(solution)/shard_map/ppermute | solution.py:310
  15.1 10.6 %collective-permute-start.1 = (f32[384,128]{1,0:T(8,128)}, f32[384,128]{1,0:T(8,128)S(1)}, u32[]{:S(2)}, u32[]{:S(2)}) collective-permute-start(f32[384,128]{1,0:T(8,128)} %get-tuple-element.14), channel_id=1, source_target_pairs={{0,8},{8,16},{16,24},{24,32},{32,40},{40,48},{48,56},{56,64},{64,7... | collective-permute-start | bytes 589832 | tf_op jit(solution)/shard_map/ppermute | solution.py:310
  19.6 6.1 %copy-start.2 = (f32[384,128]{1,0:T(8,128)}, f32[384,128]{1,0:T(8,128)S(1)}, u32[]{:S(2)}) copy-start(f32[384,128]{1,0:T(8,128)S(1)} %collective-permute-done.rhi_ref) | copy-start | bytes 589828
  25.7 0.7 %copy-start.3 = (f32[384,128]{1,0:T(8,128)}, f32[384,128]{1,0:T(8,128)S(1)}, u32[]{:S(2)}) copy-start(f32[384,128]{1,0:T(8,128)S(1)} %collective-permute-done.1.rlo_ref) | copy-start | bytes 589828
  28.2 12.0 %collective-permute-start.3 = (f32[16,384]{1,0:T(8,128)}, f32[16,384]{1,0:T(8,128)S(1)}, u32[]{:S(2)}, u32[]{:S(2)}) collective-permute-start(f32[16,384]{1,0:T(8,128)} %get-tuple-element.17), channel_id=1, source_target_pairs={{0,1},{1,2},{2,3},{3,4},{4,5},{5,6},{6,7},{8,9},{9,10},{10,11},{11... | collective-permute-start | bytes 73736 | tf_op jit(solution)/shard_map/ppermute | solution.py:310
  30.1 10.1 %collective-permute-start.4 = (f32[16,384]{1,0:T(8,128)}, f32[16,384]{1,0:T(8,128)S(1)}, u32[]{:S(2)}, u32[]{:S(2)}) collective-permute-start(f32[16,384]{1,0:T(8,128)} %get-tuple-element.18), channel_id=1, source_target_pairs={{1,0},{2,1},{3,2},{4,3},{5,4},{6,5},{7,6},{9,8},{10,9},{11,10},{12... | collective-permute-start | bytes 73736 | tf_op jit(solution)/shard_map/ppermute | solution.py:310
  33.8 27.0 %copy-start.1 = (f32[64,3,4,8,128]{4,3,2,1,0:T(8,128)S(1)}, f32[64,3,4,8,128]{4,3,2,1,0:T(8,128)}, u32[]{:S(2)}) copy-start(f32[64,3,4,8,128]{4,3,2,1,0:T(8,128)} %param.8) | copy-start | bytes 9437188
  34.7 5.4 %collective-permute-start.2 = (f32[64,24]{1,0:T(8,128)S(1)}, f32[64,24]{1,0:T(8,128)S(1)}, u32[]{:S(2)}, u32[]{:S(2)}) collective-permute-start(f32[64,24]{1,0:T(8,128)S(1)} %fusion.13), channel_id=1, source_target_pairs={{0,16},{8,24},{16,0},{24,8},{32,48},{40,56},{48,32},{56,40},{64,80... | collective-permute-start | bytes 18440 | tf_op jit(solution)/shard_map/ppermute | solution.py:28
  40.1 0.6 copy-start.5
  40.7 0.6 copy-start.6
  51.2 3.9 %collective-permute-start.5 = (f32[64,24]{1,0:T(8,128)S(1)}, f32[64,24]{1,0:T(8,128)S(1)}, u32[]{:S(2)}, u32[]{:S(2)}) collective-permute-start(f32[64,24]{1,0:T(8,128)S(1)} %add.21), channel_id=1, source_target_pairs={{0,32},{8,40},{16,48},{24,56},{32,0},{40,8},{48,16},{56,24},{64,96... | collective-permute-start | bytes 18440 | tf_op jit(solution)/shard_map/ppermute | solution.py:28
  55.1 5.4 %collective-permute-start.6 = (f32[64,24]{1,0:T(8,128)S(1)}, f32[64,24]{1,0:T(8,128)S(1)}, u32[]{:S(2)}, u32[]{:S(2)}) collective-permute-start(f32[64,24]{1,0:T(8,128)S(1)} %add.22), channel_id=1, source_target_pairs={{0,64},{8,72},{16,80},{24,88},{32,96},{40,104},{48,112},{56,120},{... | collective-permute-start | bytes 18440 | tf_op jit(solution)/shard_map/ppermute | solution.py:28

commit v8 on v6

--- a/solution.py
+++ b/solution.py
@@ -23,10 +23,16 @@
 
 def butterfly_sum(x, axis, step=1):
     size = lax.axis_size(axis)
+    if step < size:
+        x = x + lax.ppermute(x, axis, [(i, i ^ step) for i in range(size)])
+        step *= 2
+    masks = [0]
     while step < size:
-        pairs = [(i, i ^ step) for i in range(size)]
-        x = x + lax.ppermute(x, axis, pairs)
+        masks = masks + [m | step for m in masks]
         step *= 2
+    received = [lax.ppermute(x, axis, [(i, i ^ m) for i in range(size)]) for m in masks[1:]]
+    for part in received:
+        x = x + part
     return x
 
 
@@ -310,11 +316,12 @@
     vectors, terms = partial_terms.shape
     even = lax.axis_index("prow") % 2 == 0
     partner = jnp.where(even, row_hi[-vectors:, :terms], row_lo[-vectors:, :terms])
-    restricted = butterfly_sum(partial_terms + partner, "prow", 2)
     ext_first, ext_last = edges(row_lo, row_hi, col_first, col_last)
     halos = (row_lo, row_hi, line(ext_last, "pcol", cols_n, 1), line(ext_first, "pcol", cols_n, -1))
     sides = margin_sides[0, 0].astype(jnp.float32)
+
     smoothed = smoother(sides, loads, modulus, halos)
+    restricted = butterfly_sum(partial_terms + partner, "prow", 2)
 
     solved = jnp.dot(coarse_inverse[0], restricted, precision=lax.Precision.HIGHEST)
     lifted = lax.dot_general(

time: 65.9 us -> 62.9 us (0.954)
  starting transfers between devices: 22.5 us -> 20.6 us
  waiting for transfers between devices: 12.4 us -> 11.1 us
    ppermute x3 -> x4, waiting for transfers between devices: 3.13 us -> 1.83 us  [the longest x1 1.83 us: butterfly_sum(): x = x + lax.ppermute(x, axis, [(i, i ^ step) for i in range(size)])]
    ppermute x3 -> x4, starting transfers between devices: 7.16 us -> 6.18 us  [the longest x3 3.66 us: butterfly_sum(): lax.ppermute(x, axis, [(i, i ^ m) for i in range(size)])]
    ppermute x4, starting transfers between devices: 15.3 us -> 14.4 us  [line(): return lax.ppermute(source, axis, pairs)]
  transfers between devices with their start and end apart: 7 -> 8, of which waited for: 5 -> 4; matrix products, arithmetic and copies ran while one was open for 1% -> 1% of each run, Pallas kernels for 3% -> 3%
where the time goes in v8:
time: 62.9 us; the launch traced here: 61.7 us
  starting transfers between devices  20.6 us (33%)
  Pallas kernels  14.5 us (23%)
  matrix products  13 us (21%)
  waiting for transfers between devices  11.1 us (18%)
  local copies, waits for them, and re-layouts  1.85 us (3%)
    ppermute x4, starting transfers between devices, line(): return lax.ppermute(source, axis, pairs)  14.4 us
    pallas_call x1, Pallas kernels, smoother(): pl.pallas_call(smoother_kernel, out_shape=jax.ShapeDtypeStruct(loads.shap...  9.84 us
    ppermute x4, waiting for transfers between devices, line(): return lax.ppermute(source, axis, pairs)  9.27 us
    dot_general x1, matrix products, per_device_body(): lax.dot_general(coarse_vectors, right_sides, ((cell_dims, cell_dims), (()...  7.6 us
    dot_general x1, matrix products, per_device_body(): lax.dot_general(solved, coarse_vectors, (((0,), (0,)), ((), ())), precisi...  5.15 us
    ppermute x3, starting transfers between devices, butterfly_sum(): lax.ppermute(x, axis, [(i, i ^ m) for i in range(size)])  3.66 us
    pallas_call x1, Pallas kernels, pack(): pl.pallas_call(pack_kernel, out_shape=[jax.ShapeDtypeStruct((height, cols...  2.66 us
    ppermute x1, starting transfers between devices, butterfly_sum(): x = x + lax.ppermute(x, axis, [(i, i ^ step) for i in range(size)])  2.52 us
  transfers between devices with their start and end apart: 8, of which 4 were waited for; matrix products, arithmetic and copies ran while one was open for 1% of the time, Pallas kernels for 3%

profile of v8, /device:TPU:1, one launch (start us, length us, event | category | flops | bytes accessed | tf_op | source)
XLA Modules:
  0.0 61.7 jit_solution(131146012011331889)
XLA Ops:
  0.0 0.0 copy-start
  0.0 7.6 %fusion.5.partial_ref = f32[64,24]{1,0:T(8,128)} fusion(f32[24,3,4,8,128]{4,3,2,1,0:T(8,128)} %param.5, f32[64,3,4,8,128]{4,3,2,1,0:T(8,128)} %param.8), kind=kOutput, calls=%fused_computation.6 | convolution fusion | flops 226492416 | bytes 4331520 | tf_op jit(solution)/shard_map/dot_general | solution.py:301
  7.6 0.0 copy-start.4
  7.6 0.0 copy-start.7
  7.6 2.7 %shard_map.55 = (f32[384,128]{1,0:T(8,128)}, f32[384,128]{1,0:T(8,128)}, f32[8,384]{1,0:T(8,128)}, f32[8,384]{1,0:T(8,128)}) custom-call(f32[72,4,8,128]{3,2,1,0:T(8,128)} %bitcast.16, f32[4,8,128]{2,1,0:T(8,128)} %mod_ref.3, f32[64,24]{1,0:T(8,128)} %fusion.5.partial_ref), custom_call_target="tpu_custom_call" | custom-call | tf_op jit(solution)/shard_map/pallas_call | solution.py:93
  10.3 3.9 %collective-permute-start = (f32[384,128]{1,0:T(8,128)}, f32[384,128]{1,0:T(8,128)S(1)}, u32[]{:S(2)}, u32[]{:S(2)}) collective-permute-start(f32[384,128]{1,0:T(8,128)} %get-tuple-element.11), channel_id=1, source_target_pairs={{0,8},{8,16},{16,24},{24,32},{32,40},{40,48},{48,56},{56,64},{64,7... | collective-permute-start | bytes 589832 | tf_op jit(solution)/shard_map/ppermute | solution.py:312
  14.2 1.3 %collective-permute-start.1 = (f32[384,128]{1,0:T(8,128)}, f32[384,128]{1,0:T(8,128)S(1)}, u32[]{:S(2)}, u32[]{:S(2)}) collective-permute-start(f32[384,128]{1,0:T(8,128)} %get-tuple-element.12), channel_id=1, source_target_pairs={{8,0},{16,8},{24,16},{32,24},{40,32},{48,40},{56,48},{64,56},{72,6... | collective-permute-start | bytes 589832 | tf_op jit(solution)/shard_map/ppermute | solution.py:312
  15.5 2.6 %collective-permute-done.rlo_ref = f32[384,128]{1,0:T(8,128)S(1)} collective-permute-done((f32[384,128]{1,0:T(8,128)}, f32[384,128]{1,0:T(8,128)S(1)}, u32[]{:S(2)}, u32[]{:S(2)}) %collective-permute-start) | collective-permute-done | bytes 196640 | tf_op jit(solution)/shard_map/ppermute | solution.py:312
  18.1 0.0 copy-start.2
  18.1 3.7 %collective-permute-done.1.rhi_ref = f32[384,128]{1,0:T(8,128)S(1)} collective-permute-done((f32[384,128]{1,0:T(8,128)}, f32[384,128]{1,0:T(8,128)S(1)}, u32[]{:S(2)}, u32[]{:S(2)}) %collective-permute-start.1) | collective-permute-done | bytes 196640 | tf_op jit(solution)/shard_map/ppermute | solution.py:312
  21.8 0.0 copy-done.4
  21.8 0.0 copy-start.3
  21.8 2.5 %collective-permute-start.4 = (f32[64,24]{1,0:T(8,128)S(1)}, f32[64,24]{1,0:T(8,128)S(1)}, u32[]{:S(2)}, u32[]{:S(2)}) collective-permute-start(f32[64,24]{1,0:T(8,128)S(1)} %fusion.10), channel_id=1, source_target_pairs={{0,16},{8,24},{16,0},{24,8},{32,48},{40,56},{48,32},{56,40},{64,80... | collective-permute-start | bytes 18440 | tf_op jit(solution)/shard_map/ppermute | solution.py:27
  24.4 1.8 %collective-permute-done.4 = f32[64,24]{1,0:T(8,128)S(1)} collective-permute-done((f32[64,24]{1,0:T(8,128)S(1)}, f32[64,24]{1,0:T(8,128)S(1)}, u32[]{:S(2)}, u32[]{:S(2)}) %collective-permute-start.4) | collective-permute-done | bytes 6176 | tf_op jit(solution)/shard_map/ppermute | solution.py:27
  26.2 3.0 %collective-permute-start.7 = (f32[64,24]{1,0:T(8,128)S(1)}, f32[64,24]{1,0:T(8,128)S(1)}, u32[]{:S(2)}, u32[]{:S(2)}) collective-permute-start(f32[64,24]{1,0:T(8,128)S(1)} %add.24), channel_id=1, source_target_pairs={{0,96},{8,104},{16,112},{24,120},{32,64},{40,72},{48,80},{56,88},{... | collective-permute-start | bytes 18440 | tf_op jit(solution)/shard_map/ppermute | solution.py:33
  29.2 0.3 collective-permute-start.6
  29.5 0.3 collective-permute-start.5
  29.8 0.0 copy-done.7
  29.9 0.6 convert_bitcast_fusion.sides_ref
  30.4 0.0 copy-done.3
  30.4 0.0 copy-done.2
  30.4 0.0 copy-start.1
  30.4 2.0 %shard_map.56 = (f32[16,384]{1,0:T(8,128)}, f32[16,384]{1,0:T(8,128)}) custom-call(f32[384,128]{1,0:T(8,128)} %copy-done.2, f32[384,128]{1,0:T(8,128)} %copy-done.3, f32[8,384]{1,0:T(8,128)} %get-tuple-element.13.col_first_ref, f32[8,384]{1,0:T(8,128)} %get-tuple-element.14.col_last_ref), custom_call_target="tpu_custom_call" | custom-call | tf_op jit(solution)/shard_map/pallas_call | solution.py:122
  32.4 7.1 %collective-permute-start.2 = (f32[16,384]{1,0:T(8,128)}, f32[16,384]{1,0:T(8,128)S(1)}, u32[]{:S(2)}, u32[]{:S(2)}) collective-permute-start(f32[16,384]{1,0:T(8,128)} %get-tuple-element.15), channel_id=1, source_target_pairs={{0,1},{1,2},{2,3},{3,4},{4,5},{5,6},{6,7},{8,9},{9,10},{10,11},{11... | collective-permute-start | bytes 73736 | tf_op jit(solution)/shard_map/ppermute | solution.py:312
  39.5 2.1 %collective-permute-start.3 = (f32[16,384]{1,0:T(8,128)}, f32[16,384]{1,0:T(8,128)S(1)}, u32[]{:S(2)}, u32[]{:S(2)}) collective-permute-start(f32[16,384]{1,0:T(8,128)} %get-tuple-element.16), channel_id=1, source_target_pairs={{1,0},{2,1},{3,2},{4,3},{5,4},{6,5},{7,6},{9,8},{10,9},{11,10},{12... | collective-permute-start | bytes 73736 | tf_op jit(solution)/shard_map/ppermute | solution.py:312
  41.6 0.0 collective-permute-done.7
  41.6 0.0 collective-permute-done.6
  41.6 0.0 collective-permute-done.5
  41.6 0.0 copy-done
  41.7 0.2 convolution_bitcast_fusion
  41.9 0.0 collective-permute-done.2.clo_ref
  41.9 0.0 copy-start.5
  41.9 3.0 %collective-permute-done.3.chi_ref = f32[16,384]{1,0:T(8,128)S(1)} collective-permute-done((f32[16,384]{1,0:T(8,128)}, f32[16,384]{1,0:T(8,128)S(1)}, u32[]{:S(2)}, u32[]{:S(2)}) %collective-permute-start.3) | collective-permute-done | bytes 24608 | tf_op jit(solution)/shard_map/ppermute | solution.py:312
  44.9 0.0 copy-done.5
  44.9 0.0 copy-start.6
  44.9 0.6 copy-done.6
  45.5 9.8 %shard_map.57 = f32[72,4,8,128]{3,2,1,0:T(8,128)} custom-call(f32[4]{0:T(128)} %convert_bitcast_fusion.sides_ref, f32[72,4,8,128]{3,2,1,0:T(8,128)} %bitcast.17, f32[4,8,128]{2,1,0:T(8,128)} %mod_ref.3, f32[384,128]{1,0:T(8,128)} %copy-done.2, f32[384,128]{1,0:T(8,128)} %copy-done.3, f32[16,384]{1,0:T(8,128)} %copy-done.5, f32[16,384]{1,0:T(8,128)} %copy-done.6), custom_call_target="tpu_custom_call" | custom-call | tf_op jit(solution)/shard_map/pallas_call | solution.py:279
  55.3 0.0 copy-done.1
  55.3 5.1 %copy_add_fusion = f32[24,3,4,8,128]{4,0,3,2,1:T(8,128)S(1)} fusion(f32[24,3,4,8,128]{4,3,2,1,0:T(8,128)} %bitcast.18, f32[24,64,1,1,1]{1,0,4,3,2:T(8,128)S(1)} %convolution_bitcast_fusion, f32[64,3,4,8,128]{4,3,2,1,0:T(8,128)S(1)} %copy-done.1), kind=kOutput, calls=%fused_computation.4 | convolution fusion | flops 226787328 | bytes 5511168 | tf_op jit(solution)/shard_map/dot_general | solution.py:327
  60.5 1.2 %copy.12 = f32[24,3,4,8,128]{4,3,2,1,0:T(8,128)} copy(f32[24,3,4,8,128]{4,0,3,2,1:T(8,128)S(1)} %copy_add_fusion) | data formatting | bytes 2359296 | tf_op jit(solution)/shard_map/add | solution.py:330
  (2 shorter events, 0.0 us)
Async XLA Ops:
  0.0 41.6 %copy-start = (f32[1,64,64]{2,1,0:T(8,128)S(1)}, f32[1,64,64]{2,1,0:T(8,128)}, u32[]{:S(2)}) copy-start(f32[1,64,64]{2,1,0:T(8,128)} %param.9) | copy-start | bytes 49156
  7.6 14.2 %copy-start.4 = (f32[64,24]{1,0:T(8,128)S(1)}, f32[64,24]{1,0:T(8,128)}, u32[]{:S(2)}) copy-start(f32[64,24]{1,0:T(8,128)} %fusion.5.partial_ref) | copy-start | bytes 18436
  7.6 22.2 %copy-start.7 = (s32[1,1,4]{2,1,0:T(1,128)S(1)}, s32[1,1,4]{2,1,0:T(1,128)}, u32[]{:S(2)}) copy-start(s32[1,1,4]{2,1,0:T(1,128)} %param.7) | copy-start | bytes 52
  10.3 7.8 %collective-permute-start = (f32[384,128]{1,0:T(8,128)}, f32[384,128]{1,0:T(8,128)S(1)}, u32[]{:S(2)}, u32[]{:S(2)}) collective-permute-start(f32[384,128]{1,0:T(8,128)} %get-tuple-element.11), channel_id=1, source_target_pairs={{0,8},{8,16},{16,24},{24,32},{32,40},{40,48},{48,56},{56,64},{64,7... | collective-permute-start | bytes 589832 | tf_op jit(solution)/shard_map/ppermute | solution.py:312
  14.2 7.6 %collective-permute-start.1 = (f32[384,128]{1,0:T(8,128)}, f32[384,128]{1,0:T(8,128)S(1)}, u32[]{:S(2)}, u32[]{:S(2)}) collective-permute-start(f32[384,128]{1,0:T(8,128)} %get-tuple-element.12), channel_id=1, source_target_pairs={{8,0},{16,8},{24,16},{32,24},{40,32},{48,40},{56,48},{64,56},{72,6... | collective-permute-start | bytes 589832 | tf_op jit(solution)/shard_map/ppermute | solution.py:312
  18.1 12.4 %copy-start.2 = (f32[384,128]{1,0:T(8,128)}, f32[384,128]{1,0:T(8,128)S(1)}, u32[]{:S(2)}) copy-start(f32[384,128]{1,0:T(8,128)S(1)} %collective-permute-done.rlo_ref) | copy-start | bytes 589828
  21.8 8.6 %copy-start.3 = (f32[384,128]{1,0:T(8,128)}, f32[384,128]{1,0:T(8,128)S(1)}, u32[]{:S(2)}) copy-start(f32[384,128]{1,0:T(8,128)S(1)} %collective-permute-done.1.rhi_ref) | copy-start | bytes 589828
  21.8 4.3 %collective-permute-start.4 = (f32[64,24]{1,0:T(8,128)S(1)}, f32[64,24]{1,0:T(8,128)S(1)}, u32[]{:S(2)}, u32[]{:S(2)}) collective-permute-start(f32[64,24]{1,0:T(8,128)S(1)} %fusion.10), channel_id=1, source_target_pairs={{0,16},{8,24},{16,0},{24,8},{32,48},{40,56},{48,32},{56,40},{64,80... | collective-permute-start | bytes 18440 | tf_op jit(solution)/shard_map/ppermute | solution.py:27
  26.2 15.4 %collective-permute-start.7 = (f32[64,24]{1,0:T(8,128)S(1)}, f32[64,24]{1,0:T(8,128)S(1)}, u32[]{:S(2)}, u32[]{:S(2)}) collective-permute-start(f32[64,24]{1,0:T(8,128)S(1)} %add.24), channel_id=1, source_target_pairs={{0,96},{8,104},{16,112},{24,120},{32,64},{40,72},{48,80},{56,88},{... | collective-permute-start | bytes 18440 | tf_op jit(solution)/shard_map/ppermute | solution.py:33
  29.2 12.4 %collective-permute-start.6 = (f32[64,24]{1,0:T(8,128)S(1)}, f32[64,24]{1,0:T(8,128)S(1)}, u32[]{:S(2)}, u32[]{:S(2)}) collective-permute-start(f32[64,24]{1,0:T(8,128)S(1)} %add.24), channel_id=1, source_target_pairs={{0,64},{8,72},{16,80},{24,88},{32,96},{40,104},{48,112},{56,120},{... | collective-permute-start | bytes 18440 | tf_op jit(solution)/shard_map/ppermute | solution.py:33
  29.5 12.1 %collective-permute-start.5 = (f32[64,24]{1,0:T(8,128)S(1)}, f32[64,24]{1,0:T(8,128)S(1)}, u32[]{:S(2)}, u32[]{:S(2)}) collective-permute-start(f32[64,24]{1,0:T(8,128)S(1)} %add.24), channel_id=1, source_target_pairs={{0,32},{8,40},{16,48},{24,56},{32,0},{40,8},{48,16},{56,24},{64,96... | collective-permute-start | bytes 18440 | tf_op jit(solution)/shard_map/ppermute | solution.py:33
  30.4 24.9 %copy-start.1 = (f32[64,3,4,8,128]{4,3,2,1,0:T(8,128)S(1)}, f32[64,3,4,8,128]{4,3,2,1,0:T(8,128)}, u32[]{:S(2)}) copy-start(f32[64,3,4,8,128]{4,3,2,1,0:T(8,128)} %param.8) | copy-start | bytes 9437188
  32.4 9.5 %collective-permute-start.2 = (f32[16,384]{1,0:T(8,128)}, f32[16,384]{1,0:T(8,128)S(1)}, u32[]{:S(2)}, u32[]{:S(2)}) collective-permute-start(f32[16,384]{1,0:T(8,128)} %get-tuple-element.15), channel_id=1, source_target_pairs={{0,1},{1,2},{2,3},{3,4},{4,5},{5,6},{6,7},{8,9},{9,10},{10,11},{11... | collective-permute-start | bytes 73736 | tf_op jit(solution)/shard_map/ppermute | solution.py:312
  39.5 5.4 %collective-permute-start.3 = (f32[16,384]{1,0:T(8,128)}, f32[16,384]{1,0:T(8,128)S(1)}, u32[]{:S(2)}, u32[]{:S(2)}) collective-permute-start(f32[16,384]{1,0:T(8,128)} %get-tuple-element.16), channel_id=1, source_target_pairs={{1,0},{2,1},{3,2},{4,3},{5,4},{6,5},{7,6},{9,8},{10,9},{11,10},{12... | collective-permute-start | bytes 73736 | tf_op jit(solution)/shard_map/ppermute | solution.py:312
  41.9 3.0 %copy-start.5 = (f32[16,384]{1,0:T(8,128)}, f32[16,384]{1,0:T(8,128)S(1)}, u32[]{:S(2)}) copy-start(f32[16,384]{1,0:T(8,128)S(1)} %collective-permute-done.2.clo_ref) | copy-start | bytes 73732
  44.9 0.6 copy-start.6
